TPU v7x, 512 devices: a whole 4x8x8 slice. The times are simulated.
512 devices in a mesh: dp: 64 (over z, x, core), mp: 8 (over y).
Axes of the slice: x: 4, y: 8, z: 8, core: 2. Of those that a mesh axis runs over, the one named last changes fastest.
Arguments:
- micro_grads: bfloat16 [64, 2, 768, 768], P('dp', None, None, 'mp'), may hold values from -16 to 16
- master: float32 [768, 768], P('dp', 'mp'), may hold values from -0.21875 to 0.21875
- moment: float32 [768, 768], P('dp', 'mp'), may hold values from -1.5 to 1.5
- second: float32 [768, 768], P('dp', 'mp'), may hold values from 0.001 to 0.1
- left_basis: float32 [768, 768], P(None, 'dp'), may hold values from -0.21875 to 0.21875
- right_basis: float32 [768, 768], P(None, 'mp'), may hold values from -0.21875 to 0.21875
- left_stat: float32 [768, 768], P('mp'), may hold values from -2 to 5, as said below
- right_stat: float32 [768, 768], P('mp'), may hold values from -2 to 5, as said below
Outputs:
- weights_block: bfloat16 [768, 768], P(None, 'mp')
- new_master: float32 [768, 768], P('dp', 'mp')
- new_moment: float32 [768, 768], P('dp', 'mp')
- new_second: float32 [768, 768], P('dp', 'mp')
- new_left_stat: float32 [768, 768], P('mp')
- new_right_stat: float32 [768, 768], P('mp')
- new_left_basis: float32 [768, 768], P('mp')
- new_right_basis: float32 [768, 768], P('mp')
Inputs may be any that keep to these rules, and one draw needn't show every extreme that they name: `left_stat`: symmetric. `right_stat`: symmetric.
All inputs are finite; a program needn't handle non-finite values.
Results may differ from a plain program's by a relative error of at most 0.004.
The roundings to bfloat16 on the way count: a program that leaves them out, or rounds other values in their place, can miss the bound.
Values may be sent and summed in bfloat16 or wider, within the bound.
No kernel may reach another device: no remote copies, remote signals or barrier semaphores. Data moves between devices by JAX's collectives and lax.ppermute only.
A program may use at most 64 MiB of HBM per device.

v0:
```python
import jax
import jax.numpy as jnp
from jax import lax
from jax.sharding import PartitionSpec as P

beta_one = 0.9
beta_two = 0.95
beta_stat = 0.95
learn_rate = 0.02
adam_eps = 1e-08
norm_eps = 1e-06
quint_a = 1.875
quint_b = -1.25
quint_c = 0.375
highest = lax.Precision.HIGHEST


def for_sending(x):

    def short(part):
        return part.astype(jnp.bfloat16) if part.dtype == jnp.float32 else part

    return jax.tree.map(short, x)


def all_rows(pair):
    return jax.tree.map(
        lambda part, own: part.astype(own.dtype),
        lax.all_gather(for_sending(pair), "mp", axis=0, tiled=True),
        pair,
    )


def row_gram(row_part, whole_part):
    return lax.dot_general(
        row_part, whole_part, (((1,), (1,)), ((), ())), preferred_element_type=jnp.float32
    )


def per_device(micro_grads, master, moment, second, left_basis, right_basis, left_stat, right_stat):
    dp_count = lax.axis_size("dp")
    micro_count = micro_grads.shape[1]
    local_sum = jnp.sum(micro_grads[0], axis=0, dtype=jnp.float32)
    grad_piece = lax.psum_scatter(local_sum, "dp", scatter_dimension=0, tiled=True) / (
        micro_count * dp_count
    )
    new_moment = beta_one * moment + (1.0 - beta_one) * grad_piece
    grad_cols, moment_cols, left_full = (
        lax.all_gather(grad_piece, "dp", axis=0, tiled=True),
        lax.all_gather(new_moment, "dp", axis=0, tiled=True),
        lax.all_gather(left_basis, "dp", axis=1, tiled=True),
    )
    grad_full, moment_full, right_full = (
        lax.all_gather(grad_cols, "mp", axis=1, tiled=True),
        lax.all_gather(moment_cols, "mp", axis=1, tiled=True),
        lax.all_gather(right_basis, "mp", axis=1, tiled=True),
    )

    def rotate(matrix):
        left_part = lax.dot_general(left_basis, matrix, (((0,), (0,)), ((), ())), precision=highest)
        return jnp.dot(left_part, right_basis, precision=highest)

    rot_grad = rotate(grad_full)
    rot_moment = rotate(moment_full)
    new_second = beta_two * second + (1.0 - beta_two) * rot_grad * rot_grad
    rot_step = rot_moment / (jnp.sqrt(new_second) + adam_eps)
    basis_rows = right_basis
    back_half = lax.psum_scatter(
        lax.dot_general(basis_rows, rot_step, (((1,), (1,)), ((), ())), precision=highest),
        "mp",
        scatter_dimension=0,
        tiled=True,
    )
    basis_rows = left_basis
    step_piece = lax.psum_scatter(
        lax.dot_general(basis_rows, back_half, (((1,), (1,)), ((), ())), precision=highest),
        "dp",
        scatter_dimension=0,
        tiled=True,
    )
    new_master = master - learn_rate * step_piece
    weights_block = lax.all_gather(new_master.astype(jnp.bfloat16), "dp", axis=0, tiled=True)
    band_width = right_basis.shape[1]
    band_start = lax.axis_index("mp") * band_width
    grad_band = lax.dynamic_slice_in_dim(grad_full, band_start, band_width, 0)
    grad_strip = lax.dynamic_slice_in_dim(grad_full, band_start, band_width, 1)
    left_outer = lax.dot_general(grad_band, grad_full, (((1,), (1,)), ((), ())), precision=highest)
    right_outer = lax.dot_general(
        grad_strip, grad_full, (((0,), (0,)), ((), ())), precision=highest
    )
    new_left_stat = beta_stat * left_stat + (1.0 - beta_stat) * left_outer
    new_right_stat = beta_stat * right_stat + (1.0 - beta_stat) * right_outer
    order_count = left_stat.shape[1]
    power_left = jnp.dot(
        new_left_stat.astype(jnp.bfloat16),
        left_full.astype(jnp.bfloat16),
        preferred_element_type=jnp.float32,
    )
    power_right = jnp.dot(
        new_right_stat.astype(jnp.bfloat16),
        right_full.astype(jnp.bfloat16),
        preferred_element_type=jnp.float32,
    )
    total_left, total_right = lax.psum(
        (jnp.sum(power_left * power_left), jnp.sum(power_right * power_right)), "mp"
    )
    start_left = lax.optimization_barrier(
        (power_left * lax.rsqrt(total_left * (4.0 / order_count) + norm_eps)).astype(jnp.bfloat16)
    )
    start_right = lax.optimization_barrier(
        (power_right * lax.rsqrt(total_right * (4.0 / order_count) + norm_eps)).astype(jnp.bfloat16)
    )
    start_rows = (start_left, start_right)
    start_whole = all_rows(start_rows)
    gram_rows = tuple(
        (
            lax.optimization_barrier(row_gram(row_part, whole_part).astype(jnp.bfloat16))
            for row_part, whole_part in zip(start_rows, start_whole)
        )
    )
    gram_whole = all_rows(gram_rows)
    middle_rows = []
    for row_part, gram_part, gram_all, whole_part in zip(
        start_rows, gram_rows, gram_whole, start_whole
    ):
        square = jnp.dot(gram_part, gram_all, preferred_element_type=jnp.float32)
        poly_rows = (quint_b * gram_part.astype(jnp.float32) + quint_c * square).astype(
            jnp.bfloat16
        )
        middle = quint_a * row_part.astype(jnp.float32) + jnp.dot(
            poly_rows, whole_part, preferred_element_type=jnp.float32
        )
        middle_rows.append(lax.optimization_barrier(middle.astype(jnp.bfloat16)))
    middle_whole = all_rows(tuple(middle_rows))
    new_bases = []
    for row_part, whole_part in zip(middle_rows, middle_whole):
        gram_two = row_gram(row_part, whole_part).astype(jnp.bfloat16)
        new_bases.append(
            1.5 * row_part.astype(jnp.float32)
            - 0.5 * jnp.dot(gram_two, whole_part, preferred_element_type=jnp.float32)
        )
    return (
        weights_block,
        new_master,
        new_moment,
        new_second,
        new_left_stat,
        new_right_stat,
        new_bases[0],
        new_bases[1],
    )


def solution(mesh):
    in_specs = (
        P("dp", None, None, "mp"),
        P("dp", "mp"),
        P("dp", "mp"),
        P("dp", "mp"),
        P(None, "dp"),
        P(None, "mp"),
        P("mp", None),
        P("mp", None),
    )
    out_specs = (
        P(None, "mp"),
        P("dp", "mp"),
        P("dp", "mp"),
        P("dp", "mp"),
        P("mp", None),
        P("mp", None),
        P("mp", None),
        P("mp", None),
    )
    return jax.shard_map(
        per_device, mesh=mesh, in_specs=in_specs, out_specs=out_specs, check_vma=False
    )
```

profile of v0, /device:TPU:1, one launch (start us, length us, event | category | flops | bytes accessed | tf_op | source)
XLA Modules:
  0.0 921.2 jit_solution(14783238774417573509)
XLA Ops:
  7.2 1.0 convert_reduce_fusion
  10.0 1.3 dynamic-slice
  12.0 195.3 %all-reduce.6.cloned.1.call-done = f32[768,96]{1,0:T(8,128)} async-done(((f32[768,96]{1,0:T(8,128)}), f32[768,96]{1,0:T(8,128)}) %all-reduce.6.cloned.1.call-update) | async-done | bytes 294928
  208.0 50.6 %all-gather.1 = f32[64,12,96]{2,1,0:T(8,128)S(1)} all-gather(f32[1,12,96]{2,1,0:T(8,128)S(1)} %get-tuple-element.36), channel_id=1, replica_groups=mesh['dp'=64,'mp'=8] {'dp'}, dimensions={0}, use_global_device_ids=true | all-gather | bytes 299520 | tf_op jit(solution)/shard_map/all_gather | solution.py:49
  260.4 48.7 %all-gather = f32[64,12,96]{2,1,0:T(8,128)S(1)} all-gather(f32[1,12,96]{2,1,0:T(8,128)S(1)} %bitcast.49), channel_id=1, replica_groups=mesh['dp'=64,'mp'=8] {'dp'}, dimensions={0}, use_global_device_ids=true | all-gather | bytes 299520 | tf_op jit(solution)/shard_map/all_gather | solution.py:50
  310.1 3.2 reshape.25
  313.3 22.5 %all-gather.17.cloned.1.call-done = f32[768,768]{0,1:T(8,128)} async-done(((f32[768,96]{0,1:T(8,128)}), f32[768,768]{0,1:T(8,128)}) %all-gather.17.cloned.1.call-update) | async-done | bytes 2359312 | tf_op jit(solution)/shard_map/all_gather | solution.py:54
  335.8 3.7 fusion.3
  339.5 3.2 multiply_reduce_fusion.1
  342.7 2.4 fusion.2
  345.2 32.6 %all-gather.25.cloned.1.call-done = bf16[768,768]{0,1:T(8,128)(2,1)} async-done(((bf16[768,96]{0,1:T(8,128)(2,1)}), bf16[768,768]{0,1:T(8,128)(2,1)}) %all-gather.25.cloned.1.call-update) | async-done | bytes 1179664 | tf_op jit(solution)/shard_map/all_gather | solution.py:56
  377.8 2.4 multiply_reduce_fusion
  380.2 13.3 %all-reduce.2 = (f32[]{:T(128)}, f32[]{:T(128)}) all-reduce(f32[]{:T(128)} %get-tuple-element.38, f32[]{:T(128)} %get-tuple-element.40), channel_id=1, replica_groups=mesh['dp'=64,'mp'=8] {'mp'}, use_global_device_ids=true, to_apply=%region_5.0 | all-reduce | flops 2 | bytes 16 | tf_op jit(solution)/shard_map/psum | solution.py:104
  396.6 2.8 fusion.35
  399.8 25.3 %all-gather.15.cloned.1.call-done = f32[768,768]{0,1:T(8,128)} async-done(((f32[768,96]{0,1:T(8,128)}), f32[768,768]{0,1:T(8,128)}) %all-gather.15.cloned.1.call-update) | async-done | bytes 2359312 | tf_op jit(solution)/shard_map/all_gather | solution.py:55
  425.1 3.7 fusion.34
  430.5 36.0 %all-gather.19.cloned.1.call-done = bf16[768,768]{1,0:T(8,128)(2,1)} async-done(((bf16[96,768]{1,0:T(8,128)(2,1)}), bf16[768,768]{1,0:T(8,128)(2,1)}) %all-gather.19.cloned.1.call-update) | async-done | bytes 1179664 | tf_op jit(solution)/shard_map/all_gather | solution.py:29
  466.5 2.4 convolution_convert_fusion.3
  469.0 40.6 %all-gather.27.cloned.1.call-done = bf16[768,768]{1,0:T(8,128)(2,1)} async-done(((bf16[96,768]{1,0:T(8,128)(2,1)}), bf16[768,768]{1,0:T(8,128)(2,1)}) %all-gather.27.cloned.1.call-update) | async-done | bytes 1179664 | tf_op jit(solution)/shard_map/all_gather | solution.py:29
  509.6 2.4 convolution_convert_fusion.1
  512.1 38.0 %reduce-scatter.5.cloned.1.call-done = f32[96,12]{1,0:T(8,128)} async-done(((f32[768,12]{1,0:T(8,128)}), f32[96,12]{1,0:T(8,128)}) %reduce-scatter.5.cloned.1.call-update) | async-done | bytes 4624
  550.1 1.9 convolution_bitcast_fusion
  552.1 41.8 %all-gather.21.cloned.1.call-done = bf16[768,768]{1,0:T(8,128)(2,1)} async-done(((bf16[96,768]{1,0:T(8,128)(2,1)}), bf16[768,768]{1,0:T(8,128)(2,1)}) %all-gather.21.cloned.1.call-update) | async-done | bytes 1179664 | tf_op jit(solution)/shard_map/all_gather | solution.py:29
  593.9 2.5 fusion.9
  596.6 39.5 %all-gather.29.cloned.1.call-done = bf16[768,768]{1,0:T(8,128)(2,1)} async-done(((bf16[96,768]{1,0:T(8,128)(2,1)}), bf16[768,768]{1,0:T(8,128)(2,1)}) %all-gather.29.cloned.1.call-update) | async-done | bytes 1179664 | tf_op jit(solution)/shard_map/all_gather | solution.py:29
  636.1 2.5 fusion.11
  638.8 191.9 %all-reduce.8.cloned.1.call-done = f32[768,96]{0,1:T(8,128)} async-done(((f32[768,96]{0,1:T(8,128)}), f32[768,96]{0,1:T(8,128)}) %all-reduce.8.cloned.1.call-update) | async-done | bytes 294928
  830.7 1.0 convert_bitcast_fusion
  831.8 43.1 %all-gather.2 = bf16[64,12,96]{2,1,0:T(8,128)(2,1)S(1)} all-gather(bf16[1,12,96]{2,1,0:T(8,128)(2,1)S(1)} %copy.26), channel_id=1, replica_groups=mesh['dp'=64,'mp'=8] {'dp'}, dimensions={0}, use_global_device_ids=true | all-gather | bytes 149760 | tf_op jit(solution)/shard_map/all_gather | solution.py:82
  876.4 3.1 fusion.6
  879.5 32.1 %all-gather.31.cloned.1.call-done = bf16[768,768]{1,0:T(8,128)(2,1)} async-done(((bf16[96,768]{1,0:T(8,128)(2,1)}), bf16[768,768]{1,0:T(8,128)(2,1)}) %all-gather.31.cloned.1.call-update) | async-done | bytes 1179664 | tf_op jit(solution)/shard_map/all_gather | solution.py:29
  911.6 3.1 fusion.4
  (91 shorter events, 10.9 us)
Async XLA Ops:
  7.2 200.1 %copy-start.21 = (f32[12,96]{1,0:T(8,128)S(1)}, f32[12,96]{1,0:T(8,128)}, u32[]{:S(2)}) copy-start(f32[12,96]{1,0:T(8,128)} %param.10) | copy-start | bytes 13828
  7.2 200.1 %all-reduce.6.cloned.1.call-start = ((), (), s32[]{:S(2)}) async-start(), calls=%async_computation.12 | async-start | bytes 786432
  9.2 300.9 %all-gather.33.cloned.1.call-start = ((), (), s32[]{:S(2)}) async-start(), calls=%async_computation.10 | async-start | bytes 1597440 | tf_op jit(solution)/shard_map/all_gather | solution.py:51
  10.0 325.9 %all-gather.17.cloned.1.call-start = ((), (), s32[]{:S(2)}) async-start(), calls=%async_computation.2 | async-start | bytes 2654208 | tf_op jit(solution)/shard_map/all_gather | solution.py:54
  208.0 52.4 %copy-start.17 = (f32[12,96]{1,0:T(8,128)}, f32[12,96]{1,0:T(8,128)S(1)}, u32[]{:S(2)}) copy-start(f32[12,96]{1,0:T(8,128)S(1)} %get-tuple-element.37) | copy-start | bytes 13828
  208.0 51.6 %copy-start.1 = (f32[768,96]{0,1:T(8,128)S(1)}, f32[768,96]{0,1:T(8,128)}, u32[]{:S(2)}) copy-start(f32[768,96]{0,1:T(8,128)} %param.13) | copy-start | bytes 884740
  259.6 118.2 %all-gather.25.cloned.1.call-start = ((), (), s32[]{:S(2)}) async-start(), calls=%async_computation.6 | async-start | bytes 1327104 | tf_op jit(solution)/shard_map/all_gather | solution.py:56
  260.3 164.8 %all-gather.15.cloned.1.call-start = ((), (), s32[]{:S(2)}) async-start(), calls=%async_computation.1 | async-start | bytes 2654208 | tf_op jit(solution)/shard_map/all_gather | solution.py:55
  310.0 156.5 %all-gather.19.cloned.1.call-start = ((), (), s32[]{:S(2)}) async-start(), calls=%async_computation.3 | async-start | bytes 1327104 | tf_op jit(solution)/shard_map/all_gather | solution.py:29
  310.1 25.8 %copy-start.15 = (f32[96,768]{1,0:T(8,128)S(1)}, f32[96,768]{1,0:T(8,128)}, u32[]{:S(2)}) copy-start(f32[96,768]{1,0:T(8,128)} %param.14) | copy-start | bytes 884740
  335.8 6.9 copy-start
  339.5 5.6 copy-start.10
  345.1 49.7 %copy-start.11 = (f32[96,768]{1,0:T(8,128)}, f32[96,768]{1,0:T(8,128)S(1)}, u32[]{:S(2)}) copy-start(f32[96,768]{1,0:T(8,128)S(1)} %fusion.2) | copy-start | bytes 884740
  377.8 16.4 %copy-start.12 = (f32[96,768]{1,0:T(8,128)S(1)}, f32[96,768]{1,0:T(8,128)}, u32[]{:S(2)}) copy-start(f32[96,768]{1,0:T(8,128)} %get-tuple-element.39) | copy-start | bytes 884740
  394.9 114.7 %all-gather.27.cloned.1.call-start = ((), (), s32[]{:S(2)}) async-start(), calls=%async_computation.7 | async-start | bytes 1327104 | tf_op jit(solution)/shard_map/all_gather | solution.py:29
  396.3 28.8 %copy-start.14 = (f32[768,12]{0,1:T(8,128)S(1)}, f32[768,12]{0,1:T(8,128)}, u32[]{:S(2)}) copy-start(f32[768,12]{0,1:T(8,128)} %param.12) | copy-start | bytes 110596
  396.3 153.8 %reduce-scatter.5.cloned.1.call-start = ((), (), s32[]{:S(2)}) async-start(), calls=%async_computation.11 | async-start | bytes 442368
  399.7 29.1 %copy-start.18 = (f32[12,96]{1,0:T(8,128)}, f32[12,96]{1,0:T(8,128)S(1)}, u32[]{:S(2)}) copy-start(f32[12,96]{1,0:T(8,128)S(1)} %fusion.26) | copy-start | bytes 13828
  428.8 37.7 %copy-start.4 = (bf16[96,768]{1,0:T(8,128)(2,1)S(1)}, bf16[96,768]{1,0:T(8,128)(2,1)}, u32[]{:S(2)}) copy-start(bf16[96,768]{1,0:T(8,128)(2,1)} %multiply_convert_fusion.1) | copy-start | bytes 442372
  429.5 80.1 %copy-start.5 = (bf16[96,768]{1,0:T(8,128)(2,1)S(1)}, bf16[96,768]{1,0:T(8,128)(2,1)}, u32[]{:S(2)}) copy-start(bf16[96,768]{1,0:T(8,128)(2,1)} %multiply_convert_fusion) | copy-start | bytes 442372
  430.4 163.5 %all-gather.21.cloned.1.call-start = ((), (), s32[]{:S(2)}) async-start(), calls=%async_computation.4 | async-start | bytes 1327104 | tf_op jit(solution)/shard_map/all_gather | solution.py:29
  469.0 125.0 %copy-start.2 = (bf16[768,768]{1,0:T(8,128)(2,1)S(1)}, bf16[768,768]{1,0:T(8,128)(2,1)}, u32[]{:S(2)}) copy-start(bf16[768,768]{1,0:T(8,128)(2,1)} %all-gather.19.cloned.1.call-done) | copy-start | bytes 3538948
  469.0 125.0 %copy-start.8 = (bf16[96,768]{1,0:T(8,128)(2,1)S(1)}, bf16[96,768]{1,0:T(8,128)(2,1)}, u32[]{:S(2)}) copy-start(bf16[96,768]{1,0:T(8,128)(2,1)} %convolution_convert_fusion.3) | copy-start | bytes 442372
  469.0 167.1 %all-gather.29.cloned.1.call-start = ((), (), s32[]{:S(2)}) async-start(), calls=%async_computation.8 | async-start | bytes 1327104 | tf_op jit(solution)/shard_map/all_gather | solution.py:29
  512.1 318.6 %all-reduce.8.cloned.1.call-start = ((), (), s32[]{:S(2)}) async-start(), calls=%async_computation.13 | async-start | bytes 589824
  552.0 84.1 %copy-start.3 = (bf16[768,768]{1,0:T(8,128)(2,1)S(1)}, bf16[768,768]{1,0:T(8,128)(2,1)}, u32[]{:S(2)}) copy-start(bf16[768,768]{1,0:T(8,128)(2,1)} %all-gather.27.cloned.1.call-done) | copy-start | bytes 3538948
  552.0 84.1 %copy-start.7 = (bf16[96,768]{1,0:T(8,128)(2,1)S(1)}, bf16[96,768]{1,0:T(8,128)(2,1)}, u32[]{:S(2)}) copy-start(bf16[96,768]{1,0:T(8,128)(2,1)} %convolution_convert_fusion.1) | copy-start | bytes 442372
  552.1 324.4 %all-gather.23.cloned.1.call-start = ((), (), s32[]{:S(2)}) async-start(), calls=%async_computation.5 | async-start | bytes 1327104 | tf_op jit(solution)/shard_map/all_gather | solution.py:29
  596.5 42.2 %copy-start.20 = (f32[12,96]{1,0:T(8,128)S(1)}, f32[12,96]{1,0:T(8,128)}, u32[]{:S(2)}) copy-start(f32[12,96]{1,0:T(8,128)} %param.9) | copy-start | bytes 13828
  596.5 315.1 %all-gather.31.cloned.1.call-start = ((), (), s32[]{:S(2)}) async-start(), calls=%async_computation.9 | async-start | bytes 1327104 | tf_op jit(solution)/shard_map/all_gather | solution.py:29
  638.7 237.8 %copy-start.6 = (bf16[96,768]{1,0:T(8,128)(2,1)S(1)}, bf16[96,768]{1,0:T(8,128)(2,1)}, u32[]{:S(2)}) copy-start(bf16[96,768]{1,0:T(8,128)(2,1)} %fusion.9) | copy-start | bytes 442372
  876.4 35.2 %copy-start.9 = (bf16[96,768]{1,0:T(8,128)(2,1)S(1)}, bf16[96,768]{1,0:T(8,128)(2,1)}, u32[]{:S(2)}) copy-start(bf16[96,768]{1,0:T(8,128)(2,1)} %fusion.11) | copy-start | bytes 442372
  (3 other events, 8.4 us)
Sparse Core Ops, SparseCore 0:
  11.5 195.7 all-reduce.5
  211.7 83.1 all-gather.32
  297.8 37.9 all-gather.16
  338.6 39.1 all-gather.24
  380.5 44.6 all-gather.14
  427.8 38.6 all-gather.18
  469.4 40.2 all-gather.26
  512.6 37.4 reduce-scatter.4
  552.8 41.1 all-gather.20
  595.9 40.2 all-gather.28
  640.2 190.4 all-reduce.7
  833.4 35.6 all-gather.22
  871.4 40.1 all-gather.30
where the time goes:
time: 925 us; the launch traced here: 921 us
  waiting for transfers between devices  696 us (75%)
  blocking collectives  156 us (17%)
  matrix products  37.2 us (4%)
  between operations  16.2 us (2%)
  local copies, waits for them, and re-layouts  10.1 us (1%)
    unnamed x16, waiting for transfers between devices  426 us
    all_gather x6, waiting for transfers between devices, all_rows(): lax.all_gather(for_sending(pair), 'mp', axis=0, tiled=True)  190 us
    all_gather x1, blocking collectives, per_device(): lax.all_gather(grad_piece, 'dp', axis=0, tiled=True)  50.6 us
    all_gather x1, blocking collectives, per_device(): lax.all_gather(new_moment, 'dp', axis=0, tiled=True)  48.7 us
    all_gather x1, blocking collectives, per_device(): lax.all_gather(new_master.astype(jnp.bfloat16), 'dp', axis=0, tiled=True)  43.1 us
    all_gather x1, waiting for transfers between devices, per_device(): lax.all_gather(right_basis, 'mp', axis=1, tiled=True)  32.6 us
    all_gather x1, waiting for transfers between devices, per_device(): lax.all_gather(moment_cols, 'mp', axis=1, tiled=True)  25.3 us
    all_gather x1, waiting for transfers between devices, per_device(): lax.all_gather(grad_cols, 'mp', axis=1, tiled=True)  22.5 us
  transfers between devices with their start and end apart: 13, of which 11 were waited for; matrix products, arithmetic and copies ran while one was open for 5% of the time, Pallas kernels for 0%

commit v1 on v0

--- a/solution.py
+++ b/solution.py
@@ -37,24 +37,30 @@
     )
 
 
+def scatter_sum(x, axis):
+    count = lax.axis_size(axis)
+    chunks = x.reshape((count, x.shape[0] // count) + x.shape[1:])
+    return jnp.sum(lax.all_to_all(chunks, axis, 0, 0, tiled=False), axis=0)
+
+
+def gather_rows(x, axis):
+    count = lax.axis_size(axis)
+    return lax.all_to_all(jnp.broadcast_to(x[None], (count,) + x.shape), axis, 0, 0, tiled=False)
+
+
 def per_device(micro_grads, master, moment, second, left_basis, right_basis, left_stat, right_stat):
     dp_count = lax.axis_size("dp")
     micro_count = micro_grads.shape[1]
     local_sum = jnp.sum(micro_grads[0], axis=0, dtype=jnp.float32)
-    grad_piece = lax.psum_scatter(local_sum, "dp", scatter_dimension=0, tiled=True) / (
-        micro_count * dp_count
-    )
+    grad_piece = scatter_sum(local_sum, "dp") / (micro_count * dp_count)
     new_moment = beta_one * moment + (1.0 - beta_one) * grad_piece
-    grad_cols, moment_cols, left_full = (
-        lax.all_gather(grad_piece, "dp", axis=0, tiled=True),
-        lax.all_gather(new_moment, "dp", axis=0, tiled=True),
-        lax.all_gather(left_basis, "dp", axis=1, tiled=True),
-    )
-    grad_full, moment_full, right_full = (
-        lax.all_gather(grad_cols, "mp", axis=1, tiled=True),
-        lax.all_gather(moment_cols, "mp", axis=1, tiled=True),
-        lax.all_gather(right_basis, "mp", axis=1, tiled=True),
-    )
+    pieces = gather_rows(jnp.stack([grad_piece, new_moment]), "dp")
+    pieces = jnp.swapaxes(pieces, 0, 1).reshape(2, -1, pieces.shape[-1])
+    left_full = lax.all_gather(left_basis, "dp", axis=1, tiled=True)
+    both_full = lax.all_gather(pieces, "mp", axis=2, tiled=True)
+    right_full = lax.all_gather(right_basis, "mp", axis=1, tiled=True)
+    grad_full = both_full[0]
+    moment_full = both_full[1]
 
     def rotate(matrix):
         left_part = lax.dot_general(left_basis, matrix, (((0,), (0,)), ((), ())), precision=highest)
@@ -64,22 +70,18 @@
     rot_moment = rotate(moment_full)
     new_second = beta_two * second + (1.0 - beta_two) * rot_grad * rot_grad
     rot_step = rot_moment / (jnp.sqrt(new_second) + adam_eps)
-    basis_rows = right_basis
-    back_half = lax.psum_scatter(
-        lax.dot_general(basis_rows, rot_step, (((1,), (1,)), ((), ())), precision=highest),
+    back_half = scatter_sum(
+        lax.dot_general(right_basis, rot_step, (((1,), (1,)), ((), ())), precision=highest),
         "mp",
-        scatter_dimension=0,
-        tiled=True,
     )
-    basis_rows = left_basis
-    step_piece = lax.psum_scatter(
-        lax.dot_general(basis_rows, back_half, (((1,), (1,)), ((), ())), precision=highest),
+    step_piece = scatter_sum(
+        lax.dot_general(left_basis, back_half, (((1,), (1,)), ((), ())), precision=highest),
         "dp",
-        scatter_dimension=0,
-        tiled=True,
     )
     new_master = master - learn_rate * step_piece
-    weights_block = lax.all_gather(new_master.astype(jnp.bfloat16), "dp", axis=0, tiled=True)
+    weights_block = gather_rows(new_master.astype(jnp.bfloat16), "dp").reshape(
+        -1, new_master.shape[1]
+    )
     band_width = right_basis.shape[1]
     band_start = lax.axis_index("mp") * band_width
     grad_band = lax.dynamic_slice_in_dim(grad_full, band_start, band_width, 0)

time: 925 us -> 491 us (0.53)
  waiting for transfers between devices: 696 us -> 281 us
  blocking collectives: 156 us -> 138 us
    unnamed x16 -> x9, waiting for transfers between devices: 426 us -> 0.15 us
    all_gather x3 -> x0, blocking collectives: 142 us -> none  [the longest x1 50.6 us: per_device(): lax.all_gather(grad_piece, 'dp', axis=0, tiled=True)]
    all_to_all x0 -> x5, blocking collectives: none -> 125 us  [the longest x3 77.7 us: scatter_sum(): return jnp.sum(lax.all_to_all(chunks, axis, 0, 0, tiled=False), axis=0)]
    all_gather x4 -> x3, waiting for transfers between devices: 80.5 us -> 109 us  [the longest x1 57.9 us: per_device(): both_full = lax.all_gather(pieces, 'mp', axis=2, tiled=True)]
    all_gather x6, waiting for transfers between devices: 190 us -> 172 us  [all_rows(): lax.all_gather(for_sending(pair), 'mp', axis=0, tiled=True)]
    slice x0 -> x1, local copies, waits for them, and re-layouts: none -> 9.28 us  [per_device(): grad_full = both_full[0]]
  transfers between devices with their start and end apart: 13 -> 9, of which waited for: 11 -> 8; matrix products, arithmetic and copies ran while one was open for 5% -> 9% of each run, Pallas kernels for 0% -> 0%
where the time goes in v1:
time: 491 us; the launch traced here: 487 us
  waiting for transfers between devices  281 us (57%)
  blocking collectives  138 us (28%)
  matrix products  30.2 us (6%)
  local copies, waits for them, and re-layouts  16.3 us (3%)
  between operations  15.6 us (3%)
  other arithmetic  5.29 us (1%)
    all_gather x6, waiting for transfers between devices, all_rows(): lax.all_gather(for_sending(pair), 'mp', axis=0, tiled=True)  172 us
    all_to_all x3, blocking collectives, scatter_sum(): return jnp.sum(lax.all_to_all(chunks, axis, 0, 0, tiled=False), axis=0)  77.7 us
    all_gather x1, waiting for transfers between devices, per_device(): both_full = lax.all_gather(pieces, 'mp', axis=2, tiled=True)  57.9 us
    all_to_all x2, blocking collectives, gather_rows(): lax.all_to_all(jnp.broadcast_to(x[None], (count,) + x.shape), axis, 0, 0,...  47.1 us
    all_gather x1, waiting for transfers between devices, per_device(): left_full = lax.all_gather(left_basis, 'dp', axis=1, tiled=True)  28.4 us
    all_gather x1, waiting for transfers between devices, per_device(): right_full = lax.all_gather(right_basis, 'mp', axis=1, tiled=True)  22.8 us
    psum x1, blocking collectives, per_device(): lax.psum((jnp.sum(power_left * power_left), jnp.sum(power_right * power_r...  13.3 us
  transfers between devices with their start and end apart: 9, of which 8 were waited for; matrix products, arithmetic and copies ran while one was open for 9% of the time, Pallas kernels for 0%

profile of v1, /device:TPU:1, one launch (start us, length us, event | category | flops | bytes accessed | tf_op | source)
XLA Modules:
  0.0 487.2 jit_solution(16406727266121706216)
XLA Ops:
  7.2 1.4 bitcast_convert_fusion
  8.7 1.0 convert_reduce_fusion
  10.0 32.5 %all_to_all.25 = f32[64,12,96]{2,1,0:T(8,128)S(1)} all-to-all(f32[64,12,96]{2,1,0:T(8,128)S(1)} %reshape.45), channel_id=1, replica_groups=mesh['dp'=64,'mp'=8] {'dp'}, dimensions={0} | all-to-all | bytes 589824 | tf_op jit(solution)/shard_map/all_to_all | solution.py:43
  42.8 28.4 %all_to_all.26 = f32[64,2,12,96]{3,1,2,0:T(2,128)S(1)} all-to-all(f32[64,2,12,96]{3,1,2,0:T(2,128)S(1)} %broadcast_in_dim.4), channel_id=1, replica_groups=mesh['dp'=64,'mp'=8] {'dp'}, dimensions={0} | all-to-all | bytes 1179648 | tf_op jit(solution)/shard_map/all_to_all | solution.py:48
  71.2 1.2 copy.22
  73.4 28.4 %all-gather.27.cloned.1.call-done = bf16[64,12,768]{2,1,0:T(8,128)(2,1)} async-done(((bf16[1,12,768]{2,1,0:T(8,128)(2,1)}), bf16[64,12,768]{2,1,0:T(8,128)(2,1)}) %all-gather.27.cloned.1.call-update) | async-done | bytes 1179664 | tf_op jit(solution)/shard_map/all_gather | solution.py:59
  101.8 3.1 reshape.52
  105.0 57.9 %all-gather.11.cloned.1.call-done = f32[2,768,768]{1,0,2:T(2,128)} async-done(((f32[2,768,96]{1,0,2:T(2,128)}), f32[2,768,768]{1,0,2:T(2,128)}) %all-gather.11.cloned.1.call-update) | async-done | bytes 4718608 | tf_op jit(solution)/shard_map/all_gather | solution.py:60
  162.9 9.3 %fusion.53 = (f32[1,768,768]{1,0,2:T(1,128)S(1)}, f32[1,768,768]{1,0,2:T(1,128)}) fusion(f32[2,768,768]{1,0,2:T(2,128)} %all-gather.11.cloned.1.call-done), kind=kLoop, calls=%fused_computation.70 | loop fusion | bytes 9437184 | tf_op jit(solution)/shard_map/slice | solution.py:62
  172.2 0.9 constant_dynamic-slice_fusion.1
  173.1 1.5 fusion.23
  174.7 1.8 multiply_reduce_fusion.1
  176.5 2.4 fusion.20
  178.9 22.8 %all-gather.19.cloned.1.call-done = bf16[768,768]{0,1:T(8,128)(2,1)} async-done(((bf16[768,96]{0,1:T(8,128)(2,1)}), bf16[768,768]{0,1:T(8,128)(2,1)}) %all-gather.19.cloned.1.call-update) | async-done | bytes 1179664 | tf_op jit(solution)/shard_map/all_gather | solution.py:61
  201.8 2.4 multiply_reduce_fusion
  204.2 13.3 %all-reduce = (f32[]{:T(128)}, f32[]{:T(128)}) all-reduce(f32[]{:T(128)} %get-tuple-element.32, f32[]{:T(128)} %get-tuple-element.34), channel_id=1, replica_groups=mesh['dp'=64,'mp'=8] {'mp'}, use_global_device_ids=true, to_apply=%region_5.0 | all-reduce | flops 2 | bytes 16 | tf_op jit(solution)/shard_map/psum | solution.py:106
  220.4 43.0 %all-gather.21.cloned.1.call-done = bf16[768,768]{1,0:T(8,128)(2,1)} async-done(((bf16[96,768]{1,0:T(8,128)(2,1)}), bf16[768,768]{1,0:T(8,128)(2,1)}) %all-gather.21.cloned.1.call-update) | async-done | bytes 1179664 | tf_op jit(solution)/shard_map/all_gather | solution.py:29
  263.4 2.5 convolution_convert_fusion.1
  266.0 40.1 %all-gather.13.cloned.1.call-done = bf16[768,768]{1,0:T(8,128)(2,1)} async-done(((bf16[96,768]{1,0:T(8,128)(2,1)}), bf16[768,768]{1,0:T(8,128)(2,1)}) %all-gather.13.cloned.1.call-update) | async-done | bytes 1179664 | tf_op jit(solution)/shard_map/all_gather | solution.py:29
  306.2 2.4 convolution_convert_fusion.3
  308.7 40.2 %all-gather.23.cloned.1.call-done = bf16[768,768]{1,0:T(8,128)(2,1)} async-done(((bf16[96,768]{1,0:T(8,128)(2,1)}), bf16[768,768]{1,0:T(8,128)(2,1)}) %all-gather.23.cloned.1.call-update) | async-done | bytes 1179664 | tf_op jit(solution)/shard_map/all_gather | solution.py:29
  348.9 2.9 fusion.33
  352.1 2.0 fusion.4
  354.6 2.0 fusion.6
  356.6 35.2 %all-gather.15.cloned.1.call-done = bf16[768,768]{1,0:T(8,128)(2,1)} async-done(((bf16[96,768]{1,0:T(8,128)(2,1)}), bf16[768,768]{1,0:T(8,128)(2,1)}) %all-gather.15.cloned.1.call-update) | async-done | bytes 1179664 | tf_op jit(solution)/shard_map/all_gather | solution.py:29
  391.8 2.5 fusion.31
  395.1 11.5 %all_to_all.27 = f32[8,96,12]{1,2,0:T(8,128)S(1)} all-to-all(f32[8,96,12]{1,2,0:T(8,128)S(1)} %copy.23), channel_id=1, replica_groups=mesh['dp'=64,'mp'=8] {'mp'}, dimensions={0} | all-to-all | bytes 73728 | tf_op jit(solution)/shard_map/all_to_all | solution.py:43
  407.3 33.7 %all_to_all.28 = f32[64,12,96]{2,1,0:T(8,128)S(1)} all-to-all(f32[64,12,96]{2,1,0:T(8,128)S(1)} %reshape.48), channel_id=1, replica_groups=mesh['dp'=64,'mp'=8] {'dp'}, dimensions={0} | all-to-all | bytes 589824 | tf_op jit(solution)/shard_map/all_to_all | solution.py:43
  441.7 18.7 %all_to_all.29 = bf16[64,12,96]{2,1,0:T(8,128)(2,1)S(1)} all-to-all(bf16[64,12,96]{2,1,0:T(8,128)(2,1)S(1)} %broadcast_in_dim.5), channel_id=1, replica_groups=mesh['dp'=64,'mp'=8] {'dp'}, dimensions={0} | all-to-all | bytes 294912 | tf_op jit(solution)/shard_map/all_to_all | solution.py:48
  461.3 3.1 fusion.26
  464.4 13.2 %all-gather.17.cloned.1.call-done = bf16[768,768]{1,0:T(8,128)(2,1)} async-done(((bf16[96,768]{1,0:T(8,128)(2,1)}), bf16[768,768]{1,0:T(8,128)(2,1)}) %all-gather.17.cloned.1.call-update) | async-done | bytes 1179664 | tf_op jit(solution)/shard_map/all_gather | solution.py:29
  477.6 3.1 fusion.28
  (86 shorter events, 7.0 us)
Async XLA Ops:
  7.2 94.7 %all-gather.27.cloned.1.call-start = ((), (), s32[]{:S(2)}) async-start(), calls=%async_computation.13 | async-start | bytes 1597440 | tf_op jit(solution)/shard_map/all_gather | solution.py:59
  8.6 154.2 %all-gather.11.cloned.1.call-start = ((), (), s32[]{:S(2)}) async-start(), calls=%async_computation.5 | async-start | bytes 5308416 | tf_op jit(solution)/shard_map/all_gather | solution.py:60
  9.9 32.6 %copy-start.20 = (f32[12,96]{1,0:T(8,128)S(1)}, f32[12,96]{1,0:T(8,128)}, u32[]{:S(2)}) copy-start(f32[12,96]{1,0:T(8,128)} %param.10) | copy-start | bytes 13828
  42.5 28.7 %copy-start.17 = (f32[12,96]{1,0:T(8,128)}, f32[12,96]{1,0:T(8,128)S(1)}, u32[]{:S(2)}) copy-start(f32[12,96]{1,0:T(8,128)S(1)} %get-tuple-element.31) | copy-start | bytes 13828
  71.2 1.2 copy-start.1
  72.4 129.4 %all-gather.19.cloned.1.call-start = ((), (), s32[]{:S(2)}) async-start(), calls=%async_computation.9 | async-start | bytes 1327104 | tf_op jit(solution)/shard_map/all_gather | solution.py:61
  73.2 190.2 %all-gather.21.cloned.1.call-start = ((), (), s32[]{:S(2)}) async-start(), calls=%async_computation.10 | async-start | bytes 1327104 | tf_op jit(solution)/shard_map/all_gather | solution.py:29
  172.1 1.0 copy-start.14
  173.1 1.5 copy-start.3
  174.7 4.2 copy-start.10
  174.7 1.8 copy-start.15
  178.9 40.0 %copy-start.11 = (f32[96,768]{1,0:T(8,128)}, f32[96,768]{1,0:T(8,128)S(1)}, u32[]{:S(2)}) copy-start(f32[96,768]{1,0:T(8,128)S(1)} %fusion.20) | copy-start | bytes 884740
  201.8 17.8 %copy-start.12 = (f32[96,768]{1,0:T(8,128)S(1)}, f32[96,768]{1,0:T(8,128)}, u32[]{:S(2)}) copy-start(f32[96,768]{1,0:T(8,128)} %get-tuple-element.33) | copy-start | bytes 884740
  218.9 87.3 %all-gather.13.cloned.1.call-start = ((), (), s32[]{:S(2)}) async-start(), calls=%async_computation.6 | async-start | bytes 1327104 | tf_op jit(solution)/shard_map/all_gather | solution.py:29
  220.3 85.8 %copy-start.4 = (bf16[96,768]{1,0:T(8,128)(2,1)S(1)}, bf16[96,768]{1,0:T(8,128)(2,1)}, u32[]{:S(2)}) copy-start(bf16[96,768]{1,0:T(8,128)(2,1)} %multiply_convert_fusion.1) | copy-start | bytes 442372
  220.3 128.6 %all-gather.23.cloned.1.call-start = ((), (), s32[]{:S(2)}) async-start(), calls=%async_computation.11 | async-start | bytes 1327104 | tf_op jit(solution)/shard_map/all_gather | solution.py:29
  265.9 83.0 %copy-start.5 = (bf16[96,768]{1,0:T(8,128)(2,1)S(1)}, bf16[96,768]{1,0:T(8,128)(2,1)}, u32[]{:S(2)}) copy-start(bf16[96,768]{1,0:T(8,128)(2,1)} %multiply_convert_fusion) | copy-start | bytes 442372
  265.9 83.0 %copy-start.9 = (bf16[96,768]{1,0:T(8,128)(2,1)S(1)}, bf16[96,768]{1,0:T(8,128)(2,1)}, u32[]{:S(2)}) copy-start(bf16[96,768]{1,0:T(8,128)(2,1)} %convolution_convert_fusion.1) | copy-start | bytes 442372
  266.0 125.9 %all-gather.15.cloned.1.call-start = ((), (), s32[]{:S(2)}) async-start(), calls=%async_computation.7 | async-start | bytes 1327104 | tf_op jit(solution)/shard_map/all_gather | solution.py:29
  308.6 43.5 %copy-start.13 = (f32[768,12]{0,1:T(8,128)S(1)}, f32[768,12]{0,1:T(8,128)}, u32[]{:S(2)}) copy-start(f32[768,12]{0,1:T(8,128)} %param.12) | copy-start | bytes 110596
  308.6 152.7 %all-gather.25.cloned.1.call-start = ((), (), s32[]{:S(2)}) async-start(), calls=%async_computation.12 | async-start | bytes 1327104 | tf_op jit(solution)/shard_map/all_gather | solution.py:29
  351.8 2.4 copy-start.18
  351.8 125.8 %all-gather.17.cloned.1.call-start = ((), (), s32[]{:S(2)}) async-start(), calls=%async_computation.8 | async-start | bytes 1327104 | tf_op jit(solution)/shard_map/all_gather | solution.py:29
  352.1 2.4 copy-start
  354.5 39.9 %copy-start.16 = (f32[12,96]{1,0:T(8,128)}, f32[12,96]{1,0:T(8,128)S(1)}, u32[]{:S(2)}) copy-start(f32[12,96]{1,0:T(8,128)S(1)} %fusion.47) | copy-start | bytes 13828
  354.6 37.3 %copy-start.2 = (bf16[768,768]{1,0:T(8,128)(2,1)S(1)}, bf16[768,768]{1,0:T(8,128)(2,1)}, u32[]{:S(2)}) copy-start(bf16[768,768]{1,0:T(8,128)(2,1)} %all-gather.13.cloned.1.call-done) | copy-start | bytes 3538948
  354.6 37.2 %copy-start.8 = (bf16[96,768]{1,0:T(8,128)(2,1)S(1)}, bf16[96,768]{1,0:T(8,128)(2,1)}, u32[]{:S(2)}) copy-start(bf16[96,768]{1,0:T(8,128)(2,1)} %convolution_convert_fusion.3) | copy-start | bytes 442372
  407.2 33.8 %copy-start.19 = (f32[12,96]{1,0:T(8,128)S(1)}, f32[12,96]{1,0:T(8,128)}, u32[]{:S(2)}) copy-start(f32[12,96]{1,0:T(8,128)} %param.9) | copy-start | bytes 13828
  441.0 20.3 %copy-start.6 = (bf16[96,768]{1,0:T(8,128)(2,1)S(1)}, bf16[96,768]{1,0:T(8,128)(2,1)}, u32[]{:S(2)}) copy-start(bf16[96,768]{1,0:T(8,128)(2,1)} %fusion.33) | copy-start | bytes 442372
  461.3 16.3 %copy-start.7 = (bf16[96,768]{1,0:T(8,128)(2,1)S(1)}, bf16[96,768]{1,0:T(8,128)(2,1)}, u32[]{:S(2)}) copy-start(bf16[96,768]{1,0:T(8,128)(2,1)} %fusion.31) | copy-start | bytes 442372
Sparse Core Ops, SparseCore 0:
  11.9 89.8 all-gather.26
  103.9 58.9 all-gather.10
  165.5 36.2 all-gather.18
  219.0 44.3 all-gather.20
  265.9 40.2 all-gather.12
  308.7 40.2 all-gather.22
  351.6 40.2 all-gather.14
  394.5 40.2 all-gather.24
  437.4 40.1 all-gather.16

commit v2 on v1

--- a/solution.py
+++ b/solution.py
@@ -24,11 +24,8 @@
 
 
 def all_rows(pair):
-    return jax.tree.map(
-        lambda part, own: part.astype(own.dtype),
-        lax.all_gather(for_sending(pair), "mp", axis=0, tiled=True),
-        pair,
-    )
+    whole = lax.all_gather(jnp.stack(for_sending(pair)), "mp", axis=1, tiled=True)
+    return tuple(whole[side].astype(pair[side].dtype) for side in range(len(pair)))
 
 
 def row_gram(row_part, whole_part):
@@ -56,7 +53,8 @@
     new_moment = beta_one * moment + (1.0 - beta_one) * grad_piece
     pieces = gather_rows(jnp.stack([grad_piece, new_moment]), "dp")
     pieces = jnp.swapaxes(pieces, 0, 1).reshape(2, -1, pieces.shape[-1])
-    left_full = lax.all_gather(left_basis, "dp", axis=1, tiled=True)
+    left_cols = gather_rows(left_basis.astype(jnp.bfloat16), "dp")
+    left_full = jnp.moveaxis(left_cols, 0, 1).reshape(left_basis.shape[0], -1)
     both_full = lax.all_gather(pieces, "mp", axis=2, tiled=True)
     right_full = lax.all_gather(right_basis, "mp", axis=1, tiled=True)
     grad_full = both_full[0]

time: 491 us -> 372 us (0.76)
  waiting for transfers between devices: 281 us -> 165 us
  starting transfers between devices: 0.77 us -> 6.84 us
    all_gather x7 -> x3, waiting for transfers between devices: 200 us -> 91.5 us  [all_rows(): lax.all_gather(jnp.stack(for_sending(pair)), 'mp', axis=1, tiled=True)]
    all_gather x1, waiting for transfers between devices: 57.9 us -> 11.3 us  [per_device(): both_full = lax.all_gather(pieces, 'mp', axis=2, tiled=True)]
    all_to_all x0 -> x1, waiting for transfers between devices: none -> 38 us  [gather_rows(): lax.all_to_all(jnp.broadcast_to(x[None], (count,) + x.shape), axis, 0, 0,...]
    all_to_all x0 -> x1, starting transfers between devices: none -> 6.24 us  [gather_rows(): lax.all_to_all(jnp.broadcast_to(x[None], (count,) + x.shape), axis, 0, 0,...]
  transfers between devices with their start and end apart: 9 -> 6, of which waited for: 8 -> 5; matrix products, arithmetic and copies ran while one was open for 9% -> 7% of each run, Pallas kernels for 0% -> 0%
where the time goes in v2:
time: 372 us; the launch traced here: 371 us
  waiting for transfers between devices  165 us (44%)
  blocking collectives  137 us (37%)
  matrix products  25.8 us (7%)
  local copies, waits for them, and re-layouts  15.7 us (4%)
  between operations  15.5 us (4%)
  starting transfers between devices  6.84 us (2%)
  other arithmetic  6.42 us (2%)
    all_gather x3, waiting for transfers between devices, all_rows(): lax.all_gather(jnp.stack(for_sending(pair)), 'mp', axis=1, tiled=True)  91.5 us
    all_to_all x3, blocking collectives, scatter_sum(): return jnp.sum(lax.all_to_all(chunks, axis, 0, 0, tiled=False), axis=0)  76.6 us
    all_to_all x2, blocking collectives, gather_rows(): lax.all_to_all(jnp.broadcast_to(x[None], (count,) + x.shape), axis, 0, 0,...  47 us
    all_to_all x1, waiting for transfers between devices, gather_rows(): lax.all_to_all(jnp.broadcast_to(x[None], (count,) + x.shape), axis, 0, 0,...  38 us
    all_gather x1, waiting for transfers between devices, per_device(): right_full = lax.all_gather(right_basis, 'mp', axis=1, tiled=True)  23.8 us
    psum x1, blocking collectives, per_device(): lax.psum((jnp.sum(power_left * power_left), jnp.sum(power_right * power_r...  13 us
    all_gather x1, waiting for transfers between devices, per_device(): both_full = lax.all_gather(pieces, 'mp', axis=2, tiled=True)  11.3 us
    slice x1, local copies, waits for them, and re-layouts, per_device(): grad_full = both_full[0]  9.26 us
  transfers between devices with their start and end apart: 6, of which 5 were waited for; matrix products, arithmetic and copies ran while one was open for 7% of the time, Pallas kernels for 0%

profile of v2, /device:TPU:1, one launch (start us, length us, event | category | flops | bytes accessed | tf_op | source)
XLA Modules:
  0.0 371.5 jit_solution(14773298914813077104)
XLA Ops:
  7.2 1.0 convert_reduce_fusion
  8.5 32.4 %all_to_all.30 = f32[64,12,96]{2,1,0:T(8,128)S(1)} all-to-all(f32[64,12,96]{2,1,0:T(8,128)S(1)} %reshape.49), channel_id=1, replica_groups=mesh['dp'=64,'mp'=8] {'dp'}, dimensions={0} | all-to-all | bytes 589824 | tf_op jit(solution)/shard_map/all_to_all | solution.py:40
  41.2 28.3 %all_to_all.31 = f32[64,2,12,96]{3,1,2,0:T(2,128)S(1)} all-to-all(f32[64,2,12,96]{3,1,2,0:T(2,128)S(1)} %broadcast_in_dim.6), channel_id=1, replica_groups=mesh['dp'=64,'mp'=8] {'dp'}, dimensions={0} | all-to-all | bytes 1179648 | tf_op jit(solution)/shard_map/all_to_all | solution.py:45
  69.5 1.1 copy.23
  70.7 1.3 broadcast_in_dim.8
  72.0 6.2 %all-to-all-start.5 = ((bf16[64,768,12]{1,2,0:T(8,128)(2,1)}), bf16[64,768,12]{1,2,0:T(8,128)(2,1)S(1)}, u32[]{:S(2)}, u32[]{:S(2)}) async-start(bf16[64,768,12]{1,2,0:T(8,128)(2,1)} %broadcast_in_dim.8), calls=%async_computation.5 | async-start | bytes 3145728 | tf_op jit(solution)/shard_map/all_to_all | solution.py:45
  79.2 38.0 %all-to-all-done.5 = bf16[64,768,12]{1,2,0:T(8,128)(2,1)S(1)} async-done(((bf16[64,768,12]{1,2,0:T(8,128)(2,1)}), bf16[64,768,12]{1,2,0:T(8,128)(2,1)S(1)}, u32[]{:S(2)}, u32[]{:S(2)}) %all-to-all-start.5) | async-done | bytes 1179680 | tf_op jit(solution)/shard_map/all_to_all | solution.py:45
  117.2 1.2 reshape.54
  118.4 11.3 %all-gather.6.cloned.1.call-done = f32[2,768,768]{1,0,2:T(2,128)} async-done(((f32[2,768,96]{1,0,2:T(2,128)}), f32[2,768,768]{1,0,2:T(2,128)}) %all-gather.6.cloned.1.call-update) | async-done | bytes 4718608 | tf_op jit(solution)/shard_map/all_gather | solution.py:58
  129.7 9.3 %fusion.57 = (f32[1,768,768]{1,0,2:T(1,128)S(1)}, f32[1,768,768]{1,0,2:T(1,128)}) fusion(f32[2,768,768]{1,0,2:T(2,128)} %all-gather.6.cloned.1.call-done), kind=kLoop, calls=%fused_computation.81 | loop fusion | bytes 9437184 | tf_op jit(solution)/shard_map/slice | solution.py:60
  139.0 0.9 constant_dynamic-slice_fusion.1
  139.9 1.5 fusion.25
  141.5 1.1 multiply_reduce_fusion.1
  142.6 2.4 fusion.22
  145.0 23.8 %all-gather.8.cloned.1.call-done = bf16[768,768]{0,1:T(8,128)(2,1)} async-done(((bf16[768,96]{0,1:T(8,128)(2,1)}), bf16[768,768]{0,1:T(8,128)(2,1)}) %all-gather.8.cloned.1.call-update) | async-done | bytes 1179664 | tf_op jit(solution)/shard_map/all_gather | solution.py:59
  168.9 2.4 multiply_reduce_fusion
  171.3 13.0 %all-reduce = (f32[]{:T(128)}, f32[]{:T(128)}) all-reduce(f32[]{:T(128)} %get-tuple-element.32, f32[]{:T(128)} %get-tuple-element.34), channel_id=1, replica_groups=mesh['dp'=64,'mp'=8] {'mp'}, use_global_device_ids=true, to_apply=%region_5.0 | all-reduce | flops 2 | bytes 16 | tf_op jit(solution)/shard_map/psum | solution.py:104
  186.4 1.7 pad_maximum_fusion
  188.2 48.5 %all-gather.10.cloned.1.call-done = bf16[2,768,768]{2,1,0:T(8,128)(2,1)} async-done(((bf16[2,96,768]{2,1,0:T(8,128)(2,1)}), bf16[2,768,768]{2,1,0:T(8,128)(2,1)}) %all-gather.10.cloned.1.call-update) | async-done | bytes 2359312 | tf_op jit(solution)/shard_map/all_gather | solution.py:27
  236.6 1.9 convolution_convert_fusion.3
  238.5 1.8 convolution_convert_fusion.2
  241.4 43.0 %all-gather.12.cloned.1.call-done = bf16[2,768,768]{2,1,0:T(8,128)(2,1)} async-done(((bf16[2,96,768]{2,1,0:T(8,128)(2,1)}), bf16[2,768,768]{2,1,0:T(8,128)(2,1)}) %all-gather.12.cloned.1.call-update) | async-done | bytes 2359312 | tf_op jit(solution)/shard_map/all_gather | solution.py:27
  284.4 2.3 fusion.34
  286.8 2.2 fusion.35
  289.8 2.0 fusion.4
  292.2 2.0 fusion.6
  295.0 10.8 %all_to_all.32 = f32[8,96,12]{1,2,0:T(8,128)S(1)} all-to-all(f32[8,96,12]{1,2,0:T(8,128)S(1)} %copy.24), channel_id=1, replica_groups=mesh['dp'=64,'mp'=8] {'mp'}, dimensions={0} | all-to-all | bytes 73728 | tf_op jit(solution)/shard_map/all_to_all | solution.py:40
  306.5 33.4 %all_to_all.33 = f32[64,12,96]{2,1,0:T(8,128)S(1)} all-to-all(f32[64,12,96]{2,1,0:T(8,128)S(1)} %reshape.52), channel_id=1, replica_groups=mesh['dp'=64,'mp'=8] {'dp'}, dimensions={0} | all-to-all | bytes 589824 | tf_op jit(solution)/shard_map/all_to_all | solution.py:40
  340.7 18.7 %all_to_all.34 = bf16[64,12,96]{2,1,0:T(8,128)(2,1)S(1)} all-to-all(bf16[64,12,96]{2,1,0:T(8,128)(2,1)S(1)} %broadcast_in_dim.7), channel_id=1, replica_groups=mesh['dp'=64,'mp'=8] {'dp'}, dimensions={0} | all-to-all | bytes 294912 | tf_op jit(solution)/shard_map/all_to_all | solution.py:45
  359.4 0.8 copy.27
  360.2 3.2 fusion.33
  363.5 1.5 fusion.32
  (72 shorter events, 6.8 us)
Async XLA Ops:
  7.2 33.7 %copy-start.15 = (f32[12,96]{1,0:T(8,128)S(1)}, f32[12,96]{1,0:T(8,128)}, u32[]{:S(2)}) copy-start(f32[12,96]{1,0:T(8,128)} %param.10) | copy-start | bytes 13828
  7.2 122.5 %all-gather.6.cloned.1.call-start = ((), (), s32[]{:S(2)}) async-start(), calls=%async_computation.6 | async-start | bytes 5308416 | tf_op jit(solution)/shard_map/all_gather | solution.py:58
  40.8 29.8 %copy-start.5 = (f32[768,12]{0,1:T(8,128)S(1)}, f32[768,12]{0,1:T(8,128)}, u32[]{:S(2)}) copy-start(f32[768,12]{0,1:T(8,128)} %param.12) | copy-start | bytes 110596
  40.9 31.0 %copy-start.12 = (f32[12,96]{1,0:T(8,128)}, f32[12,96]{1,0:T(8,128)S(1)}, u32[]{:S(2)}) copy-start(f32[12,96]{1,0:T(8,128)S(1)} %get-tuple-element.31) | copy-start | bytes 13828
  70.6 7.6 %copy-start.1 = (f32[768,96]{0,1:T(8,128)S(1)}, f32[768,96]{0,1:T(8,128)}, u32[]{:S(2)}) copy-start(f32[768,96]{0,1:T(8,128)} %param.13) | copy-start | bytes 884740
  72.0 45.2 %all-to-all-start.5 = ((bf16[64,768,12]{1,2,0:T(8,128)(2,1)}), bf16[64,768,12]{1,2,0:T(8,128)(2,1)S(1)}, u32[]{:S(2)}, u32[]{:S(2)}) async-start(bf16[64,768,12]{1,2,0:T(8,128)(2,1)} %broadcast_in_dim.8), calls=%async_computation.5 | async-start | bytes 3145728 | tf_op jit(solution)/shard_map/all_to_all | solution.py:45
  78.2 90.7 %all-gather.8.cloned.1.call-start = ((), (), s32[]{:S(2)}) async-start(), calls=%async_computation.7 | async-start | bytes 1327104 | tf_op jit(solution)/shard_map/all_gather | solution.py:59
  79.0 157.7 %all-gather.10.cloned.1.call-start = ((), (), s32[]{:S(2)}) async-start(), calls=%async_computation.8 | async-start | bytes 2654208 | tf_op jit(solution)/shard_map/all_gather | solution.py:27
  118.4 21.5 %copy-start.8 = (f32[96,768]{1,0:T(8,128)S(1)}, f32[96,768]{1,0:T(8,128)}, u32[]{:S(2)}) copy-start(f32[96,768]{1,0:T(8,128)} %param.14) | copy-start | bytes 884740
  139.0 2.5 copy-start.2
  139.9 2.7 copy-start.9
  141.5 3.5 copy-start.3
  145.0 93.5 %copy-start.4 = (f32[96,768]{1,0:T(8,128)}, f32[96,768]{1,0:T(8,128)S(1)}, u32[]{:S(2)}) copy-start(f32[96,768]{1,0:T(8,128)S(1)} %fusion.22) | copy-start | bytes 884740
  186.4 98.1 %copy-start.7 = (bf16[96,768]{1,0:T(8,128)(2,1)S(1)}, bf16[96,768]{1,0:T(8,128)(2,1)}, u32[]{:S(2)}) copy-start(bf16[96,768]{1,0:T(8,128)(2,1)} %multiply_convert_fusion.1) | copy-start | bytes 442372
  188.1 96.3 %all-gather.12.cloned.1.call-start = ((), (), s32[]{:S(2)}) async-start(), calls=%async_computation.9 | async-start | bytes 2654208 | tf_op jit(solution)/shard_map/all_gather | solution.py:27
  238.5 2.9 copy-start.10
  241.1 119.1 %all-gather.14.cloned.1.call-start = ((), (), s32[]{:S(2)}) async-start(), calls=%async_computation.10 | async-start | bytes 2654208 | tf_op jit(solution)/shard_map/all_gather | solution.py:27
  286.7 3.0 copy-start.6
  289.0 2.9 copy-start.13
  289.8 2.4 copy-start
  292.2 14.3 %copy-start.11 = (f32[12,96]{1,0:T(8,128)}, f32[12,96]{1,0:T(8,128)S(1)}, u32[]{:S(2)}) copy-start(f32[12,96]{1,0:T(8,128)S(1)} %fusion.51) | copy-start | bytes 13828
  294.3 45.8 %copy-start.14 = (f32[12,96]{1,0:T(8,128)S(1)}, f32[12,96]{1,0:T(8,128)}, u32[]{:S(2)}) copy-start(f32[12,96]{1,0:T(8,128)} %param.9) | copy-start | bytes 13828
  360.2 3.2 copy-start.16
Sparse Core Ops, SparseCore 0:
  70.7 58.9 all-gather.5
  132.4 36.4 all-gather.7
  188.2 48.3 all-gather.9
  241.2 43.1 all-gather.11
  289.9 43.1 all-gather.13

commit v3 on v2

--- a/solution.py
+++ b/solution.py
@@ -55,8 +55,9 @@
     pieces = jnp.swapaxes(pieces, 0, 1).reshape(2, -1, pieces.shape[-1])
     left_cols = gather_rows(left_basis.astype(jnp.bfloat16), "dp")
     left_full = jnp.moveaxis(left_cols, 0, 1).reshape(left_basis.shape[0], -1)
+    right_full = lax.all_gather(right_basis, "mp", axis=1, tiled=True)
+    pieces, right_full = lax.optimization_barrier((pieces, right_full))
     both_full = lax.all_gather(pieces, "mp", axis=2, tiled=True)
-    right_full = lax.all_gather(right_basis, "mp", axis=1, tiled=True)
     grad_full = both_full[0]
     moment_full = both_full[1]
 
@@ -68,18 +69,6 @@
     rot_moment = rotate(moment_full)
     new_second = beta_two * second + (1.0 - beta_two) * rot_grad * rot_grad
     rot_step = rot_moment / (jnp.sqrt(new_second) + adam_eps)
-    back_half = scatter_sum(
-        lax.dot_general(right_basis, rot_step, (((1,), (1,)), ((), ())), precision=highest),
-        "mp",
-    )
-    step_piece = scatter_sum(
-        lax.dot_general(left_basis, back_half, (((1,), (1,)), ((), ())), precision=highest),
-        "dp",
-    )
-    new_master = master - learn_rate * step_piece
-    weights_block = gather_rows(new_master.astype(jnp.bfloat16), "dp").reshape(
-        -1, new_master.shape[1]
-    )
     band_width = right_basis.shape[1]
     band_start = lax.axis_index("mp") * band_width
     grad_band = lax.dynamic_slice_in_dim(grad_full, band_start, band_width, 0)
@@ -111,33 +100,37 @@
         (power_right * lax.rsqrt(total_right * (4.0 / order_count) + norm_eps)).astype(jnp.bfloat16)
     )
     start_rows = (start_left, start_right)
+    rot_step, start_rows = lax.optimization_barrier((rot_step, start_rows))
     start_whole = all_rows(start_rows)
-    gram_rows = tuple(
-        (
-            lax.optimization_barrier(row_gram(row_part, whole_part).astype(jnp.bfloat16))
-            for row_part, whole_part in zip(start_rows, start_whole)
+    back_half = scatter_sum(
+        lax.dot_general(right_basis, rot_step, (((1,), (1,)), ((), ())), precision=highest),
+        "mp",
+    )
+    step_piece = scatter_sum(
+        lax.dot_general(left_basis, back_half, (((1,), (1,)), ((), ())), precision=highest),
+        "dp",
+    )
+    new_master = master - learn_rate * step_piece
+    weights_block = gather_rows(new_master.astype(jnp.bfloat16), "dp").reshape(
+        -1, new_master.shape[1]
+    )
+    start_whole, weights_block, new_master = lax.optimization_barrier(
+        (start_whole, weights_block, new_master)
+    )
+    new_bases = []
+    for whole_part in start_whole:
+        gram = lax.optimization_barrier(row_gram(whole_part, whole_part).astype(jnp.bfloat16))
+        square = jnp.dot(gram, gram, preferred_element_type=jnp.float32)
+        poly = (quint_b * gram.astype(jnp.float32) + quint_c * square).astype(jnp.bfloat16)
+        middle = quint_a * whole_part.astype(jnp.float32) + jnp.dot(
+            poly, whole_part, preferred_element_type=jnp.float32
         )
-    )
-    gram_whole = all_rows(gram_rows)
-    middle_rows = []
-    for row_part, gram_part, gram_all, whole_part in zip(
-        start_rows, gram_rows, gram_whole, start_whole
-    ):
-        square = jnp.dot(gram_part, gram_all, preferred_element_type=jnp.float32)
-        poly_rows = (quint_b * gram_part.astype(jnp.float32) + quint_c * square).astype(
-            jnp.bfloat16
-        )
-        middle = quint_a * row_part.astype(jnp.float32) + jnp.dot(
-            poly_rows, whole_part, preferred_element_type=jnp.float32
-        )
-        middle_rows.append(lax.optimization_barrier(middle.astype(jnp.bfloat16)))
-    middle_whole = all_rows(tuple(middle_rows))
-    new_bases = []
-    for row_part, whole_part in zip(middle_rows, middle_whole):
-        gram_two = row_gram(row_part, whole_part).astype(jnp.bfloat16)
+        middle = lax.optimization_barrier(middle.astype(jnp.bfloat16))
+        middle_rows = lax.dynamic_slice_in_dim(middle, band_start, band_width, 0)
+        gram_two = row_gram(middle_rows, middle).astype(jnp.bfloat16)
         new_bases.append(
-            1.5 * row_part.astype(jnp.float32)
-            - 0.5 * jnp.dot(gram_two, whole_part, preferred_element_type=jnp.float32)
+            1.5 * middle_rows.astype(jnp.float32)
+            - 0.5 * jnp.dot(gram_two, middle, preferred_element_type=jnp.float32)
         )
     return (
         weights_block,

time: 372 us -> 264 us (0.71)
  waiting for transfers between devices: 165 us -> 65.1 us
  blocking collectives: 137 us -> 106 us
  starting transfers between devices: 6.84 us -> 25.6 us
    all_gather x3 -> x1, waiting for transfers between devices: 91.5 us -> 0.02 us  [all_rows(): lax.all_gather(jnp.stack(for_sending(pair)), 'mp', axis=1, tiled=True)]
    all_to_all x3 -> x2, blocking collectives: 76.6 us -> 46 us  [scatter_sum(): return jnp.sum(lax.all_to_all(chunks, axis, 0, 0, tiled=False), axis=0)]
    all_gather x1, waiting for transfers between devices: 23.8 us -> 0.01 us  [per_device(): right_full = lax.all_gather(right_basis, 'mp', axis=1, tiled=True)]
    all_to_all x0 -> x1, waiting for transfers between devices: none -> 16.9 us  [scatter_sum(): return jnp.sum(lax.all_to_all(chunks, axis, 0, 0, tiled=False), axis=0)]
    all_to_all x0 -> x1, starting transfers between devices: none -> 15 us  [scatter_sum(): return jnp.sum(lax.all_to_all(chunks, axis, 0, 0, tiled=False), axis=0)]
    all_to_all x1, starting transfers between devices: 6.24 us -> 10.3 us  [gather_rows(): lax.all_to_all(jnp.broadcast_to(x[None], (count,) + x.shape), axis, 0, 0,...]
  transfers between devices with their start and end apart: 6 -> 5, of which waited for: 5 -> 3; matrix products, arithmetic and copies ran while one was open for 7% -> 2% of each run, Pallas kernels for 0% -> 0%
where the time goes in v3:
time: 264 us; the launch traced here: 263 us
  blocking collectives  106 us (40%)
  waiting for transfers between devices  65.1 us (25%)
  matrix products  29.5 us (11%)
  starting transfers between devices  25.6 us (10%)
  local copies, waits for them, and re-layouts  17.8 us (7%)
  between operations  15.5 us (6%)
  other arithmetic  3.97 us (2%)
    all_to_all x2, blocking collectives, gather_rows(): lax.all_to_all(jnp.broadcast_to(x[None], (count,) + x.shape), axis, 0, 0,...  47 us
    all_to_all x2, blocking collectives, scatter_sum(): return jnp.sum(lax.all_to_all(chunks, axis, 0, 0, tiled=False), axis=0)  46 us
    all_to_all x1, waiting for transfers between devices, gather_rows(): lax.all_to_all(jnp.broadcast_to(x[None], (count,) + x.shape), axis, 0, 0,...  38.8 us
    all_to_all x1, waiting for transfers between devices, scatter_sum(): return jnp.sum(lax.all_to_all(chunks, axis, 0, 0, tiled=False), axis=0)  16.9 us
    all_to_all x1, starting transfers between devices, scatter_sum(): return jnp.sum(lax.all_to_all(chunks, axis, 0, 0, tiled=False), axis=0)  15 us
    psum x1, blocking collectives, per_device(): lax.psum((jnp.sum(power_left * power_left), jnp.sum(power_right * power_r...  12.8 us
    all_to_all x1, starting transfers between devices, gather_rows(): lax.all_to_all(jnp.broadcast_to(x[None], (count,) + x.shape), axis, 0, 0,...  10.3 us
    all_gather x1, waiting for transfers between devices, per_device(): both_full = lax.all_gather(pieces, 'mp', axis=2, tiled=True)  9.37 us
  transfers between devices with their start and end apart: 5, of which 3 were waited for; matrix products, arithmetic and copies ran while one was open for 2% of the time, Pallas kernels for 0%

profile of v3, /device:TPU:1, one launch (start us, length us, event | category | flops | bytes accessed | tf_op | source)
XLA Modules:
  0.0 263.2 jit_solution(14927035169419945519)
XLA Ops:
  7.2 1.0 convert_reduce_fusion
  8.4 0.8 reshape.49
  9.2 15.0 %all-to-all-start = ((f32[64,12,96]{2,1,0:T(8,128)}), f32[64,12,96]{2,1,0:T(8,128)S(1)}, u32[]{:S(2)}, u32[]{:S(2)}) async-start(f32[64,12,96]{2,1,0:T(8,128)} %reshape.49), calls=%async_computation | async-start | bytes 1048576 | tf_op jit(solution)/shard_map/all_to_all | solution.py:40
  25.0 16.9 %all-to-all-done = f32[64,12,96]{2,1,0:T(8,128)S(1)} async-done(((f32[64,12,96]{2,1,0:T(8,128)}), f32[64,12,96]{2,1,0:T(8,128)S(1)}, u32[]{:S(2)}, u32[]{:S(2)}) %all-to-all-start) | async-done | bytes 294944 | tf_op jit(solution)/shard_map/all_to_all | solution.py:40
  42.3 28.3 %all_to_all.30 = f32[64,2,12,96]{3,1,2,0:T(2,128)S(1)} all-to-all(f32[64,2,12,96]{3,1,2,0:T(2,128)S(1)} %broadcast_in_dim.6), channel_id=1, replica_groups=mesh['dp'=64,'mp'=8] {'dp'}, dimensions={0} | all-to-all | bytes 1179648 | tf_op jit(solution)/shard_map/all_to_all | solution.py:45
  70.6 1.1 copy.23
  71.7 1.3 broadcast_in_dim.7
  73.0 10.3 %all-to-all-start.2 = ((bf16[64,768,12]{1,2,0:T(8,128)(2,1)}), bf16[64,768,12]{1,2,0:T(8,128)(2,1)S(1)}, u32[]{:S(2)}, u32[]{:S(2)}) async-start(bf16[64,768,12]{1,2,0:T(8,128)(2,1)} %broadcast_in_dim.7), calls=%async_computation.2 | async-start | bytes 3145728 | tf_op jit(solution)/shard_map/all_to_all | solution.py:45
  83.6 38.8 %all-to-all-done.2 = bf16[64,768,12]{1,2,0:T(8,128)(2,1)S(1)} async-done(((bf16[64,768,12]{1,2,0:T(8,128)(2,1)}), bf16[64,768,12]{1,2,0:T(8,128)(2,1)S(1)}, u32[]{:S(2)}, u32[]{:S(2)}) %all-to-all-start.2) | async-done | bytes 1179680 | tf_op jit(solution)/shard_map/all_to_all | solution.py:45
  122.3 1.2 reshape.51
  123.5 9.4 %all-gather.6.cloned.1.call-done = f32[2,768,768]{1,0,2:T(2,128)} async-done(((f32[2,768,96]{1,0,2:T(2,128)}), f32[2,768,768]{1,0,2:T(2,128)}) %all-gather.6.cloned.1.call-update) | async-done | bytes 4718608 | tf_op jit(solution)/shard_map/all_gather | solution.py:60
  132.9 7.8 %fusion.47 = (f32[1,768,768]{1,0,2:T(1,128)S(1)}, f32[1,768,768]{1,0,2:T(1,128)S(1)}) fusion(f32[2,768,768]{1,0,2:T(2,128)} %all-gather.6.cloned.1.call-done), kind=kLoop, calls=%fused_computation.63 | loop fusion | bytes 9437184 | tf_op jit(solution)/shard_map/slice | solution.py:61
  140.8 0.9 constant_dynamic-slice_fusion.1
  141.7 2.7 %fusion.4 = f32[768,12]{0,1:T(8,128)} fusion(f32[768,12]{0,1:T(8,128)S(1)} %copy-done.6, f32[1,768,768]{1,0,2:T(1,128)S(1)} %get-tuple-element.46), kind=kOutput, calls=%fused_computation.4 | convolution fusion | flops 84934656 | bytes 2433024 | tf_op jit(solution)/shard_map/dot_general | solution.py:65
  144.4 2.4 fusion.20
  146.8 1.1 multiply_reduce_fusion
  147.9 1.6 fusion.23
  149.5 1.1 multiply_reduce_fusion.1
  150.7 12.8 %all-reduce = (f32[]{:T(128)}, f32[]{:T(128)}) all-reduce(f32[]{:T(128)} %get-tuple-element.52, f32[]{:T(128)} %get-tuple-element.54), channel_id=1, replica_groups=mesh['dp'=64,'mp'=8] {'mp'}, use_global_device_ids=true, to_apply=%region_3.0 | all-reduce | flops 2 | bytes 16 | tf_op jit(solution)/shard_map/psum | solution.py:93
  165.6 2.9 %fusion.6 = f32[768,12]{0,1:T(8,128)S(1)} fusion(f32[768,12]{0,1:T(8,128)} %param.12, f32[1,768,768]{1,0,2:T(1,128)S(1)} %get-tuple-element.47), kind=kOutput, calls=%fused_computation.6 | convolution fusion | flops 84934656 | bytes 2433024 | tf_op jit(solution)/shard_map/dot_general | solution.py:65
  170.4 12.3 %all_to_all.31 = f32[8,96,12]{1,2,0:T(8,128)S(1)} all-to-all(f32[8,96,12]{1,2,0:T(8,128)S(1)} %copy.24), channel_id=1, replica_groups=mesh['dp'=64,'mp'=8] {'mp'}, dimensions={0} | all-to-all | bytes 73728 | tf_op jit(solution)/shard_map/all_to_all | solution.py:40
  183.4 33.7 %all_to_all.32 = f32[64,12,96]{2,1,0:T(8,128)S(1)} all-to-all(f32[64,12,96]{2,1,0:T(8,128)S(1)} %reshape.53), channel_id=1, replica_groups=mesh['dp'=64,'mp'=8] {'dp'}, dimensions={0} | all-to-all | bytes 589824 | tf_op jit(solution)/shard_map/all_to_all | solution.py:40
  217.8 18.7 %all_to_all.33 = bf16[64,12,96]{2,1,0:T(8,128)(2,1)S(1)} all-to-all(bf16[64,12,96]{2,1,0:T(8,128)(2,1)S(1)} %broadcast_in_dim.8), channel_id=1, replica_groups=mesh['dp'=64,'mp'=8] {'dp'}, dimensions={0} | all-to-all | bytes 294912 | tf_op jit(solution)/shard_map/all_to_all | solution.py:45
  236.6 1.8 slice_bitcast_fusion
  238.4 1.0 copy-done.5
  239.4 2.1 convolution_convert_fusion
  241.6 4.9 %add_convert_fusion = bf16[768,768]{1,0:T(8,128)(2,1)S(1)} fusion(bf16[768,768]{1,0:T(8,128)(2,1)} %copy-done.5, bf16[768,768]{1,0:T(8,128)(2,1)} %convolution_convert_fusion), kind=kOutput, calls=%fused_computation.9 | convolution fusion | flops 1817247744 | bytes 3538944 | tf_op jit(solution)/shard_map/dot_general | solution.py:125
  246.5 1.5 fusion.26
  247.9 2.1 convolution_convert_fusion.1
  250.1 4.3 %add_convert_fusion.2 = bf16[768,768]{1,0:T(8,128)(2,1)S(1)} fusion(bf16[768,768]{1,0:T(8,128)(2,1)S(1)} %get-tuple-element.24, bf16[768,768]{1,0:T(8,128)(2,1)} %convolution_convert_fusion.1), kind=kOutput, calls=%fused_computation.11 | convolution fusion | flops 1817247744 | bytes 3538944 | tf_op jit(solution)/shard_map/dot_general | solution.py:125
  254.4 1.5 fusion.27
  255.8 0.8 copy.27
  (66 shorter events, 5.6 us)
Async XLA Ops:
  8.2 16.0 %copy-start = (f32[768,96]{0,1:T(8,128)S(1)}, f32[768,96]{0,1:T(8,128)}, u32[]{:S(2)}) copy-start(f32[768,96]{0,1:T(8,128)} %param.13) | copy-start | bytes 884740
  9.2 32.8 %copy-start.16 = (f32[12,96]{1,0:T(8,128)S(1)}, f32[12,96]{1,0:T(8,128)}, u32[]{:S(2)}) copy-start(f32[12,96]{1,0:T(8,128)} %param.10) | copy-start | bytes 13828
  9.2 32.7 %all-to-all-start = ((f32[64,12,96]{2,1,0:T(8,128)}), f32[64,12,96]{2,1,0:T(8,128)S(1)}, u32[]{:S(2)}, u32[]{:S(2)}) async-start(f32[64,12,96]{2,1,0:T(8,128)} %reshape.49), calls=%async_computation | async-start | bytes 1048576 | tf_op jit(solution)/shard_map/all_to_all | solution.py:40
  24.2 46.4 %all-gather.4.cloned.1.call-start = ((), (), s32[]{:S(2)}) async-start(), calls=%async_computation.6 | async-start | bytes 1327104 | tf_op jit(solution)/shard_map/all_gather | solution.py:58
  25.0 107.9 %all-gather.6.cloned.1.call-start = ((), (), s32[]{:S(2)}) async-start(), calls=%async_computation.7 | async-start | bytes 5308416 | tf_op jit(solution)/shard_map/all_gather | solution.py:60
  42.0 28.5 %copy-start.13 = (f32[12,96]{1,0:T(8,128)}, f32[12,96]{1,0:T(8,128)S(1)}, u32[]{:S(2)}) copy-start(f32[12,96]{1,0:T(8,128)S(1)} %get-tuple-element.51) | copy-start | bytes 13828
  70.6 1.2 copy-start.6
  73.0 49.3 %all-to-all-start.2 = ((bf16[64,768,12]{1,2,0:T(8,128)(2,1)}), bf16[64,768,12]{1,2,0:T(8,128)(2,1)S(1)}, u32[]{:S(2)}, u32[]{:S(2)}) async-start(bf16[64,768,12]{1,2,0:T(8,128)(2,1)} %broadcast_in_dim.7), calls=%async_computation.2 | async-start | bytes 3145728 | tf_op jit(solution)/shard_map/all_to_all | solution.py:45
  83.3 153.3 %all-gather.8.cloned.1.call-start = ((), (), s32[]{:S(2)}) async-start(), calls=%async_computation.8 | async-start | bytes 2654208 | tf_op jit(solution)/shard_map/all_gather | solution.py:27
  141.7 2.7 %copy-start.9 = (f32[96,768]{1,0:T(8,128)S(1)}, f32[96,768]{1,0:T(8,128)}, u32[]{:S(2)}) copy-start(f32[96,768]{1,0:T(8,128)} %param.15) | copy-start | bytes 884740
  144.3 2.4 copy-start.4
  146.8 2.8 %copy-start.2 = (f32[96,768]{1,0:T(8,128)}, f32[96,768]{1,0:T(8,128)S(1)}, u32[]{:S(2)}) copy-start(f32[96,768]{1,0:T(8,128)S(1)} %fusion.20) | copy-start | bytes 884740
  146.8 1.1 copy-start.10
  147.9 1.6 copy-start.1
  149.5 16.0 %copy-start.3 = (f32[96,768]{1,0:T(8,128)}, f32[96,768]{1,0:T(8,128)S(1)}, u32[]{:S(2)}) copy-start(f32[96,768]{1,0:T(8,128)S(1)} %fusion.23) | copy-start | bytes 884740
  165.6 2.9 %copy-start.11 = (f32[768,12]{0,1:T(8,128)S(1)}, f32[768,12]{0,1:T(8,128)}, u32[]{:S(2)}) copy-start(f32[768,12]{0,1:T(8,128)} %fusion.4) | copy-start | bytes 110596
  165.6 2.9 %copy-start.14 = (f32[12,96]{1,0:T(8,128)S(1)}, f32[12,96]{1,0:T(8,128)}, u32[]{:S(2)}) copy-start(f32[12,96]{1,0:T(8,128)} %param.11) | copy-start | bytes 13828
  165.6 3.6 %copy-start.8 = (bf16[96,768]{1,0:T(8,128)(2,1)S(1)}, bf16[96,768]{1,0:T(8,128)(2,1)}, u32[]{:S(2)}) copy-start(bf16[96,768]{1,0:T(8,128)(2,1)} %multiply_convert_fusion) | copy-start | bytes 442372
  168.5 14.2 %copy-start.7 = (f32[768,12]{0,1:T(8,128)S(1)}, f32[768,12]{0,1:T(8,128)}, u32[]{:S(2)}) copy-start(f32[768,12]{0,1:T(8,128)} %param.12) | copy-start | bytes 110596
  168.8 14.3 %copy-start.12 = (f32[12,96]{1,0:T(8,128)}, f32[12,96]{1,0:T(8,128)S(1)}, u32[]{:S(2)}) copy-start(f32[12,96]{1,0:T(8,128)S(1)} %fusion.37) | copy-start | bytes 13828
  183.3 33.9 %copy-start.15 = (f32[12,96]{1,0:T(8,128)S(1)}, f32[12,96]{1,0:T(8,128)}, u32[]{:S(2)}) copy-start(f32[12,96]{1,0:T(8,128)} %param.9) | copy-start | bytes 13828
  238.4 1.0 copy-start.5
Sparse Core Ops, SparseCore 0:
  27.7 38.5 all-gather.3
  71.8 60.9 all-gather.5
  170.1 44.9 all-gather.7

commit v4 on v3

--- a/solution.py
+++ b/solution.py
@@ -13,19 +13,6 @@
 quint_b = -1.25
 quint_c = 0.375
 highest = lax.Precision.HIGHEST
-
-
-def for_sending(x):
-
-    def short(part):
-        return part.astype(jnp.bfloat16) if part.dtype == jnp.float32 else part
-
-    return jax.tree.map(short, x)
-
-
-def all_rows(pair):
-    whole = lax.all_gather(jnp.stack(for_sending(pair)), "mp", axis=1, tiled=True)
-    return tuple(whole[side].astype(pair[side].dtype) for side in range(len(pair)))
 
 
 def row_gram(row_part, whole_part):
@@ -90,18 +77,9 @@
         right_full.astype(jnp.bfloat16),
         preferred_element_type=jnp.float32,
     )
-    total_left, total_right = lax.psum(
-        (jnp.sum(power_left * power_left), jnp.sum(power_right * power_right)), "mp"
-    )
-    start_left = lax.optimization_barrier(
-        (power_left * lax.rsqrt(total_left * (4.0 / order_count) + norm_eps)).astype(jnp.bfloat16)
-    )
-    start_right = lax.optimization_barrier(
-        (power_right * lax.rsqrt(total_right * (4.0 / order_count) + norm_eps)).astype(jnp.bfloat16)
-    )
-    start_rows = (start_left, start_right)
-    rot_step, start_rows = lax.optimization_barrier((rot_step, start_rows))
-    start_whole = all_rows(start_rows)
+    power_rows = jnp.stack([power_left, power_right])
+    rot_step, power_rows = lax.optimization_barrier((rot_step, power_rows))
+    power_whole = lax.all_gather(power_rows, "mp", axis=1, tiled=True)
     back_half = scatter_sum(
         lax.dot_general(right_basis, rot_step, (((1,), (1,)), ((), ())), precision=highest),
         "mp",
@@ -114,11 +92,12 @@
     weights_block = gather_rows(new_master.astype(jnp.bfloat16), "dp").reshape(
         -1, new_master.shape[1]
     )
-    start_whole, weights_block, new_master = lax.optimization_barrier(
-        (start_whole, weights_block, new_master)
-    )
     new_bases = []
-    for whole_part in start_whole:
+    for power_part in power_whole:
+        total = jnp.sum(power_part * power_part)
+        whole_part = lax.optimization_barrier(
+            (power_part * lax.rsqrt(total * (4.0 / order_count) + norm_eps)).astype(jnp.bfloat16)
+        )
         gram = lax.optimization_barrier(row_gram(whole_part, whole_part).astype(jnp.bfloat16))
         square = jnp.dot(gram, gram, preferred_element_type=jnp.float32)
         poly = (quint_b * gram.astype(jnp.float32) + quint_c * square).astype(jnp.bfloat16)

time: 264 us -> 243 us (0.920)
  blocking collectives: 106 us -> 88.1 us
  matrix products: 29.5 us -> 23.2 us
  other arithmetic: 3.97 us -> 9.71 us
  local copies, waits for them, and re-layouts: 17.8 us -> 14.8 us
    psum x1 -> x0, blocking collectives: 12.8 us -> none  [per_device(): lax.psum((jnp.sum(power_left * power_left), jnp.sum(power_right * power_r...]
    all_to_all x2, blocking collectives: 46 us -> 41.2 us  [scatter_sum(): return jnp.sum(lax.all_to_all(chunks, axis, 0, 0, tiled=False), axis=0)]
    reduce_sum x0 -> x1, other arithmetic: none -> 3.59 us  [per_device(): total = jnp.sum(power_part * power_part)]
    dot_general x2, matrix products: 9.15 us -> 6.42 us  [per_device(): jnp.dot(poly, whole_part, preferred_element_type=jnp.float32)]
where the time goes in v4:
time: 243 us
  blocking collectives  88.1 us (36%)
  waiting for transfers between devices  66 us (27%)
  starting transfers between devices  25.4 us (10%)
  matrix products  23.2 us (10%)
  between operations  15.5 us (6%)
  local copies, waits for them, and re-layouts  14.8 us (6%)
  other arithmetic  9.71 us (4%)
    all_to_all x2, blocking collectives, gather_rows(): lax.all_to_all(jnp.broadcast_to(x[None], (count,) + x.shape), axis, 0, 0,...  47 us
    all_to_all x2, blocking collectives, scatter_sum(): return jnp.sum(lax.all_to_all(chunks, axis, 0, 0, tiled=False), axis=0)  41.2 us
    all_to_all x1, waiting for transfers between devices, gather_rows(): lax.all_to_all(jnp.broadcast_to(x[None], (count,) + x.shape), axis, 0, 0,...  38.9 us
    all_to_all x1, waiting for transfers between devices, scatter_sum(): return jnp.sum(lax.all_to_all(chunks, axis, 0, 0, tiled=False), axis=0)  16.9 us
    all_to_all x1, starting transfers between devices, scatter_sum(): return jnp.sum(lax.all_to_all(chunks, axis, 0, 0, tiled=False), axis=0)  15 us
    all_to_all x1, starting transfers between devices, gather_rows(): lax.all_to_all(jnp.broadcast_to(x[None], (count,) + x.shape), axis, 0, 0,...  10.3 us
    all_gather x1, waiting for transfers between devices, per_device(): both_full = lax.all_gather(pieces, 'mp', axis=2, tiled=True)  10.1 us
    slice x1, local copies, waits for them, and re-layouts, per_device(): grad_full = both_full[0]  7.82 us
  transfers between devices with their start and end apart: 5, of which 3 were waited for; matrix products, arithmetic and copies ran while one was open for 2% of the time, Pallas kernels for 0%

profile of v4, /device:TPU:1, one launch (start us, length us, event | category | flops | bytes accessed | tf_op | source)
XLA Modules:
  0.0 242.7 jit_solution(772689149317146680)
XLA Ops:
  7.2 1.0 convert_reduce_fusion
  8.4 0.8 reshape.57
  9.2 15.0 %all-to-all-start = ((f32[64,12,96]{2,1,0:T(8,128)}), f32[64,12,96]{2,1,0:T(8,128)S(1)}, u32[]{:S(2)}, u32[]{:S(2)}) async-start(f32[64,12,96]{2,1,0:T(8,128)} %reshape.57), calls=%async_computation | async-start | bytes 1048576 | tf_op jit(solution)/shard_map/all_to_all | solution.py:27
  24.3 0.7 convert
  25.0 16.9 %all-to-all-done = f32[64,12,96]{2,1,0:T(8,128)S(1)} async-done(((f32[64,12,96]{2,1,0:T(8,128)}), f32[64,12,96]{2,1,0:T(8,128)S(1)}, u32[]{:S(2)}, u32[]{:S(2)}) %all-to-all-start) | async-done | bytes 294944 | tf_op jit(solution)/shard_map/all_to_all | solution.py:27
  42.3 28.3 %all_to_all.30 = f32[64,2,12,96]{3,1,2,0:T(2,128)S(1)} all-to-all(f32[64,2,12,96]{3,1,2,0:T(2,128)S(1)} %broadcast_in_dim.6), channel_id=1, replica_groups=mesh['dp'=64,'mp'=8] {'dp'}, dimensions={0} | all-to-all | bytes 1179648 | tf_op jit(solution)/shard_map/all_to_all | solution.py:32
  70.6 1.1 copy.23
  71.7 1.3 broadcast_in_dim.7
  73.0 10.3 %all-to-all-start.2 = ((bf16[64,768,12]{1,2,0:T(8,128)(2,1)}), bf16[64,768,12]{1,2,0:T(8,128)(2,1)S(1)}, u32[]{:S(2)}, u32[]{:S(2)}) async-start(bf16[64,768,12]{1,2,0:T(8,128)(2,1)} %broadcast_in_dim.7), calls=%async_computation.2 | async-start | bytes 3145728 | tf_op jit(solution)/shard_map/all_to_all | solution.py:32
  83.4 38.9 %all-to-all-done.2 = bf16[64,768,12]{1,2,0:T(8,128)(2,1)S(1)} async-done(((bf16[64,768,12]{1,2,0:T(8,128)(2,1)}), bf16[64,768,12]{1,2,0:T(8,128)(2,1)S(1)}, u32[]{:S(2)}, u32[]{:S(2)}) %all-to-all-start.2) | async-done | bytes 1179680 | tf_op jit(solution)/shard_map/all_to_all | solution.py:32
  122.8 10.1 %all-gather.6.cloned.1.call-done = f32[2,768,768]{1,0,2:T(2,128)} async-done(((f32[2,768,96]{1,0,2:T(2,128)}), f32[2,768,768]{1,0,2:T(2,128)}) %all-gather.6.cloned.1.call-update) | async-done | bytes 4718608 | tf_op jit(solution)/shard_map/all_gather | solution.py:47
  132.9 7.8 %fusion.51 = (f32[1,768,768]{1,0,2:T(1,128)S(1)}, f32[1,768,768]{1,0,2:T(1,128)S(1)}) fusion(f32[2,768,768]{1,0,2:T(2,128)} %all-gather.6.cloned.1.call-done), kind=kLoop, calls=%fused_computation.64 | loop fusion | bytes 9437184 | tf_op jit(solution)/shard_map/slice | solution.py:48
  140.8 0.9 constant_dynamic-slice_fusion.1
  141.7 2.0 fusion.4
  143.7 2.0 fusion.6
  145.8 2.4 fusion.25
  149.3 1.6 fusion.28
  150.9 0.7 convolution_bitcast_fusion
  151.6 0.9 pad_maximum_fusion
  153.6 11.3 %all_to_all.31 = f32[8,96,12]{1,2,0:T(8,128)S(1)} all-to-all(f32[8,96,12]{1,2,0:T(8,128)S(1)} %copy.24), channel_id=1, replica_groups=mesh['dp'=64,'mp'=8] {'mp'}, dimensions={0} | all-to-all | bytes 73728 | tf_op jit(solution)/shard_map/all_to_all | solution.py:27
  165.6 29.9 %all_to_all.32 = f32[64,12,96]{2,1,0:T(8,128)S(1)} all-to-all(f32[64,12,96]{2,1,0:T(8,128)S(1)} %reshape.61), channel_id=1, replica_groups=mesh['dp'=64,'mp'=8] {'dp'}, dimensions={0} | all-to-all | bytes 589824 | tf_op jit(solution)/shard_map/all_to_all | solution.py:27
  195.6 0.6 fusion.50
  196.2 18.7 %all_to_all.33 = bf16[64,12,96]{2,1,0:T(8,128)(2,1)S(1)} all-to-all(bf16[64,12,96]{2,1,0:T(8,128)(2,1)S(1)} %broadcast_in_dim.8), channel_id=1, replica_groups=mesh['dp'=64,'mp'=8] {'dp'}, dimensions={0} | all-to-all | bytes 294912 | tf_op jit(solution)/shard_map/all_to_all | solution.py:32
  215.0 0.8 copy.27
  215.8 3.6 %multiply_reduce_fusion = (f32[]{:T(128)}, f32[]{:T(128)}) fusion(f32[2,768,768]{2,1,0:T(8,128)} %all-gather.8.cloned.1.call-done), kind=kLoop, calls=%fused_computation.12 | loop fusion | flops 2359294 | bytes 4718600 | tf_op jit(solution)/shard_map/reduce_sum | solution.py:97
  220.8 2.7 %fusion.13 = (bf16[768,768]{1,0:T(8,128)(2,1)S(1)}, bf16[768,768]{1,0:T(8,128)(2,1)S(1)}) fusion(f32[2,768,768]{2,1,0:T(8,128)} %all-gather.8.cloned.1.call-done, f32[]{:T(128)S(6)} %rsqrt.7, f32[]{:T(128)S(6)} %rsqrt.6), kind=kLoop, calls=%fused_computation.23 | loop fusion | flops 2359296 | bytes 7077896 | tf_op jit(solution)/shard_map/convert_element_type | solution.py:99
  223.5 2.1 convolution_convert_fusion
  225.7 4.3 %add_convert_fusion = bf16[768,768]{1,0:T(8,128)(2,1)S(1)} fusion(bf16[768,768]{1,0:T(8,128)(2,1)S(1)} %get-tuple-element.36, bf16[768,768]{1,0:T(8,128)(2,1)} %convolution_convert_fusion), kind=kOutput, calls=%fused_computation.9 | convolution fusion | flops 1817247744 | bytes 3538944 | tf_op jit(solution)/shard_map/dot_general | solution.py:104
  230.0 1.5 fusion.31
  231.4 1.1 convolution_convert_fusion.1
  232.5 2.1 add_convert_fusion.2
  234.7 1.5 fusion.32
  (54 shorter events, 4.3 us)
Async XLA Ops:
  8.2 16.1 %copy-start = (f32[768,96]{0,1:T(8,128)S(1)}, f32[768,96]{0,1:T(8,128)}, u32[]{:S(2)}) copy-start(f32[768,96]{0,1:T(8,128)} %param.13) | copy-start | bytes 884740
  9.2 32.8 %copy-start.11 = (f32[12,96]{1,0:T(8,128)S(1)}, f32[12,96]{1,0:T(8,128)}, u32[]{:S(2)}) copy-start(f32[12,96]{1,0:T(8,128)} %param.10) | copy-start | bytes 13828
  9.2 32.7 %all-to-all-start = ((f32[64,12,96]{2,1,0:T(8,128)}), f32[64,12,96]{2,1,0:T(8,128)S(1)}, u32[]{:S(2)}, u32[]{:S(2)}) async-start(f32[64,12,96]{2,1,0:T(8,128)} %reshape.57), calls=%async_computation | async-start | bytes 1048576 | tf_op jit(solution)/shard_map/all_to_all | solution.py:27
  24.2 46.4 %all-gather.4.cloned.1.call-start = ((), (), s32[]{:S(2)}) async-start(), calls=%async_computation.6 | async-start | bytes 1327104 | tf_op jit(solution)/shard_map/all_gather | solution.py:45
  25.0 107.9 %all-gather.6.cloned.1.call-start = ((), (), s32[]{:S(2)}) async-start(), calls=%async_computation.7 | async-start | bytes 5308416 | tf_op jit(solution)/shard_map/all_gather | solution.py:47
  42.0 28.5 %copy-start.8 = (f32[12,96]{1,0:T(8,128)}, f32[12,96]{1,0:T(8,128)S(1)}, u32[]{:S(2)}) copy-start(f32[12,96]{1,0:T(8,128)S(1)} %get-tuple-element.41) | copy-start | bytes 13828
  70.6 1.2 copy-start.4
  73.0 49.3 %all-to-all-start.2 = ((bf16[64,768,12]{1,2,0:T(8,128)(2,1)}), bf16[64,768,12]{1,2,0:T(8,128)(2,1)S(1)}, u32[]{:S(2)}, u32[]{:S(2)}) async-start(bf16[64,768,12]{1,2,0:T(8,128)(2,1)} %broadcast_in_dim.7), calls=%async_computation.2 | async-start | bytes 3145728 | tf_op jit(solution)/shard_map/all_to_all | solution.py:32
  83.3 132.5 %all-gather.8.cloned.1.call-start = ((), (), s32[]{:S(2)}) async-start(), calls=%async_computation.8 | async-start | bytes 5308416 | tf_op jit(solution)/shard_map/all_gather | solution.py:82
  143.7 2.1 copy-start.5
  145.8 2.4 copy-start.3
  148.2 2.7 %copy-start.1 = (f32[96,768]{1,0:T(8,128)}, f32[96,768]{1,0:T(8,128)S(1)}, u32[]{:S(2)}) copy-start(f32[96,768]{1,0:T(8,128)S(1)} %fusion.25) | copy-start | bytes 884740
  148.2 1.1 copy-start.6
  150.9 1.6 copy-start.2
  150.9 1.6 copy-start.9
  152.8 12.7 %copy-start.7 = (f32[12,96]{1,0:T(8,128)}, f32[12,96]{1,0:T(8,128)S(1)}, u32[]{:S(2)}) copy-start(f32[12,96]{1,0:T(8,128)S(1)} %fusion.41) | copy-start | bytes 13828
  165.6 30.0 %copy-start.10 = (f32[12,96]{1,0:T(8,128)S(1)}, f32[12,96]{1,0:T(8,128)}, u32[]{:S(2)}) copy-start(f32[12,96]{1,0:T(8,128)} %param.9) | copy-start | bytes 13828
Sparse Core Ops, SparseCore 0:
  27.7 38.5 all-gather.3
  71.8 60.9 all-gather.5
  153.4 61.0 all-gather.7

commit v5 on v4

--- a/solution.py
+++ b/solution.py
@@ -38,22 +38,26 @@
     local_sum = jnp.sum(micro_grads[0], axis=0, dtype=jnp.float32)
     grad_piece = scatter_sum(local_sum, "dp") / (micro_count * dp_count)
     new_moment = beta_one * moment + (1.0 - beta_one) * grad_piece
-    pieces = gather_rows(jnp.stack([grad_piece, new_moment]), "dp")
-    pieces = jnp.swapaxes(pieces, 0, 1).reshape(2, -1, pieces.shape[-1])
+    moment_rows = gather_rows(moment, "mp")
+    moment_rows = jnp.moveaxis(moment_rows, 0, 1).reshape(moment.shape[0], -1)
+    moment_right = jnp.dot(moment_rows, right_basis, precision=highest)
+    moment_right = gather_rows(moment_right, "dp").reshape(-1, moment.shape[1])
+    moment_turned = lax.dot_general(
+        left_basis, moment_right, (((0,), (0,)), ((), ())), precision=highest
+    )
+    pieces = gather_rows(grad_piece, "dp").reshape(-1, grad_piece.shape[1])
     left_cols = gather_rows(left_basis.astype(jnp.bfloat16), "dp")
     left_full = jnp.moveaxis(left_cols, 0, 1).reshape(left_basis.shape[0], -1)
     right_full = lax.all_gather(right_basis, "mp", axis=1, tiled=True)
     pieces, right_full = lax.optimization_barrier((pieces, right_full))
-    both_full = lax.all_gather(pieces, "mp", axis=2, tiled=True)
-    grad_full = both_full[0]
-    moment_full = both_full[1]
+    grad_full = lax.all_gather(pieces, "mp", axis=1, tiled=True)
 
     def rotate(matrix):
         left_part = lax.dot_general(left_basis, matrix, (((0,), (0,)), ((), ())), precision=highest)
         return jnp.dot(left_part, right_basis, precision=highest)
 
     rot_grad = rotate(grad_full)
-    rot_moment = rotate(moment_full)
+    rot_moment = beta_one * moment_turned + (1.0 - beta_one) * rot_grad
     new_second = beta_two * second + (1.0 - beta_two) * rot_grad * rot_grad
     rot_step = rot_moment / (jnp.sqrt(new_second) + adam_eps)
     band_width = right_basis.shape[1]

time: 243 us -> 249 us (1.025)
  blocking collectives: 88.1 us -> 123 us
  starting transfers between devices: 25.4 us -> 13 us
  waiting for transfers between devices: 66 us -> 56.7 us
  local copies, waits for them, and re-layouts: 14.8 us -> 5.78 us
    all_to_all x2 -> x3, blocking collectives: 41.2 us -> 67.5 us  [scatter_sum(): return jnp.sum(lax.all_to_all(chunks, axis, 0, 0, tiled=False), axis=0)]
    all_to_all x1 -> x2, waiting for transfers between devices: 38.9 us -> 56.6 us  [gather_rows(): lax.all_to_all(jnp.broadcast_to(x[None], (count,) + x.shape), axis, 0, 0,...]
    all_to_all x1 -> x0, waiting for transfers between devices: 16.9 us -> none  [scatter_sum(): return jnp.sum(lax.all_to_all(chunks, axis, 0, 0, tiled=False), axis=0)]
    all_to_all x1 -> x0, starting transfers between devices: 15 us -> none  [scatter_sum(): return jnp.sum(lax.all_to_all(chunks, axis, 0, 0, tiled=False), axis=0)]
    all_gather x1, waiting for transfers between devices: 10.1 us -> 0.02 us  [per_device(): grad_full = lax.all_gather(pieces, 'mp', axis=1, tiled=True)]
    all_to_all x2 -> x3, blocking collectives: 47 us -> 55.8 us  [gather_rows(): lax.all_to_all(jnp.broadcast_to(x[None], (count,) + x.shape), axis, 0, 0,...]
    slice x1 -> x0, local copies, waits for them, and re-layouts: 7.82 us -> none  [per_device(): grad_full = both_full[0]]
    all_to_all x1 -> x2, starting transfers between devices: 10.3 us -> 12.9 us  [gather_rows(): lax.all_to_all(jnp.broadcast_to(x[None], (count,) + x.shape), axis, 0, 0,...]
  transfers between devices with their start and end apart: 5 -> 5, of which waited for: 3 -> 2; matrix products, arithmetic and copies ran while one was open for 2% -> 3% of each run, Pallas kernels for 0% -> 0%
where the time goes in v5:
time: 249 us
  blocking collectives  123 us (49%)
  waiting for transfers between devices  56.7 us (23%)
  matrix products  23.1 us (9%)
  between operations  15.5 us (6%)
  starting transfers between devices  13 us (5%)
  other arithmetic  11.3 us (5%)
  local copies, waits for them, and re-layouts  5.78 us (2%)
    all_to_all x3, blocking collectives, scatter_sum(): return jnp.sum(lax.all_to_all(chunks, axis, 0, 0, tiled=False), axis=0)  67.5 us
    all_to_all x2, waiting for transfers between devices, gather_rows(): lax.all_to_all(jnp.broadcast_to(x[None], (count,) + x.shape), axis, 0, 0,...  56.6 us
    all_to_all x3, blocking collectives, gather_rows(): lax.all_to_all(jnp.broadcast_to(x[None], (count,) + x.shape), axis, 0, 0,...  55.8 us
    all_to_all x2, starting transfers between devices, gather_rows(): lax.all_to_all(jnp.broadcast_to(x[None], (count,) + x.shape), axis, 0, 0,...  12.9 us
    dot_general x2, matrix products, per_device(): jnp.dot(poly, whole_part, preferred_element_type=jnp.float32)  6.42 us
  transfers between devices with their start and end apart: 5, of which 2 were waited for; matrix products, arithmetic and copies ran while one was open for 3% of the time, Pallas kernels for 0%

profile of v5, /device:TPU:1, one launch (start us, length us, event | category | flops | bytes accessed | tf_op | source)
XLA Modules:
  0.0 248.7 jit_solution(3923971289928613496)
XLA Ops:
  7.2 1.6 convert
  8.9 1.0 convert_reduce_fusion
  10.2 32.4 %all_to_all.40 = f32[64,12,96]{2,1,0:T(8,128)S(1)} all-to-all(f32[64,12,96]{2,1,0:T(8,128)S(1)} %reshape.58), channel_id=1, replica_groups=mesh['dp'=64,'mp'=8] {'dp'}, dimensions={0} | all-to-all | bytes 589824 | tf_op jit(solution)/shard_map/all_to_all | solution.py:27
  42.6 0.6 multiply_add_fusion
  43.3 23.2 %all_to_all.41 = f32[64,12,96]{2,1,0:T(8,128)S(1)} all-to-all(f32[64,12,96]{2,1,0:T(8,128)S(1)} %broadcast_in_dim.12), channel_id=1, replica_groups=mesh['dp'=64,'mp'=8] {'dp'}, dimensions={0} | all-to-all | bytes 589824 | tf_op jit(solution)/shard_map/all_to_all | solution.py:32
  66.6 0.9 copy.22
  67.5 13.9 %all_to_all.42 = f32[8,12,96]{2,1,0:T(8,128)S(1)} all-to-all(f32[8,12,96]{2,1,0:T(8,128)S(1)} %broadcast_in_dim.10), channel_id=1, replica_groups=mesh['dp'=64,'mp'=8] {'mp'}, dimensions={0} | all-to-all | bytes 73728 | tf_op jit(solution)/shard_map/all_to_all | solution.py:32
  81.8 0.9 broadcast_in_dim.11
  82.7 7.1 %all-to-all-start.1 = ((f32[64,12,96]{2,1,0:T(8,128)}), f32[64,12,96]{2,1,0:T(8,128)S(1)}, u32[]{:S(2)}, u32[]{:S(2)}) async-start(f32[64,12,96]{2,1,0:T(8,128)} %broadcast_in_dim.11), calls=%async_computation.1 | async-start | bytes 1048576 | tf_op jit(solution)/shard_map/all_to_all | solution.py:32
  89.8 17.7 %all-to-all-done.1 = f32[64,12,96]{2,1,0:T(8,128)S(1)} async-done(((f32[64,12,96]{2,1,0:T(8,128)}), f32[64,12,96]{2,1,0:T(8,128)S(1)}, u32[]{:S(2)}, u32[]{:S(2)}) %all-to-all-start.1) | async-done | bytes 294944 | tf_op jit(solution)/shard_map/all_to_all | solution.py:32
  107.5 1.2 broadcast_in_dim.13
  108.8 5.7 %all-to-all-start.4 = ((bf16[64,768,12]{1,2,0:T(8,128)(2,1)}), bf16[64,768,12]{1,2,0:T(8,128)(2,1)S(1)}, u32[]{:S(2)}, u32[]{:S(2)}) async-start(bf16[64,768,12]{1,2,0:T(8,128)(2,1)} %broadcast_in_dim.13), calls=%async_computation.4 | async-start | bytes 3145728 | tf_op jit(solution)/shard_map/all_to_all | solution.py:32
  114.6 38.9 %all-to-all-done.4 = bf16[64,768,12]{1,2,0:T(8,128)(2,1)S(1)} async-done(((bf16[64,768,12]{1,2,0:T(8,128)(2,1)}), bf16[64,768,12]{1,2,0:T(8,128)(2,1)S(1)}, u32[]{:S(2)}, u32[]{:S(2)}) %all-to-all-start.4) | async-done | bytes 1179680 | tf_op jit(solution)/shard_map/all_to_all | solution.py:32
  153.9 3.8 %fusion.35 = f32[768,12]{0,1:T(8,128)S(1)} fusion(f32[768,768]{0,1:T(8,128)} %all-gather.6.cloned.1.call-done, f32[768,12]{0,1:T(8,128)S(1)} %copy-done.5), kind=kOutput, calls=%fused_computation.55 | convolution fusion | flops 84934656 | bytes 2433024 | tf_op jit(solution)/shard_map/dot_general | solution.py:56
  158.1 2.4 fusion.7
  161.0 0.6 copy-done.7
  161.6 1.6 fusion.8
  163.3 0.5 convolution_bitcast_fusion
  164.0 0.9 pad_maximum_fusion
  165.6 9.8 %all_to_all.43 = f32[8,96,12]{1,2,0:T(8,128)S(1)} all-to-all(f32[8,96,12]{1,2,0:T(8,128)S(1)} %copy.23), channel_id=1, replica_groups=mesh['dp'=64,'mp'=8] {'mp'}, dimensions={0} | all-to-all | bytes 73728 | tf_op jit(solution)/shard_map/all_to_all | solution.py:27
  176.1 25.4 %all_to_all.44 = f32[64,12,96]{2,1,0:T(8,128)S(1)} all-to-all(f32[64,12,96]{2,1,0:T(8,128)S(1)} %reshape.62), channel_id=1, replica_groups=mesh['dp'=64,'mp'=8] {'dp'}, dimensions={0} | all-to-all | bytes 589824 | tf_op jit(solution)/shard_map/all_to_all | solution.py:27
  201.5 0.6 fusion.33
  202.2 18.7 %all_to_all.45 = bf16[64,12,96]{2,1,0:T(8,128)(2,1)S(1)} all-to-all(bf16[64,12,96]{2,1,0:T(8,128)(2,1)S(1)} %broadcast_in_dim.14), channel_id=1, replica_groups=mesh['dp'=64,'mp'=8] {'dp'}, dimensions={0} | all-to-all | bytes 294912 | tf_op jit(solution)/shard_map/all_to_all | solution.py:32
  221.0 0.8 copy.26
  221.8 3.6 %multiply_reduce_fusion = (f32[]{:T(128)}, f32[]{:T(128)}) fusion(f32[2,768,768]{2,1,0:T(8,128)} %all-gather.8.cloned.1.call-done), kind=kLoop, calls=%fused_computation.3 | loop fusion | flops 2359294 | bytes 4718600 | tf_op jit(solution)/shard_map/reduce_sum | solution.py:101
  226.7 2.7 %fusion.1 = (bf16[768,768]{1,0:T(8,128)(2,1)S(1)}, bf16[768,768]{1,0:T(8,128)(2,1)S(1)}) fusion(f32[2,768,768]{2,1,0:T(8,128)} %all-gather.8.cloned.1.call-done, f32[]{:T(128)S(6)} %rsqrt.7, f32[]{:T(128)S(6)} %rsqrt.6), kind=kLoop, calls=%fused_computation.11 | loop fusion | flops 2359296 | bytes 7077896 | tf_op jit(solution)/shard_map/convert_element_type | solution.py:103
  229.5 2.2 convolution_convert_fusion.1
  231.6 4.3 %add_convert_fusion.2 = bf16[768,768]{1,0:T(8,128)(2,1)S(1)} fusion(bf16[768,768]{1,0:T(8,128)(2,1)S(1)} %get-tuple-element.37, bf16[768,768]{1,0:T(8,128)(2,1)} %convolution_convert_fusion.1), kind=kOutput, calls=%fused_computation.4 | convolution fusion | flops 1817247744 | bytes 3538944 | tf_op jit(solution)/shard_map/dot_general | solution.py:108
  235.9 1.5 fusion.10
  237.4 1.1 convolution_convert_fusion
  238.5 2.1 add_convert_fusion
  240.7 1.5 fusion.9
  (57 shorter events, 4.0 us)
Async XLA Ops:
  7.2 59.4 %all-gather.4.cloned.1.call-start = ((), (), s32[]{:S(2)}) async-start(), calls=%async_computation.8 | async-start | bytes 1327104 | tf_op jit(solution)/shard_map/all_gather | solution.py:51
  8.9 145.0 %all-gather.6.cloned.1.call-start = ((), (), s32[]{:S(2)}) async-start(), calls=%async_computation.9 | async-start | bytes 2654208 | tf_op jit(solution)/shard_map/all_gather | solution.py:53
  10.1 32.5 %copy-start.9 = (f32[12,96]{1,0:T(8,128)S(1)}, f32[12,96]{1,0:T(8,128)}, u32[]{:S(2)}) copy-start(f32[12,96]{1,0:T(8,128)} %param.10) | copy-start | bytes 13828
  66.5 15.0 %copy-start.1 = (f32[768,96]{0,1:T(8,128)S(1)}, f32[768,96]{0,1:T(8,128)}, u32[]{:S(2)}) copy-start(f32[768,96]{0,1:T(8,128)} %param.13) | copy-start | bytes 884740
  67.5 22.3 %copy-start.5 = (f32[768,12]{0,1:T(8,128)S(1)}, f32[768,12]{0,1:T(8,128)}, u32[]{:S(2)}) copy-start(f32[768,12]{0,1:T(8,128)} %param.12) | copy-start | bytes 110596
  82.7 24.9 %all-to-all-start.1 = ((f32[64,12,96]{2,1,0:T(8,128)}), f32[64,12,96]{2,1,0:T(8,128)S(1)}, u32[]{:S(2)}, u32[]{:S(2)}) async-start(f32[64,12,96]{2,1,0:T(8,128)} %broadcast_in_dim.11), calls=%async_computation.1 | async-start | bytes 1048576 | tf_op jit(solution)/shard_map/all_to_all | solution.py:32
  108.8 44.7 %all-to-all-start.4 = ((bf16[64,768,12]{1,2,0:T(8,128)(2,1)}), bf16[64,768,12]{1,2,0:T(8,128)(2,1)S(1)}, u32[]{:S(2)}, u32[]{:S(2)}) async-start(bf16[64,768,12]{1,2,0:T(8,128)(2,1)} %broadcast_in_dim.13), calls=%async_computation.4 | async-start | bytes 3145728 | tf_op jit(solution)/shard_map/all_to_all | solution.py:32
  114.5 107.3 %all-gather.8.cloned.1.call-start = ((), (), s32[]{:S(2)}) async-start(), calls=%async_computation.10 | async-start | bytes 5308416 | tf_op jit(solution)/shard_map/all_gather | solution.py:86
  153.8 3.9 %copy-start.10 = (f32[12,96]{1,0:T(8,128)S(1)}, f32[12,96]{1,0:T(8,128)}, u32[]{:S(2)}) copy-start(f32[12,96]{1,0:T(8,128)} %param.11) | copy-start | bytes 13828
  153.8 4.3 %copy-start.6 = (f32[96,768]{1,0:T(8,128)S(1)}, f32[96,768]{1,0:T(8,128)}, u32[]{:S(2)}) copy-start(f32[96,768]{1,0:T(8,128)} %param.15) | copy-start | bytes 884740
  153.8 4.2 %copy-start = (f32[768,768]{0,1:T(8,128)S(1)}, f32[768,768]{0,1:T(8,128)}, u32[]{:S(2)}) copy-start(f32[768,768]{0,1:T(8,128)} %all-gather.6.cloned.1.call-done) | copy-start | bytes 7077892
  158.1 6.8 %copy-start.8 = (f32[12,96]{1,0:T(8,128)}, f32[12,96]{1,0:T(8,128)S(1)}, u32[]{:S(2)}) copy-start(f32[12,96]{1,0:T(8,128)S(1)} %get-tuple-element.40) | copy-start | bytes 13828
  158.1 2.4 copy-start.4
  160.5 2.7 %copy-start.2 = (f32[96,768]{1,0:T(8,128)}, f32[96,768]{1,0:T(8,128)S(1)}, u32[]{:S(2)}) copy-start(f32[96,768]{1,0:T(8,128)S(1)} %fusion.7) | copy-start | bytes 884740
  160.5 1.1 copy-start.7
  163.3 0.7 copy-start.3
  176.0 25.5 %copy-start.11 = (f32[12,96]{1,0:T(8,128)S(1)}, f32[12,96]{1,0:T(8,128)}, u32[]{:S(2)}) copy-start(f32[12,96]{1,0:T(8,128)} %param.9) | copy-start | bytes 13828
Sparse Core Ops, SparseCore 0:
  10.7 43.0 all-gather.3
  67.6 37.5 all-gather.5
  165.3 54.5 all-gather.7

commit v6 on v4

--- a/solution.py
+++ b/solution.py
@@ -67,19 +67,9 @@
     new_left_stat = beta_stat * left_stat + (1.0 - beta_stat) * left_outer
     new_right_stat = beta_stat * right_stat + (1.0 - beta_stat) * right_outer
     order_count = left_stat.shape[1]
-    power_left = jnp.dot(
-        new_left_stat.astype(jnp.bfloat16),
-        left_full.astype(jnp.bfloat16),
-        preferred_element_type=jnp.float32,
-    )
-    power_right = jnp.dot(
-        new_right_stat.astype(jnp.bfloat16),
-        right_full.astype(jnp.bfloat16),
-        preferred_element_type=jnp.float32,
-    )
-    power_rows = jnp.stack([power_left, power_right])
-    rot_step, power_rows = lax.optimization_barrier((rot_step, power_rows))
-    power_whole = lax.all_gather(power_rows, "mp", axis=1, tiled=True)
+    stat_rows = jnp.stack([new_left_stat, new_right_stat]).astype(jnp.bfloat16)
+    rot_step, stat_rows = lax.optimization_barrier((rot_step, stat_rows))
+    stat_whole = lax.all_gather(stat_rows, "mp", axis=1, tiled=True)
     back_half = scatter_sum(
         lax.dot_general(right_basis, rot_step, (((1,), (1,)), ((), ())), precision=highest),
         "mp",
@@ -93,7 +83,10 @@
         -1, new_master.shape[1]
     )
     new_bases = []
-    for power_part in power_whole:
+    for stat_part, basis_part in zip(stat_whole, (left_full, right_full)):
+        power_part = jnp.dot(
+            stat_part, basis_part.astype(jnp.bfloat16), preferred_element_type=jnp.float32
+        )
         total = jnp.sum(power_part * power_part)
         whole_part = lax.optimization_barrier(
             (power_part * lax.rsqrt(total * (4.0 / order_count) + norm_eps)).astype(jnp.bfloat16)

time: 243 us -> 293 us (1.21)
  waiting for transfers between devices: 66 us -> 147 us
  blocking collectives: 88.1 us -> 39.6 us
  starting transfers between devices: 25.4 us -> 39.9 us
  other arithmetic: 9.71 us -> 3.66 us
  matrix products: 23.2 us -> 29 us
    all_gather x1, waiting for transfers between devices: 10.1 us -> 60.9 us  [per_device(): both_full = lax.all_gather(pieces, 'mp', axis=2, tiled=True)]
    all_to_all x2 -> x1, blocking collectives: 41.2 us -> 11.3 us  [scatter_sum(): return jnp.sum(lax.all_to_all(chunks, axis, 0, 0, tiled=False), axis=0)]
    all_to_all x2 -> x1, blocking collectives: 47 us -> 28.3 us  [gather_rows(): lax.all_to_all(jnp.broadcast_to(x[None], (count,) + x.shape), axis, 0, 0,...]
    all_to_all x1 -> x2, waiting for transfers between devices: 16.9 us -> 34.6 us  [scatter_sum(): return jnp.sum(lax.all_to_all(chunks, axis, 0, 0, tiled=False), axis=0)]
    all_to_all x1 -> x2, starting transfers between devices: 15 us -> 27.3 us  [scatter_sum(): return jnp.sum(lax.all_to_all(chunks, axis, 0, 0, tiled=False), axis=0)]
    all_to_all x1 -> x2, waiting for transfers between devices: 38.9 us -> 51.1 us  [gather_rows(): lax.all_to_all(jnp.broadcast_to(x[None], (count,) + x.shape), axis, 0, 0,...]
    dot_general x2, matrix products: 1.2 us -> 6.74 us  [per_device(): jnp.dot(stat_part, basis_part.astype(jnp.bfloat16), preferred_element_typ...]
    reduce_sum x1 -> x0, other arithmetic: 3.59 us -> none  [per_device(): total = jnp.sum(power_part * power_part)]
  transfers between devices with their start and end apart: 5 -> 7, of which waited for: 3 -> 5; matrix products, arithmetic and copies ran while one was open for 2% -> 2% of each run, Pallas kernels for 0% -> 0%
where the time goes in v6:
time: 293 us; the launch traced here: 292 us
  waiting for transfers between devices  147 us (50%)
  starting transfers between devices  39.9 us (14%)
  blocking collectives  39.6 us (14%)
  matrix products  29 us (10%)
  local copies, waits for them, and re-layouts  17.6 us (6%)
  between operations  15.5 us (5%)
  other arithmetic  3.66 us (1%)
    all_gather x1, waiting for transfers between devices, per_device(): both_full = lax.all_gather(pieces, 'mp', axis=2, tiled=True)  60.9 us
    all_to_all x2, waiting for transfers between devices, gather_rows(): lax.all_to_all(jnp.broadcast_to(x[None], (count,) + x.shape), axis, 0, 0,...  51.1 us
    all_to_all x2, waiting for transfers between devices, scatter_sum(): return jnp.sum(lax.all_to_all(chunks, axis, 0, 0, tiled=False), axis=0)  34.6 us
    all_to_all x1, blocking collectives, gather_rows(): lax.all_to_all(jnp.broadcast_to(x[None], (count,) + x.shape), axis, 0, 0,...  28.3 us
    all_to_all x2, starting transfers between devices, scatter_sum(): return jnp.sum(lax.all_to_all(chunks, axis, 0, 0, tiled=False), axis=0)  27.3 us
    all_to_all x2, starting transfers between devices, gather_rows(): lax.all_to_all(jnp.broadcast_to(x[None], (count,) + x.shape), axis, 0, 0,...  12.3 us
    all_to_all x1, blocking collectives, scatter_sum(): return jnp.sum(lax.all_to_all(chunks, axis, 0, 0, tiled=False), axis=0)  11.3 us
    slice x1, local copies, waits for them, and re-layouts, per_device(): grad_full = both_full[0]  7.82 us
  transfers between devices with their start and end apart: 7, of which 5 were waited for; matrix products, arithmetic and copies ran while one was open for 2% of the time, Pallas kernels for 0%

profile of v6, /device:TPU:1, one launch (start us, length us, event | category | flops | bytes accessed | tf_op | source)
XLA Modules:
  0.0 292.1 jit_solution(14827559212118366138)
XLA Ops:
  7.2 1.0 convert_reduce_fusion
  8.4 0.8 reshape.49
  9.2 15.0 %all-to-all-start = ((f32[64,12,96]{2,1,0:T(8,128)}), f32[64,12,96]{2,1,0:T(8,128)S(1)}, u32[]{:S(2)}, u32[]{:S(2)}) async-start(f32[64,12,96]{2,1,0:T(8,128)} %reshape.49), calls=%async_computation | async-start | bytes 1048576 | tf_op jit(solution)/shard_map/all_to_all | solution.py:27
  25.0 16.9 %all-to-all-done = f32[64,12,96]{2,1,0:T(8,128)S(1)} async-done(((f32[64,12,96]{2,1,0:T(8,128)}), f32[64,12,96]{2,1,0:T(8,128)S(1)}, u32[]{:S(2)}, u32[]{:S(2)}) %all-to-all-start) | async-done | bytes 294944 | tf_op jit(solution)/shard_map/all_to_all | solution.py:27
  42.3 28.3 %all_to_all.30 = f32[64,2,12,96]{3,1,2,0:T(2,128)S(1)} all-to-all(f32[64,2,12,96]{3,1,2,0:T(2,128)S(1)} %broadcast_in_dim.6), channel_id=1, replica_groups=mesh['dp'=64,'mp'=8] {'dp'}, dimensions={0} | all-to-all | bytes 1179648 | tf_op jit(solution)/shard_map/all_to_all | solution.py:32
  70.6 1.1 copy.23
  72.0 60.9 %all-gather.6.cloned.1.call-done = f32[2,768,768]{1,0,2:T(2,128)} async-done(((f32[2,768,96]{1,0,2:T(2,128)}), f32[2,768,768]{1,0,2:T(2,128)}) %all-gather.6.cloned.1.call-update) | async-done | bytes 4718608 | tf_op jit(solution)/shard_map/all_gather | solution.py:47
  132.9 7.8 %fusion.45 = (f32[1,768,768]{1,0,2:T(1,128)S(1)}, f32[1,768,768]{1,0,2:T(1,128)S(1)}) fusion(f32[2,768,768]{1,0,2:T(2,128)} %all-gather.6.cloned.1.call-done), kind=kLoop, calls=%fused_computation.63 | loop fusion | bytes 9437184 | tf_op jit(solution)/shard_map/slice | solution.py:48
  140.7 0.9 constant_dynamic-slice_fusion.1
  141.7 2.0 fusion.4
  143.8 2.0 fusion.6
  145.8 1.6 fusion.24
  147.5 2.4 fusion.21
  152.0 11.3 %all_to_all.31 = f32[8,96,12]{1,2,0:T(8,128)S(1)} all-to-all(f32[8,96,12]{1,2,0:T(8,128)S(1)} %copy.24), channel_id=1, replica_groups=mesh['dp'=64,'mp'=8] {'mp'}, dimensions={0} | all-to-all | bytes 73728 | tf_op jit(solution)/shard_map/all_to_all | solution.py:27
  164.0 0.8 reshape.52
  164.8 12.4 %all-to-all-start.3 = ((f32[64,12,96]{2,1,0:T(8,128)}), f32[64,12,96]{2,1,0:T(8,128)S(1)}, u32[]{:S(2)}, u32[]{:S(2)}) async-start(f32[64,12,96]{2,1,0:T(8,128)} %reshape.52), calls=%async_computation.3 | async-start | bytes 1048576 | tf_op jit(solution)/shard_map/all_to_all | solution.py:27
  177.2 17.7 %all-to-all-done.3 = f32[64,12,96]{2,1,0:T(8,128)S(1)} async-done(((f32[64,12,96]{2,1,0:T(8,128)}), f32[64,12,96]{2,1,0:T(8,128)S(1)}, u32[]{:S(2)}, u32[]{:S(2)}) %all-to-all-start.3) | async-done | bytes 294944 | tf_op jit(solution)/shard_map/all_to_all | solution.py:27
  194.9 1.3 broadcast_in_dim.8
  196.1 5.9 %all-to-all-start.5 = ((bf16[64,768,12]{1,2,0:T(8,128)(2,1)}), bf16[64,768,12]{1,2,0:T(8,128)(2,1)S(1)}, u32[]{:S(2)}, u32[]{:S(2)}) async-start(bf16[64,768,12]{1,2,0:T(8,128)(2,1)} %broadcast_in_dim.8), calls=%async_computation.5 | async-start | bytes 3145728 | tf_op jit(solution)/shard_map/all_to_all | solution.py:32
  202.7 38.3 %all-to-all-done.5 = bf16[64,768,12]{1,2,0:T(8,128)(2,1)S(1)} async-done(((bf16[64,768,12]{1,2,0:T(8,128)(2,1)}), bf16[64,768,12]{1,2,0:T(8,128)(2,1)S(1)}, u32[]{:S(2)}, u32[]{:S(2)}) %all-to-all-start.5) | async-done | bytes 1179680 | tf_op jit(solution)/shard_map/all_to_all | solution.py:32
  241.7 6.5 %all-to-all-start.4 = ((bf16[64,12,96]{2,1,0:T(8,128)(2,1)}), bf16[64,12,96]{2,1,0:T(8,128)(2,1)S(1)}, u32[]{:S(2)}, u32[]{:S(2)}) async-start(bf16[64,12,96]{2,1,0:T(8,128)(2,1)} %broadcast_in_dim.7), calls=%async_computation.4 | async-start | bytes 524288 | tf_op jit(solution)/shard_map/all_to_all | solution.py:32
  248.5 12.8 %all-to-all-done.4 = bf16[64,12,96]{2,1,0:T(8,128)(2,1)S(1)} async-done(((bf16[64,12,96]{2,1,0:T(8,128)(2,1)}), bf16[64,12,96]{2,1,0:T(8,128)(2,1)S(1)}, u32[]{:S(2)}, u32[]{:S(2)}) %all-to-all-start.4) | async-done | bytes 147488 | tf_op jit(solution)/shard_map/all_to_all | solution.py:32
  262.3 3.5 %multiply_reduce_fusion = (f32[]{:T(128)}, f32[768,768]{1,0:T(8,128)S(1)}) fusion(bf16[768,768]{0,1:T(8,128)(2,1)} %all-gather.4.cloned.1.call-done, bf16[2,768,768]{2,1,0:T(8,128)(2,1)} %all-gather.8.cloned.1.call-done), kind=kOutput, calls=%fused_computation.12 | convolution fusion | flops 907149312 | bytes 4718596 | tf_op jit(solution)/shard_map/dot_general | solution.py:87
  266.7 1.0 copy-done.3
  267.7 1.1 convolution_convert_fusion
  268.9 3.8 %add_convert_fusion = bf16[768,768]{1,0:T(8,128)(2,1)S(1)} fusion(bf16[768,768]{1,0:T(8,128)(2,1)} %copy-done.3, bf16[768,768]{1,0:T(8,128)(2,1)S(1)} %convolution_convert_fusion), kind=kOutput, calls=%fused_computation.9 | convolution fusion | flops 1817247744 | bytes 3538944 | tf_op jit(solution)/shard_map/dot_general | solution.py:97
  272.7 1.5 fusion.27
  274.1 3.2 %multiply_reduce_fusion.1 = (f32[]{:T(128)}, f32[768,768]{1,0:T(8,128)S(1)}) fusion(bf16[768,768]{0,1:T(8,128)(2,1)S(1)} %reshape.54, bf16[2,768,768]{2,1,0:T(8,128)(2,1)} %all-gather.8.cloned.1.call-done), kind=kOutput, calls=%fused_computation.16 | convolution fusion | flops 907149312 | bytes 4718596 | tf_op jit(solution)/shard_map/dot_general | solution.py:87
  278.2 1.0 copy-done.4
  279.2 1.1 convolution_convert_fusion.1
  280.4 3.8 %add_convert_fusion.2 = bf16[768,768]{1,0:T(8,128)(2,1)S(1)} fusion(bf16[768,768]{1,0:T(8,128)(2,1)} %copy-done.4, bf16[768,768]{1,0:T(8,128)(2,1)S(1)} %convolution_convert_fusion.1), kind=kOutput, calls=%fused_computation.13 | convolution fusion | flops 1817247744 | bytes 3538944 | tf_op jit(solution)/shard_map/dot_general | solution.py:97
  284.1 1.5 fusion.28
  (59 shorter events, 7.3 us)
Async XLA Ops:
  8.2 16.1 %copy-start = (f32[768,96]{0,1:T(8,128)S(1)}, f32[768,96]{0,1:T(8,128)}, u32[]{:S(2)}) copy-start(f32[768,96]{0,1:T(8,128)} %param.13) | copy-start | bytes 884740
  9.2 32.8 %copy-start.12 = (f32[12,96]{1,0:T(8,128)S(1)}, f32[12,96]{1,0:T(8,128)}, u32[]{:S(2)}) copy-start(f32[12,96]{1,0:T(8,128)} %param.10) | copy-start | bytes 13828
  9.2 32.7 %all-to-all-start = ((f32[64,12,96]{2,1,0:T(8,128)}), f32[64,12,96]{2,1,0:T(8,128)S(1)}, u32[]{:S(2)}, u32[]{:S(2)}) async-start(f32[64,12,96]{2,1,0:T(8,128)} %reshape.49), calls=%async_computation | async-start | bytes 1048576 | tf_op jit(solution)/shard_map/all_to_all | solution.py:27
  24.2 46.4 %all-gather.4.cloned.1.call-start = ((), (), s32[]{:S(2)}) async-start(), calls=%async_computation.6 | async-start | bytes 1327104 | tf_op jit(solution)/shard_map/all_gather | solution.py:45
  25.0 107.9 %all-gather.6.cloned.1.call-start = ((), (), s32[]{:S(2)}) async-start(), calls=%async_computation.7 | async-start | bytes 5308416 | tf_op jit(solution)/shard_map/all_gather | solution.py:47
  42.0 28.5 %copy-start.9 = (f32[12,96]{1,0:T(8,128)}, f32[12,96]{1,0:T(8,128)S(1)}, u32[]{:S(2)}) copy-start(f32[12,96]{1,0:T(8,128)S(1)} %get-tuple-element.37) | copy-start | bytes 13828
  71.7 190.5 %all-gather.8.cloned.1.call-start = ((), (), s32[]{:S(2)}) async-start(), calls=%async_computation.8 | async-start | bytes 2654208 | tf_op jit(solution)/shard_map/all_gather | solution.py:72
  140.7 1.0 copy-start.5
  143.7 2.1 copy-start.6
  145.8 1.6 copy-start.7
  147.4 2.4 copy-start.1
  149.9 1.8 copy-start.2
  149.9 0.8 copy-start.10
  151.0 13.0 %copy-start.8 = (f32[12,96]{1,0:T(8,128)}, f32[12,96]{1,0:T(8,128)S(1)}, u32[]{:S(2)}) copy-start(f32[12,96]{1,0:T(8,128)S(1)} %fusion.35) | copy-start | bytes 13828
  164.8 30.1 %all-to-all-start.3 = ((f32[64,12,96]{2,1,0:T(8,128)}), f32[64,12,96]{2,1,0:T(8,128)S(1)}, u32[]{:S(2)}, u32[]{:S(2)}) async-start(f32[64,12,96]{2,1,0:T(8,128)} %reshape.52), calls=%async_computation.3 | async-start | bytes 1048576 | tf_op jit(solution)/shard_map/all_to_all | solution.py:27
  196.1 6.0 %copy-start.11 = (f32[12,96]{1,0:T(8,128)S(1)}, f32[12,96]{1,0:T(8,128)}, u32[]{:S(2)}) copy-start(f32[12,96]{1,0:T(8,128)} %param.9) | copy-start | bytes 13828
  196.1 44.9 %all-to-all-start.5 = ((bf16[64,768,12]{1,2,0:T(8,128)(2,1)}), bf16[64,768,12]{1,2,0:T(8,128)(2,1)S(1)}, u32[]{:S(2)}, u32[]{:S(2)}) async-start(bf16[64,768,12]{1,2,0:T(8,128)(2,1)} %broadcast_in_dim.8), calls=%async_computation.5 | async-start | bytes 3145728 | tf_op jit(solution)/shard_map/all_to_all | solution.py:32
  241.7 19.6 %all-to-all-start.4 = ((bf16[64,12,96]{2,1,0:T(8,128)(2,1)}), bf16[64,12,96]{2,1,0:T(8,128)(2,1)S(1)}, u32[]{:S(2)}, u32[]{:S(2)}) async-start(bf16[64,12,96]{2,1,0:T(8,128)(2,1)} %broadcast_in_dim.7), calls=%async_computation.4 | async-start | bytes 524288 | tf_op jit(solution)/shard_map/all_to_all | solution.py:32
  266.7 1.1 copy-start.3
  278.2 1.1 copy-start.4
Sparse Core Ops, SparseCore 0:
  27.7 38.5 all-gather.3
  71.8 60.9 all-gather.5
  151.8 40.1 all-gather.7

commit v7 on v6

--- a/solution.py
+++ b/solution.py
@@ -45,6 +45,7 @@
     right_full = lax.all_gather(right_basis, "mp", axis=1, tiled=True)
     pieces, right_full = lax.optimization_barrier((pieces, right_full))
     both_full = lax.all_gather(pieces, "mp", axis=2, tiled=True)
+    both_full, left_full = lax.optimization_barrier((both_full, left_full))
     grad_full = both_full[0]
     moment_full = both_full[1]
 

time: 293 us -> 239 us (0.82)
  waiting for transfers between devices: 147 us -> 65.3 us
  blocking collectives: 39.6 us -> 88.1 us
  starting transfers between devices: 39.9 us -> 25.4 us
  matrix products: 29 us -> 25.4 us
    all_gather x1, waiting for transfers between devices: 60.9 us -> 9.37 us  [per_device(): both_full = lax.all_gather(pieces, 'mp', axis=2, tiled=True)]
    all_to_all x1 -> x2, blocking collectives: 11.3 us -> 41.2 us  [scatter_sum(): return jnp.sum(lax.all_to_all(chunks, axis, 0, 0, tiled=False), axis=0)]
    all_to_all x1 -> x2, blocking collectives: 28.3 us -> 47 us  [gather_rows(): lax.all_to_all(jnp.broadcast_to(x[None], (count,) + x.shape), axis, 0, 0,...]
    all_to_all x2 -> x1, waiting for transfers between devices: 34.6 us -> 16.9 us  [scatter_sum(): return jnp.sum(lax.all_to_all(chunks, axis, 0, 0, tiled=False), axis=0)]
    all_to_all x2 -> x1, starting transfers between devices: 27.3 us -> 15 us  [scatter_sum(): return jnp.sum(lax.all_to_all(chunks, axis, 0, 0, tiled=False), axis=0)]
    all_to_all x2 -> x1, waiting for transfers between devices: 51.1 us -> 38.9 us  [gather_rows(): lax.all_to_all(jnp.broadcast_to(x[None], (count,) + x.shape), axis, 0, 0,...]
    dot_general x2, matrix products: 7.54 us -> 4.25 us  [per_device(): jnp.dot(poly, whole_part, preferred_element_type=jnp.float32)]
    all_to_all x2 -> x1, starting transfers between devices: 12.3 us -> 10.3 us  [gather_rows(): lax.all_to_all(jnp.broadcast_to(x[None], (count,) + x.shape), axis, 0, 0,...]
  transfers between devices with their start and end apart: 7 -> 5, of which waited for: 5 -> 3; matrix products, arithmetic and copies ran while one was open for 2% -> 3% of each run, Pallas kernels for 0% -> 0%
where the time goes in v7:
time: 239 us; the launch traced here: 238 us
  blocking collectives  88.1 us (37%)
  waiting for transfers between devices  65.3 us (27%)
  starting transfers between devices  25.4 us (11%)
  matrix products  25.4 us (11%)
  between operations  15.5 us (6%)
  local copies, waits for them, and re-layouts  15 us (6%)
  other arithmetic  3.65 us (2%)
    all_to_all x2, blocking collectives, gather_rows(): lax.all_to_all(jnp.broadcast_to(x[None], (count,) + x.shape), axis, 0, 0,...  47 us
    all_to_all x2, blocking collectives, scatter_sum(): return jnp.sum(lax.all_to_all(chunks, axis, 0, 0, tiled=False), axis=0)  41.2 us
    all_to_all x1, waiting for transfers between devices, gather_rows(): lax.all_to_all(jnp.broadcast_to(x[None], (count,) + x.shape), axis, 0, 0,...  38.9 us
    all_to_all x1, waiting for transfers between devices, scatter_sum(): return jnp.sum(lax.all_to_all(chunks, axis, 0, 0, tiled=False), axis=0)  16.9 us
    all_to_all x1, starting transfers between devices, scatter_sum(): return jnp.sum(lax.all_to_all(chunks, axis, 0, 0, tiled=False), axis=0)  15 us
    all_to_all x1, starting transfers between devices, gather_rows(): lax.all_to_all(jnp.broadcast_to(x[None], (count,) + x.shape), axis, 0, 0,...  10.3 us
    all_gather x1, waiting for transfers between devices, per_device(): both_full = lax.all_gather(pieces, 'mp', axis=2, tiled=True)  9.37 us
    slice x1, local copies, waits for them, and re-layouts, per_device(): grad_full = both_full[0]  7.82 us
  transfers between devices with their start and end apart: 5, of which 3 were waited for; matrix products, arithmetic and copies ran while one was open for 3% of the time, Pallas kernels for 0%

profile of v7, /device:TPU:1, one launch (start us, length us, event | category | flops | bytes accessed | tf_op | source)
XLA Modules:
  0.0 238.3 jit_solution(184012834796314135)
XLA Ops:
  7.2 1.0 convert_reduce_fusion
  8.4 0.8 reshape.49
  9.2 15.0 %all-to-all-start = ((f32[64,12,96]{2,1,0:T(8,128)}), f32[64,12,96]{2,1,0:T(8,128)S(1)}, u32[]{:S(2)}, u32[]{:S(2)}) async-start(f32[64,12,96]{2,1,0:T(8,128)} %reshape.49), calls=%async_computation | async-start | bytes 1048576 | tf_op jit(solution)/shard_map/all_to_all | solution.py:27
  24.2 0.7 convert.12
  25.0 16.9 %all-to-all-done = f32[64,12,96]{2,1,0:T(8,128)S(1)} async-done(((f32[64,12,96]{2,1,0:T(8,128)}), f32[64,12,96]{2,1,0:T(8,128)S(1)}, u32[]{:S(2)}, u32[]{:S(2)}) %all-to-all-start) | async-done | bytes 294944 | tf_op jit(solution)/shard_map/all_to_all | solution.py:27
  42.3 28.3 %all_to_all.30 = f32[64,2,12,96]{3,1,2,0:T(2,128)S(1)} all-to-all(f32[64,2,12,96]{3,1,2,0:T(2,128)S(1)} %broadcast_in_dim.6), channel_id=1, replica_groups=mesh['dp'=64,'mp'=8] {'dp'}, dimensions={0} | all-to-all | bytes 1179648 | tf_op jit(solution)/shard_map/all_to_all | solution.py:32
  70.6 1.1 copy.23
  71.7 1.3 broadcast_in_dim.7
  73.0 10.3 %all-to-all-start.2 = ((bf16[64,768,12]{1,2,0:T(8,128)(2,1)}), bf16[64,768,12]{1,2,0:T(8,128)(2,1)S(1)}, u32[]{:S(2)}, u32[]{:S(2)}) async-start(bf16[64,768,12]{1,2,0:T(8,128)(2,1)} %broadcast_in_dim.7), calls=%async_computation.2 | async-start | bytes 3145728 | tf_op jit(solution)/shard_map/all_to_all | solution.py:32
  83.4 38.9 %all-to-all-done.2 = bf16[64,768,12]{1,2,0:T(8,128)(2,1)S(1)} async-done(((bf16[64,768,12]{1,2,0:T(8,128)(2,1)}), bf16[64,768,12]{1,2,0:T(8,128)(2,1)S(1)}, u32[]{:S(2)}, u32[]{:S(2)}) %all-to-all-start.2) | async-done | bytes 1179680 | tf_op jit(solution)/shard_map/all_to_all | solution.py:32
  122.3 1.2 reshape.51
  123.5 9.4 %all-gather.6.cloned.1.call-done = f32[2,768,768]{1,0,2:T(2,128)} async-done(((f32[2,768,96]{1,0,2:T(2,128)}), f32[2,768,768]{1,0,2:T(2,128)}) %all-gather.6.cloned.1.call-update) | async-done | bytes 4718608 | tf_op jit(solution)/shard_map/all_gather | solution.py:47
  132.9 7.8 %fusion.45 = (f32[1,768,768]{1,0,2:T(1,128)S(1)}, f32[1,768,768]{1,0,2:T(1,128)S(1)}) fusion(f32[2,768,768]{1,0,2:T(2,128)} %all-gather.6.cloned.1.call-done), kind=kLoop, calls=%fused_computation.63 | loop fusion | bytes 9437184 | tf_op jit(solution)/shard_map/slice | solution.py:49
  140.7 0.9 constant_dynamic-slice_fusion.1
  141.7 2.0 fusion.4
  143.7 2.0 fusion.6
  145.8 1.6 fusion.24
  147.4 2.4 %fusion.21 = f32[96,768]{1,0:T(8,128)S(1)} fusion(f32[1,768,768]{1,0,2:T(1,128)S(1)} %get-tuple-element.38, f32[1,768,96]{1,0,2:T(1,128)S(1)} %constant_dynamic-slice_fusion, f32[96,768]{1,0:T(8,128)S(1)} %copy-done.6), kind=kOutput, calls=%fused_computation.29 | convolution fusion | flops 679698432 | bytes 3244032 | tf_op jit(solution)/shard_map/dot_general | solution.py:65
  149.9 0.7 pad_maximum_fusion
  152.0 11.2 %all_to_all.31 = f32[8,96,12]{1,2,0:T(8,128)S(1)} all-to-all(f32[8,96,12]{1,2,0:T(8,128)S(1)} %copy.24), channel_id=1, replica_groups=mesh['dp'=64,'mp'=8] {'mp'}, dimensions={0} | all-to-all | bytes 73728 | tf_op jit(solution)/shard_map/all_to_all | solution.py:27
  163.9 30.0 %all_to_all.32 = f32[64,12,96]{2,1,0:T(8,128)S(1)} all-to-all(f32[64,12,96]{2,1,0:T(8,128)S(1)} %reshape.53), channel_id=1, replica_groups=mesh['dp'=64,'mp'=8] {'dp'}, dimensions={0} | all-to-all | bytes 589824 | tf_op jit(solution)/shard_map/all_to_all | solution.py:27
  193.9 0.6 fusion.44
  194.6 18.7 %all_to_all.33 = bf16[64,12,96]{2,1,0:T(8,128)(2,1)S(1)} all-to-all(bf16[64,12,96]{2,1,0:T(8,128)(2,1)S(1)} %broadcast_in_dim.8), channel_id=1, replica_groups=mesh['dp'=64,'mp'=8] {'dp'}, dimensions={0} | all-to-all | bytes 294912 | tf_op jit(solution)/shard_map/all_to_all | solution.py:32
  213.4 0.8 copy.27
  214.2 3.2 %multiply_reduce_fusion = (f32[]{:T(128)}, f32[768,768]{1,0:T(8,128)S(1)}) fusion(bf16[768,768]{0,1:T(8,128)(2,1)S(1)} %copy-done.12, bf16[2,768,768]{2,1,0:T(8,128)(2,1)} %all-gather.8.cloned.1.call-done), kind=kOutput, calls=%fused_computation.12 | convolution fusion | flops 907149312 | bytes 4718596 | tf_op jit(solution)/shard_map/dot_general | solution.py:88
  218.2 1.1 convolution_convert_fusion
  219.4 2.1 add_convert_fusion
  221.5 1.5 fusion.27
  223.0 3.2 %multiply_reduce_fusion.1 = (f32[]{:T(128)}, f32[768,768]{1,0:T(8,128)S(1)}) fusion(bf16[768,768]{0,1:T(8,128)(2,1)S(1)} %copy-done.3, bf16[2,768,768]{2,1,0:T(8,128)(2,1)} %all-gather.8.cloned.1.call-done), kind=kOutput, calls=%fused_computation.16 | convolution fusion | flops 907149312 | bytes 4718596 | tf_op jit(solution)/shard_map/dot_general | solution.py:88
  227.0 1.1 convolution_convert_fusion.1
  228.2 2.1 add_convert_fusion.2
  230.3 1.5 fusion.28
  (57 shorter events, 3.3 us)
Async XLA Ops:
  8.2 16.0 %copy-start = (f32[768,96]{0,1:T(8,128)S(1)}, f32[768,96]{0,1:T(8,128)}, u32[]{:S(2)}) copy-start(f32[768,96]{0,1:T(8,128)} %param.13) | copy-start | bytes 884740
  9.2 32.8 %copy-start.11 = (f32[12,96]{1,0:T(8,128)S(1)}, f32[12,96]{1,0:T(8,128)}, u32[]{:S(2)}) copy-start(f32[12,96]{1,0:T(8,128)} %param.10) | copy-start | bytes 13828
  9.2 32.7 %all-to-all-start = ((f32[64,12,96]{2,1,0:T(8,128)}), f32[64,12,96]{2,1,0:T(8,128)S(1)}, u32[]{:S(2)}, u32[]{:S(2)}) async-start(f32[64,12,96]{2,1,0:T(8,128)} %reshape.49), calls=%async_computation | async-start | bytes 1048576 | tf_op jit(solution)/shard_map/all_to_all | solution.py:27
  24.2 46.4 %all-gather.4.cloned.1.call-start = ((), (), s32[]{:S(2)}) async-start(), calls=%async_computation.6 | async-start | bytes 1327104 | tf_op jit(solution)/shard_map/all_gather | solution.py:45
  25.0 107.9 %all-gather.6.cloned.1.call-start = ((), (), s32[]{:S(2)}) async-start(), calls=%async_computation.7 | async-start | bytes 5308416 | tf_op jit(solution)/shard_map/all_gather | solution.py:47
  42.0 28.5 %copy-start.8 = (f32[12,96]{1,0:T(8,128)}, f32[12,96]{1,0:T(8,128)S(1)}, u32[]{:S(2)}) copy-start(f32[12,96]{1,0:T(8,128)S(1)} %get-tuple-element.41) | copy-start | bytes 13828
  70.5 1.2 copy-start.4
  73.0 49.3 %all-to-all-start.2 = ((bf16[64,768,12]{1,2,0:T(8,128)(2,1)}), bf16[64,768,12]{1,2,0:T(8,128)(2,1)S(1)}, u32[]{:S(2)}, u32[]{:S(2)}) async-start(bf16[64,768,12]{1,2,0:T(8,128)(2,1)} %broadcast_in_dim.7), calls=%async_computation.2 | async-start | bytes 3145728 | tf_op jit(solution)/shard_map/all_to_all | solution.py:32
  83.3 130.9 %all-gather.8.cloned.1.call-start = ((), (), s32[]{:S(2)}) async-start(), calls=%async_computation.8 | async-start | bytes 2654208 | tf_op jit(solution)/shard_map/all_gather | solution.py:73
  143.7 2.1 copy-start.5
  145.8 1.6 copy-start.6
  147.4 2.4 %copy-start.1 = (f32[96,768]{1,0:T(8,128)}, f32[96,768]{1,0:T(8,128)S(1)}, u32[]{:S(2)}) copy-start(f32[96,768]{1,0:T(8,128)S(1)} %fusion.24) | copy-start | bytes 884740
  149.8 1.8 copy-start.2
  149.8 0.8 copy-start.9
  150.9 12.9 %copy-start.7 = (f32[12,96]{1,0:T(8,128)}, f32[12,96]{1,0:T(8,128)S(1)}, u32[]{:S(2)}) copy-start(f32[12,96]{1,0:T(8,128)S(1)} %fusion.35) | copy-start | bytes 13828
  163.8 30.1 %copy-start.10 = (f32[12,96]{1,0:T(8,128)S(1)}, f32[12,96]{1,0:T(8,128)}, u32[]{:S(2)}) copy-start(f32[12,96]{1,0:T(8,128)} %param.9) | copy-start | bytes 13828
  193.8 20.3 %copy-start.12 = (bf16[768,768]{0,1:T(8,128)(2,1)S(1)}, bf16[768,768]{0,1:T(8,128)(2,1)}, u32[]{:S(2)}) copy-start(bf16[768,768]{0,1:T(8,128)(2,1)} %all-gather.4.cloned.1.call-done) | copy-start | bytes 3538948
  221.5 1.5 copy-start.3
Sparse Core Ops, SparseCore 0:
  27.7 38.5 all-gather.3
  71.8 60.9 all-gather.5
  151.7 40.2 all-gather.7

commit v8 on v7

--- a/solution.py
+++ b/solution.py
@@ -12,7 +12,7 @@
 quint_a = 1.875
 quint_b = -1.25
 quint_c = 0.375
-highest = lax.Precision.HIGHEST
+highest = lax.Precision.HIGH
 
 
 def row_gram(row_part, whole_part):

time: 239 us -> 235 us (0.983)
  matrix products: 25.4 us -> 21 us
where the time goes in v8:
time: 235 us; the launch traced here: 234 us
  blocking collectives  88.1 us (37%)
  waiting for transfers between devices  65.1 us (28%)
  starting transfers between devices  25.6 us (11%)
  matrix products  21 us (9%)
  between operations  15.4 us (7%)
  local copies, waits for them, and re-layouts  14.9 us (6%)
  other arithmetic  3.65 us (2%)
    all_to_all x2, blocking collectives, gather_rows(): lax.all_to_all(jnp.broadcast_to(x[None], (count,) + x.shape), axis, 0, 0,...  47 us
    all_to_all x2, blocking collectives, scatter_sum(): return jnp.sum(lax.all_to_all(chunks, axis, 0, 0, tiled=False), axis=0)  41.2 us
    all_to_all x1, waiting for transfers between devices, gather_rows(): lax.all_to_all(jnp.broadcast_to(x[None], (count,) + x.shape), axis, 0, 0,...  38.8 us
    all_to_all x1, waiting for transfers between devices, scatter_sum(): return jnp.sum(lax.all_to_all(chunks, axis, 0, 0, tiled=False), axis=0)  16.9 us
    all_to_all x1, starting transfers between devices, scatter_sum(): return jnp.sum(lax.all_to_all(chunks, axis, 0, 0, tiled=False), axis=0)  15 us
    all_to_all x1, starting transfers between devices, gather_rows(): lax.all_to_all(jnp.broadcast_to(x[None], (count,) + x.shape), axis, 0, 0,...  10.3 us
    all_gather x1, waiting for transfers between devices, per_device(): both_full = lax.all_gather(pieces, 'mp', axis=2, tiled=True)  9.37 us
    slice x1, local copies, waits for them, and re-layouts, per_device(): grad_full = both_full[0]  7.82 us
  transfers between devices with their start and end apart: 5, of which 3 were waited for; matrix products, arithmetic and copies ran while one was open for 3% of the time, Pallas kernels for 0%

profile of v8, /device:TPU:1, one launch (start us, length us, event | category | flops | bytes accessed | tf_op | source)
XLA Modules:
  0.0 233.9 jit_solution(13046074864099732043)
XLA Ops:
  7.2 1.0 convert_reduce_fusion
  8.4 0.8 reshape.49
  9.2 15.0 %all-to-all-start = ((f32[64,12,96]{2,1,0:T(8,128)}), f32[64,12,96]{2,1,0:T(8,128)S(1)}, u32[]{:S(2)}, u32[]{:S(2)}) async-start(f32[64,12,96]{2,1,0:T(8,128)} %reshape.49), calls=%async_computation | async-start | bytes 1048576 | tf_op jit(solution)/shard_map/all_to_all | solution.py:27
  24.2 0.7 convert.12
  25.0 16.9 %all-to-all-done = f32[64,12,96]{2,1,0:T(8,128)S(1)} async-done(((f32[64,12,96]{2,1,0:T(8,128)}), f32[64,12,96]{2,1,0:T(8,128)S(1)}, u32[]{:S(2)}, u32[]{:S(2)}) %all-to-all-start) | async-done | bytes 294944 | tf_op jit(solution)/shard_map/all_to_all | solution.py:27
  42.3 28.3 %all_to_all.30 = f32[64,2,12,96]{3,1,2,0:T(2,128)S(1)} all-to-all(f32[64,2,12,96]{3,1,2,0:T(2,128)S(1)} %broadcast_in_dim.6), channel_id=1, replica_groups=mesh['dp'=64,'mp'=8] {'dp'}, dimensions={0} | all-to-all | bytes 1179648 | tf_op jit(solution)/shard_map/all_to_all | solution.py:32
  70.6 1.1 copy.23
  71.7 1.3 broadcast_in_dim.7
  73.0 10.3 %all-to-all-start.2 = ((bf16[64,768,12]{1,2,0:T(8,128)(2,1)}), bf16[64,768,12]{1,2,0:T(8,128)(2,1)S(1)}, u32[]{:S(2)}, u32[]{:S(2)}) async-start(bf16[64,768,12]{1,2,0:T(8,128)(2,1)} %broadcast_in_dim.7), calls=%async_computation.2 | async-start | bytes 3145728 | tf_op jit(solution)/shard_map/all_to_all | solution.py:32
  83.6 38.8 %all-to-all-done.2 = bf16[64,768,12]{1,2,0:T(8,128)(2,1)S(1)} async-done(((bf16[64,768,12]{1,2,0:T(8,128)(2,1)}), bf16[64,768,12]{1,2,0:T(8,128)(2,1)S(1)}, u32[]{:S(2)}, u32[]{:S(2)}) %all-to-all-start.2) | async-done | bytes 1179680 | tf_op jit(solution)/shard_map/all_to_all | solution.py:32
  122.3 1.2 reshape.51
  123.5 9.4 %all-gather.6.cloned.1.call-done = f32[2,768,768]{1,0,2:T(2,128)} async-done(((f32[2,768,96]{1,0,2:T(2,128)}), f32[2,768,768]{1,0,2:T(2,128)}) %all-gather.6.cloned.1.call-update) | async-done | bytes 4718608 | tf_op jit(solution)/shard_map/all_gather | solution.py:47
  132.9 7.8 %fusion.45 = (f32[1,768,768]{1,0,2:T(1,128)S(1)}, f32[1,768,768]{1,0,2:T(1,128)S(1)}) fusion(f32[2,768,768]{1,0,2:T(2,128)} %all-gather.6.cloned.1.call-done), kind=kLoop, calls=%fused_computation.63 | loop fusion | bytes 9437184 | tf_op jit(solution)/shard_map/slice | solution.py:49
  140.7 0.9 constant_dynamic-slice_fusion.1
  141.7 1.1 fusion.4
  142.7 1.1 fusion.6
  143.8 0.9 fusion.24
  144.8 1.2 fusion.21
  146.1 0.7 pad_maximum_fusion
  147.7 11.2 %all_to_all.31 = f32[8,96,12]{1,2,0:T(8,128)S(1)} all-to-all(f32[8,96,12]{1,2,0:T(8,128)S(1)} %copy.24), channel_id=1, replica_groups=mesh['dp'=64,'mp'=8] {'mp'}, dimensions={0} | all-to-all | bytes 73728 | tf_op jit(solution)/shard_map/all_to_all | solution.py:27
  159.5 30.0 %all_to_all.32 = f32[64,12,96]{2,1,0:T(8,128)S(1)} all-to-all(f32[64,12,96]{2,1,0:T(8,128)S(1)} %reshape.53), channel_id=1, replica_groups=mesh['dp'=64,'mp'=8] {'dp'}, dimensions={0} | all-to-all | bytes 589824 | tf_op jit(solution)/shard_map/all_to_all | solution.py:27
  189.5 0.6 fusion.44
  190.2 18.7 %all_to_all.33 = bf16[64,12,96]{2,1,0:T(8,128)(2,1)S(1)} all-to-all(bf16[64,12,96]{2,1,0:T(8,128)(2,1)S(1)} %broadcast_in_dim.8), channel_id=1, replica_groups=mesh['dp'=64,'mp'=8] {'dp'}, dimensions={0} | all-to-all | bytes 294912 | tf_op jit(solution)/shard_map/all_to_all | solution.py:32
  208.9 0.8 copy.27
  209.8 3.2 %multiply_reduce_fusion = (f32[]{:T(128)}, f32[768,768]{1,0:T(8,128)S(1)}) fusion(bf16[768,768]{0,1:T(8,128)(2,1)S(1)} %copy-done.12, bf16[2,768,768]{2,1,0:T(8,128)(2,1)} %all-gather.8.cloned.1.call-done), kind=kOutput, calls=%fused_computation.12 | convolution fusion | flops 907149312 | bytes 4718596 | tf_op jit(solution)/shard_map/dot_general | solution.py:88
  213.8 1.1 convolution_convert_fusion
  214.9 2.1 add_convert_fusion
  217.1 1.5 fusion.27
  218.6 3.2 %multiply_reduce_fusion.1 = (f32[]{:T(128)}, f32[768,768]{1,0:T(8,128)S(1)}) fusion(bf16[768,768]{0,1:T(8,128)(2,1)S(1)} %copy-done.3, bf16[2,768,768]{2,1,0:T(8,128)(2,1)} %all-gather.8.cloned.1.call-done), kind=kOutput, calls=%fused_computation.16 | convolution fusion | flops 907149312 | bytes 4718596 | tf_op jit(solution)/shard_map/dot_general | solution.py:88
  222.6 1.1 convolution_convert_fusion.1
  223.7 2.1 add_convert_fusion.2
  225.9 1.5 fusion.28
  (57 shorter events, 2.9 us)
Async XLA Ops:
  8.2 16.0 %copy-start = (f32[768,96]{0,1:T(8,128)S(1)}, f32[768,96]{0,1:T(8,128)}, u32[]{:S(2)}) copy-start(f32[768,96]{0,1:T(8,128)} %param.13) | copy-start | bytes 884740
  9.2 32.8 %copy-start.11 = (f32[12,96]{1,0:T(8,128)S(1)}, f32[12,96]{1,0:T(8,128)}, u32[]{:S(2)}) copy-start(f32[12,96]{1,0:T(8,128)} %param.10) | copy-start | bytes 13828
  9.2 32.7 %all-to-all-start = ((f32[64,12,96]{2,1,0:T(8,128)}), f32[64,12,96]{2,1,0:T(8,128)S(1)}, u32[]{:S(2)}, u32[]{:S(2)}) async-start(f32[64,12,96]{2,1,0:T(8,128)} %reshape.49), calls=%async_computation | async-start | bytes 1048576 | tf_op jit(solution)/shard_map/all_to_all | solution.py:27
  24.2 46.4 %all-gather.4.cloned.1.call-start = ((), (), s32[]{:S(2)}) async-start(), calls=%async_computation.6 | async-start | bytes 1327104 | tf_op jit(solution)/shard_map/all_gather | solution.py:45
  25.0 107.9 %all-gather.6.cloned.1.call-start = ((), (), s32[]{:S(2)}) async-start(), calls=%async_computation.7 | async-start | bytes 5308416 | tf_op jit(solution)/shard_map/all_gather | solution.py:47
  42.0 28.5 %copy-start.8 = (f32[12,96]{1,0:T(8,128)}, f32[12,96]{1,0:T(8,128)S(1)}, u32[]{:S(2)}) copy-start(f32[12,96]{1,0:T(8,128)S(1)} %get-tuple-element.41) | copy-start | bytes 13828
  70.5 1.2 copy-start.4
  73.0 49.3 %all-to-all-start.2 = ((bf16[64,768,12]{1,2,0:T(8,128)(2,1)}), bf16[64,768,12]{1,2,0:T(8,128)(2,1)S(1)}, u32[]{:S(2)}, u32[]{:S(2)}) async-start(bf16[64,768,12]{1,2,0:T(8,128)(2,1)} %broadcast_in_dim.7), calls=%async_computation.2 | async-start | bytes 3145728 | tf_op jit(solution)/shard_map/all_to_all | solution.py:32
  83.3 126.4 %all-gather.8.cloned.1.call-start = ((), (), s32[]{:S(2)}) async-start(), calls=%async_computation.8 | async-start | bytes 2654208 | tf_op jit(solution)/shard_map/all_gather | solution.py:73
  142.7 1.1 copy-start.5
  143.8 1.0 copy-start.6
  144.8 1.2 copy-start.1
  146.0 1.4 copy-start.2
  146.0 0.8 copy-start.9
  147.0 12.4 %copy-start.7 = (f32[12,96]{1,0:T(8,128)}, f32[12,96]{1,0:T(8,128)S(1)}, u32[]{:S(2)}) copy-start(f32[12,96]{1,0:T(8,128)S(1)} %fusion.35) | copy-start | bytes 13828
  159.4 30.1 %copy-start.10 = (f32[12,96]{1,0:T(8,128)S(1)}, f32[12,96]{1,0:T(8,128)}, u32[]{:S(2)}) copy-start(f32[12,96]{1,0:T(8,128)} %param.9) | copy-start | bytes 13828
  189.4 20.3 %copy-start.12 = (bf16[768,768]{0,1:T(8,128)(2,1)S(1)}, bf16[768,768]{0,1:T(8,128)(2,1)}, u32[]{:S(2)}) copy-start(bf16[768,768]{0,1:T(8,128)(2,1)} %all-gather.4.cloned.1.call-done) | copy-start | bytes 3538948
  217.1 1.5 copy-start.3
Sparse Core Ops, SparseCore 0:
  27.7 38.5 all-gather.3
  71.8 60.9 all-gather.5
  147.5 40.1 all-gather.7

commit v9 on v8

--- a/solution.py
+++ b/solution.py
@@ -38,23 +38,27 @@
     local_sum = jnp.sum(micro_grads[0], axis=0, dtype=jnp.float32)
     grad_piece = scatter_sum(local_sum, "dp") / (micro_count * dp_count)
     new_moment = beta_one * moment + (1.0 - beta_one) * grad_piece
-    pieces = gather_rows(jnp.stack([grad_piece, new_moment]), "dp")
+    moment_rows = gather_rows(moment, "mp")
+    moment_rows = jnp.moveaxis(moment_rows, 0, 1).reshape(moment.shape[0], -1)
+    moment_right = jnp.dot(moment_rows, right_basis, precision=highest)
+    pieces = gather_rows(jnp.stack([grad_piece, moment_right]), "dp")
     pieces = jnp.swapaxes(pieces, 0, 1).reshape(2, -1, pieces.shape[-1])
     left_cols = gather_rows(left_basis.astype(jnp.bfloat16), "dp")
     left_full = jnp.moveaxis(left_cols, 0, 1).reshape(left_basis.shape[0], -1)
     right_full = lax.all_gather(right_basis, "mp", axis=1, tiled=True)
     pieces, right_full = lax.optimization_barrier((pieces, right_full))
-    both_full = lax.all_gather(pieces, "mp", axis=2, tiled=True)
-    both_full, left_full = lax.optimization_barrier((both_full, left_full))
-    grad_full = both_full[0]
-    moment_full = both_full[1]
+    grad_full = lax.all_gather(pieces[0], "mp", axis=1, tiled=True)
+    grad_full, left_full = lax.optimization_barrier((grad_full, left_full))
+    moment_turned = lax.dot_general(
+        left_basis, pieces[1], (((0,), (0,)), ((), ())), precision=highest
+    )
 
     def rotate(matrix):
         left_part = lax.dot_general(left_basis, matrix, (((0,), (0,)), ((), ())), precision=highest)
         return jnp.dot(left_part, right_basis, precision=highest)
 
     rot_grad = rotate(grad_full)
-    rot_moment = rotate(moment_full)
+    rot_moment = beta_one * moment_turned + (1.0 - beta_one) * rot_grad
     new_second = beta_two * second + (1.0 - beta_two) * rot_grad * rot_grad
     rot_step = rot_moment / (jnp.sqrt(new_second) + adam_eps)
     band_width = right_basis.shape[1]

time: 235 us -> 229 us (0.974)
  blocking collectives: 88.1 us -> 81.9 us
  waiting for transfers between devices: 65.1 us -> 60.8 us
  starting transfers between devices: 25.6 us -> 29.4 us
  matrix products: 21 us -> 24.3 us
  local copies, waits for them, and re-layouts: 14.9 us -> 11.8 us
    all_gather x1, waiting for transfers between devices: 9.37 us -> 0.01 us  [per_device(): grad_full = lax.all_gather(pieces[0], 'mp', axis=1, tiled=True)]
    slice x1 -> x2, local copies, waits for them, and re-layouts: 7.82 us -> 1.58 us  [per_device(): grad_full = lax.all_gather(pieces[0], 'mp', axis=1, tiled=True)]
    all_to_all x2, blocking collectives: 41.2 us -> 34.9 us  [scatter_sum(): return jnp.sum(lax.all_to_all(chunks, axis, 0, 0, tiled=False), axis=0)]
    all_to_all x1 -> x2, waiting for transfers between devices: 38.8 us -> 44.1 us  [gather_rows(): lax.all_to_all(jnp.broadcast_to(x[None], (count,) + x.shape), axis, 0, 0,...]
    unnamed x27 -> x26, local copies, waits for them, and re-layouts: 0.92 us -> 4.74 us
    all_to_all x1 -> x2, starting transfers between devices: 10.3 us -> 13.9 us  [gather_rows(): lax.all_to_all(jnp.broadcast_to(x[None], (count,) + x.shape), axis, 0, 0,...]
    dot_general x2, matrix products: 4.25 us -> 7.51 us  [per_device(): jnp.dot(poly, whole_part, preferred_element_type=jnp.float32)]
  transfers between devices with their start and end apart: 5 -> 6, of which waited for: 3 -> 3; matrix products, arithmetic and copies ran while one was open for 3% -> 4% of each run, Pallas kernels for 0% -> 0%
where the time goes in v9:
time: 229 us; the launch traced here: 228 us
  blocking collectives  81.9 us (36%)
  waiting for transfers between devices  60.8 us (27%)
  starting transfers between devices  29.4 us (13%)
  matrix products  24.3 us (11%)
  between operations  15.4 us (7%)
  local copies, waits for them, and re-layouts  11.8 us (5%)
  other arithmetic  4.25 us (2%)
    all_to_all x2, blocking collectives, gather_rows(): lax.all_to_all(jnp.broadcast_to(x[None], (count,) + x.shape), axis, 0, 0,...  47 us
    all_to_all x2, waiting for transfers between devices, gather_rows(): lax.all_to_all(jnp.broadcast_to(x[None], (count,) + x.shape), axis, 0, 0,...  44.1 us
    all_to_all x2, blocking collectives, scatter_sum(): return jnp.sum(lax.all_to_all(chunks, axis, 0, 0, tiled=False), axis=0)  34.9 us
    all_to_all x1, waiting for transfers between devices, scatter_sum(): return jnp.sum(lax.all_to_all(chunks, axis, 0, 0, tiled=False), axis=0)  16.6 us
    all_to_all x1, starting transfers between devices, scatter_sum(): return jnp.sum(lax.all_to_all(chunks, axis, 0, 0, tiled=False), axis=0)  15.4 us
    all_to_all x2, starting transfers between devices, gather_rows(): lax.all_to_all(jnp.broadcast_to(x[None], (count,) + x.shape), axis, 0, 0,...  13.9 us
    dot_general x2, matrix products, per_device(): jnp.dot(poly, whole_part, preferred_element_type=jnp.float32)  7.51 us
    dot_general x2, matrix products, per_device(): jnp.dot(stat_part, basis_part.astype(jnp.bfloat16), preferred_element_typ...  7.09 us
  transfers between devices with their start and end apart: 6, of which 3 were waited for; matrix products, arithmetic and copies ran while one was open for 4% of the time, Pallas kernels for 0%

profile of v9, /device:TPU:1, one launch (start us, length us, event | category | flops | bytes accessed | tf_op | source)
XLA Modules:
  0.0 227.9 jit_solution(16702691302008084459)
XLA Ops:
  7.2 1.3 broadcast_in_dim.8
  8.5 7.7 %all-to-all-start.1 = ((f32[8,12,96]{2,1,0:T(8,128)}), f32[8,12,96]{2,1,0:T(8,128)S(1)}, u32[]{:S(2)}, u32[]{:S(2)}) async-start(f32[8,12,96]{2,1,0:T(8,128)} %broadcast_in_dim.8), calls=%async_computation.1 | async-start | bytes 131072 | tf_op jit(solution)/shard_map/all_to_all | solution.py:32
  16.1 1.0 convert_reduce_fusion
  17.4 0.8 reshape.51
  18.2 5.2 %all-to-all-done.1 = f32[8,12,96]{2,1,0:T(8,128)S(1)} async-done(((f32[8,12,96]{2,1,0:T(8,128)}), f32[8,12,96]{2,1,0:T(8,128)S(1)}, u32[]{:S(2)}, u32[]{:S(2)}) %all-to-all-start.1) | async-done | bytes 36896 | tf_op jit(solution)/shard_map/all_to_all | solution.py:32
  23.4 15.4 %all-to-all-start = ((f32[64,12,96]{2,1,0:T(8,128)}), f32[64,12,96]{2,1,0:T(8,128)S(1)}, u32[]{:S(2)}, u32[]{:S(2)}) async-start(f32[64,12,96]{2,1,0:T(8,128)} %reshape.51), calls=%async_computation | async-start | bytes 1048576 | tf_op jit(solution)/shard_map/all_to_all | solution.py:27
  39.9 16.6 %all-to-all-done = f32[64,12,96]{2,1,0:T(8,128)S(1)} async-done(((f32[64,12,96]{2,1,0:T(8,128)}), f32[64,12,96]{2,1,0:T(8,128)S(1)}, u32[]{:S(2)}, u32[]{:S(2)}) %all-to-all-start) | async-done | bytes 294944 | tf_op jit(solution)/shard_map/all_to_all | solution.py:27
  57.5 28.3 %all_to_all.35 = f32[64,2,12,96]{3,1,2,0:T(2,128)S(1)} all-to-all(f32[64,2,12,96]{3,1,2,0:T(2,128)S(1)} %broadcast_in_dim.9), channel_id=1, replica_groups=mesh['dp'=64,'mp'=8] {'dp'}, dimensions={0} | all-to-all | bytes 1179648 | tf_op jit(solution)/shard_map/all_to_all | solution.py:32
  86.4 1.0 copy.24
  87.4 1.2 broadcast_in_dim.10
  88.6 6.2 %all-to-all-start.3 = ((bf16[64,768,12]{1,2,0:T(8,128)(2,1)}), bf16[64,768,12]{1,2,0:T(8,128)(2,1)S(1)}, u32[]{:S(2)}, u32[]{:S(2)}) async-start(bf16[64,768,12]{1,2,0:T(8,128)(2,1)} %broadcast_in_dim.10), calls=%async_computation.3 | async-start | bytes 3145728 | tf_op jit(solution)/shard_map/all_to_all | solution.py:32
  94.9 38.9 %all-to-all-done.3 = bf16[64,768,12]{1,2,0:T(8,128)(2,1)S(1)} async-done(((bf16[64,768,12]{1,2,0:T(8,128)(2,1)}), bf16[64,768,12]{1,2,0:T(8,128)(2,1)S(1)}, u32[]{:S(2)}, u32[]{:S(2)}) %all-to-all-start.3) | async-done | bytes 1179680 | tf_op jit(solution)/shard_map/all_to_all | solution.py:32
  133.9 1.2 reshape.54
  135.0 1.8 copy.32
  136.9 1.1 fusion.29
  137.9 1.3 fusion.3
  139.3 1.1 fusion.4
  140.4 0.7 pad_maximum_fusion
  142.0 9.7 %all_to_all.36 = f32[8,96,12]{1,2,0:T(8,128)S(1)} all-to-all(f32[8,96,12]{1,2,0:T(8,128)S(1)} %copy.25), channel_id=1, replica_groups=mesh['dp'=64,'mp'=8] {'mp'}, dimensions={0} | all-to-all | bytes 73728 | tf_op jit(solution)/shard_map/all_to_all | solution.py:27
  152.2 25.3 %all_to_all.37 = f32[64,12,96]{2,1,0:T(8,128)S(1)} all-to-all(f32[64,12,96]{2,1,0:T(8,128)S(1)} %reshape.56), channel_id=1, replica_groups=mesh['dp'=64,'mp'=8] {'dp'}, dimensions={0} | all-to-all | bytes 589824 | tf_op jit(solution)/shard_map/all_to_all | solution.py:27
  178.2 18.7 %all_to_all.38 = bf16[64,12,96]{2,1,0:T(8,128)(2,1)S(1)} all-to-all(bf16[64,12,96]{2,1,0:T(8,128)(2,1)S(1)} %broadcast_in_dim.11), channel_id=1, replica_groups=mesh['dp'=64,'mp'=8] {'dp'}, dimensions={0} | all-to-all | bytes 294912 | tf_op jit(solution)/shard_map/all_to_all | solution.py:32
  197.0 0.8 copy.28
  197.8 3.5 %multiply_reduce_fusion = (f32[]{:T(128)}, f32[768,768]{1,0:T(8,128)S(1)}) fusion(bf16[768,768]{0,1:T(8,128)(2,1)} %all-gather.5.cloned.1.call-done, bf16[2,768,768]{2,1,0:T(8,128)(2,1)} %all-gather.7.cloned.1.call-done), kind=kOutput, calls=%fused_computation.4 | convolution fusion | flops 907149312 | bytes 4718596 | tf_op jit(solution)/shard_map/dot_general | solution.py:92
  202.2 1.0 copy-done.3
  203.3 1.1 convolution_convert_fusion
  204.4 3.8 %add_convert_fusion = bf16[768,768]{1,0:T(8,128)(2,1)S(1)} fusion(bf16[768,768]{1,0:T(8,128)(2,1)} %copy-done.3, bf16[768,768]{1,0:T(8,128)(2,1)S(1)} %convolution_convert_fusion), kind=kOutput, calls=%fused_computation.1 | convolution fusion | flops 1817247744 | bytes 3538944 | tf_op jit(solution)/shard_map/dot_general | solution.py:102
  208.1 1.5 fusion.5
  209.6 3.5 %multiply_reduce_fusion.1 = (f32[]{:T(128)}, f32[768,768]{1,0:T(8,128)S(1)}) fusion(bf16[768,768]{0,1:T(8,128)(2,1)} %reshape.54, bf16[2,768,768]{2,1,0:T(8,128)(2,1)} %all-gather.7.cloned.1.call-done), kind=kOutput, calls=%fused_computation.8 | convolution fusion | flops 907149312 | bytes 4718596 | tf_op jit(solution)/shard_map/dot_general | solution.py:92
  214.0 1.0 copy-done.4
  215.1 1.1 convolution_convert_fusion.1
  216.2 3.8 %add_convert_fusion.2 = bf16[768,768]{1,0:T(8,128)(2,1)S(1)} fusion(bf16[768,768]{1,0:T(8,128)(2,1)} %copy-done.4, bf16[768,768]{1,0:T(8,128)(2,1)S(1)} %convolution_convert_fusion.1), kind=kOutput, calls=%fused_computation.5 | convolution fusion | flops 1817247744 | bytes 3538944 | tf_op jit(solution)/shard_map/dot_general | solution.py:102
  219.9 1.5 fusion.6
  (59 shorter events, 5.4 us)
Async XLA Ops:
  8.5 14.9 %all-to-all-start.1 = ((f32[8,12,96]{2,1,0:T(8,128)}), f32[8,12,96]{2,1,0:T(8,128)S(1)}, u32[]{:S(2)}, u32[]{:S(2)}) async-start(f32[8,12,96]{2,1,0:T(8,128)} %broadcast_in_dim.8), calls=%async_computation.1 | async-start | bytes 131072 | tf_op jit(solution)/shard_map/all_to_all | solution.py:32
  17.2 21.7 %copy-start = (f32[768,96]{0,1:T(8,128)S(1)}, f32[768,96]{0,1:T(8,128)}, u32[]{:S(2)}) copy-start(f32[768,96]{0,1:T(8,128)} %param.13) | copy-start | bytes 884740
  18.2 38.4 %copy-start.9 = (f32[12,96]{1,0:T(8,128)S(1)}, f32[12,96]{1,0:T(8,128)}, u32[]{:S(2)}) copy-start(f32[12,96]{1,0:T(8,128)} %param.10) | copy-start | bytes 13828
  23.4 33.2 %all-to-all-start = ((f32[64,12,96]{2,1,0:T(8,128)}), f32[64,12,96]{2,1,0:T(8,128)S(1)}, u32[]{:S(2)}, u32[]{:S(2)}) async-start(f32[64,12,96]{2,1,0:T(8,128)} %reshape.51), calls=%async_computation | async-start | bytes 1048576 | tf_op jit(solution)/shard_map/all_to_all | solution.py:27
  38.8 46.9 %all-gather.5.cloned.1.call-start = ((), (), s32[]{:S(2)}) async-start(), calls=%async_computation.7 | async-start | bytes 1327104 | tf_op jit(solution)/shard_map/all_gather | solution.py:48
  39.6 95.4 %all-gather.9.cloned.1.call-start = ((), (), s32[]{:S(2)}) async-start(), calls=%async_computation.9 | async-start | bytes 2654208 | tf_op jit(solution)/shard_map/all_gather | solution.py:50
  85.7 1.6 copy-start.5
  88.6 45.2 %all-to-all-start.3 = ((bf16[64,768,12]{1,2,0:T(8,128)(2,1)}), bf16[64,768,12]{1,2,0:T(8,128)(2,1)S(1)}, u32[]{:S(2)}, u32[]{:S(2)}) async-start(bf16[64,768,12]{1,2,0:T(8,128)(2,1)} %broadcast_in_dim.10), calls=%async_computation.3 | async-start | bytes 3145728 | tf_op jit(solution)/shard_map/all_to_all | solution.py:32
  94.9 102.9 %all-gather.7.cloned.1.call-start = ((), (), s32[]{:S(2)}) async-start(), calls=%async_computation.8 | async-start | bytes 2654208 | tf_op jit(solution)/shard_map/all_gather | solution.py:77
  136.8 1.1 copy-start.6
  137.9 1.3 copy-start.7
  139.2 1.1 copy-start.1
  140.3 1.3 copy-start.2
  140.3 0.8 copy-start.10
  141.3 10.8 %copy-start.8 = (f32[12,96]{1,0:T(8,128)}, f32[12,96]{1,0:T(8,128)S(1)}, u32[]{:S(2)}) copy-start(f32[12,96]{1,0:T(8,128)S(1)} %get-tuple-element.42) | copy-start | bytes 13828
  152.2 25.4 %copy-start.11 = (f32[12,96]{1,0:T(8,128)S(1)}, f32[12,96]{1,0:T(8,128)}, u32[]{:S(2)}) copy-start(f32[12,96]{1,0:T(8,128)} %param.9) | copy-start | bytes 13828
  202.2 1.0 copy-start.3
  214.0 1.0 copy-start.4
Sparse Core Ops, SparseCore 0:
  42.3 32.8 all-gather.4
  87.5 34.5 all-gather.8
  141.8 33.8 all-gather.6

commit v10 on v9

--- a/solution.py
+++ b/solution.py
@@ -38,8 +38,7 @@
     local_sum = jnp.sum(micro_grads[0], axis=0, dtype=jnp.float32)
     grad_piece = scatter_sum(local_sum, "dp") / (micro_count * dp_count)
     new_moment = beta_one * moment + (1.0 - beta_one) * grad_piece
-    moment_rows = gather_rows(moment, "mp")
-    moment_rows = jnp.moveaxis(moment_rows, 0, 1).reshape(moment.shape[0], -1)
+    moment_rows = lax.all_gather(moment, "mp", axis=1, tiled=True)
     moment_right = jnp.dot(moment_rows, right_basis, precision=highest)
     pieces = gather_rows(jnp.stack([grad_piece, moment_right]), "dp")
     pieces = jnp.swapaxes(pieces, 0, 1).reshape(2, -1, pieces.shape[-1])

time: 229 us -> 231 us (level)
  blocking collectives: 81.9 us -> 115 us
  waiting for transfers between devices: 60.8 us -> 39 us
  starting transfers between devices: 29.4 us -> 21.2 us
    all_gather x0 -> x1, blocking collectives: none -> 21.2 us  [per_device(): moment_rows = lax.all_gather(moment, 'mp', axis=1, tiled=True)]
    all_to_all x1, waiting for transfers between devices: 16.6 us -> 0.03 us  [scatter_sum(): return jnp.sum(lax.all_to_all(chunks, axis, 0, 0, tiled=False), axis=0)]
    all_to_all x2, blocking collectives: 47 us -> 56.5 us  [gather_rows(): lax.all_to_all(jnp.broadcast_to(x[None], (count,) + x.shape), axis, 0, 0,...]
    all_to_all x2 -> x1, starting transfers between devices: 13.9 us -> 6.24 us  [gather_rows(): lax.all_to_all(jnp.broadcast_to(x[None], (count,) + x.shape), axis, 0, 0,...]
    all_to_all x2 -> x1, waiting for transfers between devices: 44.1 us -> 38.9 us  [gather_rows(): lax.all_to_all(jnp.broadcast_to(x[None], (count,) + x.shape), axis, 0, 0,...]
    all_to_all x2, blocking collectives: 34.9 us -> 37.8 us  [scatter_sum(): return jnp.sum(lax.all_to_all(chunks, axis, 0, 0, tiled=False), axis=0)]
    unnamed x26 -> x27, local copies, waits for them, and re-layouts: 4.74 us -> 4.84 us
  transfers between devices with their start and end apart: 6 -> 5, of which waited for: 3 -> 1; matrix products, arithmetic and copies ran while one was open for 4% -> 3% of each run, Pallas kernels for 0% -> 0%
where the time goes in v10:
time: 231 us; the launch traced here: 230 us
  blocking collectives  115 us (50%)
  waiting for transfers between devices  39 us (17%)
  matrix products  24.3 us (11%)
  starting transfers between devices  21.2 us (9%)
  between operations  15.5 us (7%)
  local copies, waits for them, and re-layouts  10.5 us (5%)
  other arithmetic  4.28 us (2%)
    all_to_all x2, blocking collectives, gather_rows(): lax.all_to_all(jnp.broadcast_to(x[None], (count,) + x.shape), axis, 0, 0,...  56.5 us
    all_to_all x1, waiting for transfers between devices, gather_rows(): lax.all_to_all(jnp.broadcast_to(x[None], (count,) + x.shape), axis, 0, 0,...  38.9 us
    all_to_all x2, blocking collectives, scatter_sum(): return jnp.sum(lax.all_to_all(chunks, axis, 0, 0, tiled=False), axis=0)  37.8 us
    all_gather x1, blocking collectives, per_device(): moment_rows = lax.all_gather(moment, 'mp', axis=1, tiled=True)  21.2 us
    all_to_all x1, starting transfers between devices, scatter_sum(): return jnp.sum(lax.all_to_all(chunks, axis, 0, 0, tiled=False), axis=0)  14.8 us
    dot_general x2, matrix products, per_device(): jnp.dot(poly, whole_part, preferred_element_type=jnp.float32)  7.52 us
    dot_general x2, matrix products, per_device(): jnp.dot(stat_part, basis_part.astype(jnp.bfloat16), preferred_element_typ...  7.09 us
    all_to_all x1, starting transfers between devices, gather_rows(): lax.all_to_all(jnp.broadcast_to(x[None], (count,) + x.shape), axis, 0, 0,...  6.24 us
  transfers between devices with their start and end apart: 5, of which 1 were waited for; matrix products, arithmetic and copies ran while one was open for 3% of the time, Pallas kernels for 0%

profile of v10, /device:TPU:1, one launch (start us, length us, event | category | flops | bytes accessed | tf_op | source)
XLA Modules:
  0.0 230.2 jit_solution(916054371275139337)
XLA Ops:
  7.2 1.0 convert_reduce_fusion
  8.4 0.8 reshape.47
  9.2 14.8 %all-to-all-start = ((f32[64,12,96]{2,1,0:T(8,128)}), f32[64,12,96]{2,1,0:T(8,128)S(1)}, u32[]{:S(2)}, u32[]{:S(2)}) async-start(f32[64,12,96]{2,1,0:T(8,128)} %reshape.47), calls=%async_computation | async-start | bytes 1048576 | tf_op jit(solution)/shard_map/all_to_all | solution.py:27
  24.1 0.7 convert.12
  24.9 21.2 %all-gather.1 = f32[8,96,12]{1,2,0:T(8,128)S(1)} all-gather(f32[1,96,12]{1,2,0:T(8,128)S(1)} %bitcast.81), channel_id=1, replica_groups=mesh['dp'=64,'mp'=8] {'mp'}, dimensions={0}, use_global_device_ids=true | all-gather | bytes 41472 | tf_op jit(solution)/shard_map/all_gather | solution.py:41
  46.5 0.6 multiply_add_fusion
  47.4 37.8 %all_to_all.30 = f32[64,2,12,96]{3,1,2,0:T(2,128)S(1)} all-to-all(f32[64,2,12,96]{3,1,2,0:T(2,128)S(1)} %broadcast_in_dim.6), channel_id=1, replica_groups=mesh['dp'=64,'mp'=8] {'dp'}, dimensions={0} | all-to-all | bytes 1179648 | tf_op jit(solution)/shard_map/all_to_all | solution.py:32
  85.2 0.6 fusion.28
  85.8 1.0 copy.25
  86.8 1.2 broadcast_in_dim.7
  88.0 6.2 %all-to-all-start.2 = ((bf16[64,768,12]{1,2,0:T(8,128)(2,1)}), bf16[64,768,12]{1,2,0:T(8,128)(2,1)S(1)}, u32[]{:S(2)}, u32[]{:S(2)}) async-start(bf16[64,768,12]{1,2,0:T(8,128)(2,1)} %broadcast_in_dim.7), calls=%async_computation.2 | async-start | bytes 3145728 | tf_op jit(solution)/shard_map/all_to_all | solution.py:32
  94.3 38.9 %all-to-all-done.2 = bf16[64,768,12]{1,2,0:T(8,128)(2,1)S(1)} async-done(((bf16[64,768,12]{1,2,0:T(8,128)(2,1)}), bf16[64,768,12]{1,2,0:T(8,128)(2,1)S(1)}, u32[]{:S(2)}, u32[]{:S(2)}) %all-to-all-start.2) | async-done | bytes 1179680 | tf_op jit(solution)/shard_map/all_to_all | solution.py:32
  133.3 1.2 reshape.49
  134.4 1.8 copy.33
  136.3 1.1 fusion.29
  137.3 1.3 fusion.3
  138.7 1.1 fusion.4
  139.8 0.7 pad_maximum_fusion
  141.4 12.4 %all_to_all.31 = f32[8,96,12]{1,2,0:T(8,128)S(1)} all-to-all(f32[8,96,12]{1,2,0:T(8,128)S(1)} %copy.26), channel_id=1, replica_groups=mesh['dp'=64,'mp'=8] {'mp'}, dimensions={0} | all-to-all | bytes 73728 | tf_op jit(solution)/shard_map/all_to_all | solution.py:27
  154.3 25.4 %all_to_all.32 = f32[64,12,96]{2,1,0:T(8,128)S(1)} all-to-all(f32[64,12,96]{2,1,0:T(8,128)S(1)} %reshape.51), channel_id=1, replica_groups=mesh['dp'=64,'mp'=8] {'dp'}, dimensions={0} | all-to-all | bytes 589824 | tf_op jit(solution)/shard_map/all_to_all | solution.py:27
  180.5 18.7 %all_to_all.33 = bf16[64,12,96]{2,1,0:T(8,128)(2,1)S(1)} all-to-all(bf16[64,12,96]{2,1,0:T(8,128)(2,1)S(1)} %broadcast_in_dim.8), channel_id=1, replica_groups=mesh['dp'=64,'mp'=8] {'dp'}, dimensions={0} | all-to-all | bytes 294912 | tf_op jit(solution)/shard_map/all_to_all | solution.py:32
  199.2 0.8 copy.29
  200.1 3.5 %multiply_reduce_fusion = (f32[]{:T(128)}, f32[768,768]{1,0:T(8,128)S(1)}) fusion(bf16[768,768]{0,1:T(8,128)(2,1)} %all-gather.6.cloned.1.call-done, bf16[2,768,768]{2,1,0:T(8,128)(2,1)} %all-gather.8.cloned.1.call-done), kind=kOutput, calls=%fused_computation.4 | convolution fusion | flops 907149312 | bytes 4718596 | tf_op jit(solution)/shard_map/dot_general | solution.py:91
  204.5 1.0 copy-done.3
  205.5 1.1 convolution_convert_fusion
  206.6 3.8 %add_convert_fusion = bf16[768,768]{1,0:T(8,128)(2,1)S(1)} fusion(bf16[768,768]{1,0:T(8,128)(2,1)} %copy-done.3, bf16[768,768]{1,0:T(8,128)(2,1)S(1)} %convolution_convert_fusion), kind=kOutput, calls=%fused_computation.1 | convolution fusion | flops 1817247744 | bytes 3538944 | tf_op jit(solution)/shard_map/dot_general | solution.py:101
  210.4 1.5 fusion.5
  211.8 3.5 %multiply_reduce_fusion.1 = (f32[]{:T(128)}, f32[768,768]{1,0:T(8,128)S(1)}) fusion(bf16[768,768]{0,1:T(8,128)(2,1)} %reshape.49, bf16[2,768,768]{2,1,0:T(8,128)(2,1)} %all-gather.8.cloned.1.call-done), kind=kOutput, calls=%fused_computation.8 | convolution fusion | flops 907149312 | bytes 4718596 | tf_op jit(solution)/shard_map/dot_general | solution.py:91
  216.3 1.0 copy-done.4
  217.3 1.1 convolution_convert_fusion.1
  218.4 3.8 %add_convert_fusion.2 = bf16[768,768]{1,0:T(8,128)(2,1)S(1)} fusion(bf16[768,768]{1,0:T(8,128)(2,1)} %copy-done.4, bf16[768,768]{1,0:T(8,128)(2,1)S(1)} %convolution_convert_fusion.1), kind=kOutput, calls=%fused_computation.5 | convolution fusion | flops 1817247744 | bytes 3538944 | tf_op jit(solution)/shard_map/dot_general | solution.py:101
  222.2 1.5 fusion.6
  (57 shorter events, 3.5 us)
Async XLA Ops:
  8.2 15.9 %copy-start = (f32[768,96]{0,1:T(8,128)S(1)}, f32[768,96]{0,1:T(8,128)}, u32[]{:S(2)}) copy-start(f32[768,96]{0,1:T(8,128)} %param.13) | copy-start | bytes 884740
  8.4 16.5 %copy-start.9 = (f32[12,96]{1,0:T(8,128)S(1)}, f32[12,96]{1,0:T(8,128)}, u32[]{:S(2)}) copy-start(f32[12,96]{1,0:T(8,128)} %param.10) | copy-start | bytes 13828
  9.2 37.2 %all-to-all-start = ((f32[64,12,96]{2,1,0:T(8,128)}), f32[64,12,96]{2,1,0:T(8,128)S(1)}, u32[]{:S(2)}, u32[]{:S(2)}) async-start(f32[64,12,96]{2,1,0:T(8,128)} %reshape.47), calls=%async_computation | async-start | bytes 1048576 | tf_op jit(solution)/shard_map/all_to_all | solution.py:27
  24.1 61.1 %all-gather.6.cloned.1.call-start = ((), (), s32[]{:S(2)}) async-start(), calls=%async_computation.6 | async-start | bytes 1327104 | tf_op jit(solution)/shard_map/all_gather | solution.py:47
  24.8 109.6 %all-gather.10.cloned.1.call-start = ((), (), s32[]{:S(2)}) async-start(), calls=%async_computation.8 | async-start | bytes 2654208 | tf_op jit(solution)/shard_map/all_gather | solution.py:49
  85.1 1.6 copy-start.5
  88.0 45.2 %all-to-all-start.2 = ((bf16[64,768,12]{1,2,0:T(8,128)(2,1)}), bf16[64,768,12]{1,2,0:T(8,128)(2,1)S(1)}, u32[]{:S(2)}, u32[]{:S(2)}) async-start(bf16[64,768,12]{1,2,0:T(8,128)(2,1)} %broadcast_in_dim.7), calls=%async_computation.2 | async-start | bytes 3145728 | tf_op jit(solution)/shard_map/all_to_all | solution.py:32
  94.3 105.8 %all-gather.8.cloned.1.call-start = ((), (), s32[]{:S(2)}) async-start(), calls=%async_computation.7 | async-start | bytes 2654208 | tf_op jit(solution)/shard_map/all_gather | solution.py:76
  136.2 1.1 copy-start.6
  137.3 1.3 copy-start.7
  138.6 1.1 copy-start.1
  139.7 1.3 copy-start.2
  139.7 0.8 copy-start.10
  140.7 13.5 %copy-start.8 = (f32[12,96]{1,0:T(8,128)}, f32[12,96]{1,0:T(8,128)S(1)}, u32[]{:S(2)}) copy-start(f32[12,96]{1,0:T(8,128)S(1)} %get-tuple-element.42) | copy-start | bytes 13828
  154.3 25.6 %copy-start.11 = (f32[12,96]{1,0:T(8,128)S(1)}, f32[12,96]{1,0:T(8,128)}, u32[]{:S(2)}) copy-start(f32[12,96]{1,0:T(8,128)} %param.9) | copy-start | bytes 13828
  204.5 1.0 copy-start.3
  216.3 1.0 copy-start.4
Sparse Core Ops, SparseCore 0:
  27.6 38.0 all-gather.5
  86.9 36.4 all-gather.9
  141.2 36.6 all-gather.7

commit v11 on v9

--- a/solution.py
+++ b/solution.py
@@ -32,6 +32,21 @@
     return lax.all_to_all(jnp.broadcast_to(x[None], (count,) + x.shape), axis, 0, 0, tiled=False)
 
 
+def doubling_gather(x, axis):
+    count = lax.axis_size(axis)
+    index = lax.axis_index(axis)
+    parts = x[None]
+    step = 1
+    while step < count:
+        other = lax.ppermute(parts, axis, [(i, i ^ step) for i in range(count)])
+        lower = (index // step) % 2 == 0
+        parts = jnp.concatenate(
+            [jnp.where(lower, parts, other), jnp.where(lower, other, parts)], axis=0
+        )
+        step *= 2
+    return parts
+
+
 def per_device(micro_grads, master, moment, second, left_basis, right_basis, left_stat, right_stat):
     dp_count = lax.axis_size("dp")
     micro_count = micro_grads.shape[1]
@@ -43,12 +58,11 @@
     moment_right = jnp.dot(moment_rows, right_basis, precision=highest)
     pieces = gather_rows(jnp.stack([grad_piece, moment_right]), "dp")
     pieces = jnp.swapaxes(pieces, 0, 1).reshape(2, -1, pieces.shape[-1])
-    left_cols = gather_rows(left_basis.astype(jnp.bfloat16), "dp")
+    left_cols = doubling_gather(left_basis.astype(jnp.bfloat16), "dp")
     left_full = jnp.moveaxis(left_cols, 0, 1).reshape(left_basis.shape[0], -1)
     right_full = lax.all_gather(right_basis, "mp", axis=1, tiled=True)
     pieces, right_full = lax.optimization_barrier((pieces, right_full))
     grad_full = lax.all_gather(pieces[0], "mp", axis=1, tiled=True)
-    grad_full, left_full = lax.optimization_barrier((grad_full, left_full))
     moment_turned = lax.dot_general(
         left_basis, pieces[1], (((0,), (0,)), ((), ())), precision=highest
     )

time: 229 us -> 279 us (1.22)
  starting transfers between devices: 29.4 us -> 101 us
  blocking collectives: 81.9 us -> 28.3 us
  waiting for transfers between devices: 60.8 us -> 89.4 us
    all_to_all x2 -> x0, blocking collectives: 34.9 us -> none  [scatter_sum(): return jnp.sum(lax.all_to_all(chunks, axis, 0, 0, tiled=False), axis=0)]
    all_gather x1, waiting for transfers between devices: 0.01 us -> 34.7 us  [per_device(): grad_full = lax.all_gather(pieces[0], 'mp', axis=1, tiled=True)]
    ppermute x0 -> x6, starting transfers between devices: none -> 28.4 us  [doubling_gather(): other = lax.ppermute(parts, axis, [(i, i ^ step) for i in range(count)])]
    all_to_all x2, waiting for transfers between devices: 44.1 us -> 17.4 us  [gather_rows(): lax.all_to_all(jnp.broadcast_to(x[None], (count,) + x.shape), axis, 0, 0,...]
    all_to_all x2, starting transfers between devices: 13.9 us -> 38.3 us  [gather_rows(): lax.all_to_all(jnp.broadcast_to(x[None], (count,) + x.shape), axis, 0, 0,...]
    all_to_all x1 -> x3, starting transfers between devices: 15.4 us -> 34.5 us  [scatter_sum(): return jnp.sum(lax.all_to_all(chunks, axis, 0, 0, tiled=False), axis=0)]
    all_to_all x2 -> x1, blocking collectives: 47 us -> 28.3 us  [gather_rows(): lax.all_to_all(jnp.broadcast_to(x[None], (count,) + x.shape), axis, 0, 0,...]
    all_to_all x1 -> x3, waiting for transfers between devices: 16.6 us -> 29.1 us  [scatter_sum(): return jnp.sum(lax.all_to_all(chunks, axis, 0, 0, tiled=False), axis=0)]
  transfers between devices with their start and end apart: 6 -> 14, of which waited for: 3 -> 10; matrix products, arithmetic and copies ran while one was open for 4% -> 4% of each run, Pallas kernels for 0% -> 0%
where the time goes in v11:
time: 279 us; the launch traced here: 278 us
  starting transfers between devices  101 us (36%)
  waiting for transfers between devices  89.4 us (32%)
  blocking collectives  28.3 us (10%)
  matrix products  25.5 us (9%)
  between operations  15.7 us (6%)
  local copies, waits for them, and re-layouts  11.9 us (4%)
  other arithmetic  6.21 us (2%)
    all_to_all x2, starting transfers between devices, gather_rows(): lax.all_to_all(jnp.broadcast_to(x[None], (count,) + x.shape), axis, 0, 0,...  38.3 us
    all_gather x1, waiting for transfers between devices, per_device(): grad_full = lax.all_gather(pieces[0], 'mp', axis=1, tiled=True)  34.7 us
    all_to_all x3, starting transfers between devices, scatter_sum(): return jnp.sum(lax.all_to_all(chunks, axis, 0, 0, tiled=False), axis=0)  34.5 us
    all_to_all x3, waiting for transfers between devices, scatter_sum(): return jnp.sum(lax.all_to_all(chunks, axis, 0, 0, tiled=False), axis=0)  29.1 us
    ppermute x6, starting transfers between devices, doubling_gather(): other = lax.ppermute(parts, axis, [(i, i ^ step) for i in range(count)])  28.4 us
    all_to_all x1, blocking collectives, gather_rows(): lax.all_to_all(jnp.broadcast_to(x[None], (count,) + x.shape), axis, 0, 0,...  28.3 us
    all_to_all x2, waiting for transfers between devices, gather_rows(): lax.all_to_all(jnp.broadcast_to(x[None], (count,) + x.shape), axis, 0, 0,...  17.4 us
    ppermute x6, waiting for transfers between devices, doubling_gather(): other = lax.ppermute(parts, axis, [(i, i ^ step) for i in range(count)])  8.23 us
  transfers between devices with their start and end apart: 14, of which 10 were waited for; matrix products, arithmetic and copies ran while one was open for 4% of the time, Pallas kernels for 0%

profile of v11, /device:TPU:1, one launch (start us, length us, event | category | flops | bytes accessed | tf_op | source)
XLA Modules:
  0.0 278.4 jit_solution(284571066530246054)
XLA Ops:
  7.2 1.3 broadcast_in_dim.8
  8.5 7.7 %all-to-all-start.1 = ((f32[8,12,96]{2,1,0:T(8,128)}), f32[8,12,96]{2,1,0:T(8,128)S(1)}, u32[]{:S(2)}, u32[]{:S(2)}) async-start(f32[8,12,96]{2,1,0:T(8,128)} %broadcast_in_dim.8), calls=%async_computation.1 | async-start | bytes 131072 | tf_op jit(solution)/shard_map/all_to_all | solution.py:32
  18.2 5.1 %all-to-all-done.1 = f32[8,12,96]{2,1,0:T(8,128)S(1)} async-done(((f32[8,12,96]{2,1,0:T(8,128)}), f32[8,12,96]{2,1,0:T(8,128)S(1)}, u32[]{:S(2)}, u32[]{:S(2)}) %all-to-all-start.1) | async-done | bytes 36896 | tf_op jit(solution)/shard_map/all_to_all | solution.py:32
  23.4 15.4 %all-to-all-start = ((f32[64,12,96]{2,1,0:T(8,128)}), f32[64,12,96]{2,1,0:T(8,128)S(1)}, u32[]{:S(2)}, u32[]{:S(2)}) async-start(f32[64,12,96]{2,1,0:T(8,128)} %reshape.50), calls=%async_computation | async-start | bytes 1048576 | tf_op jit(solution)/shard_map/all_to_all | solution.py:27
  39.9 16.6 %all-to-all-done = f32[64,12,96]{2,1,0:T(8,128)S(1)} async-done(((f32[64,12,96]{2,1,0:T(8,128)}), f32[64,12,96]{2,1,0:T(8,128)S(1)}, u32[]{:S(2)}, u32[]{:S(2)}) %all-to-all-start) | async-done | bytes 294944 | tf_op jit(solution)/shard_map/all_to_all | solution.py:27
  57.5 28.3 %all_to_all.30 = f32[64,2,12,96]{3,1,2,0:T(2,128)S(1)} all-to-all(f32[64,2,12,96]{3,1,2,0:T(2,128)S(1)} %broadcast_in_dim.9), channel_id=1, replica_groups=mesh['dp'=64,'mp'=8] {'dp'}, dimensions={0} | all-to-all | bytes 1179648 | tf_op jit(solution)/shard_map/all_to_all | solution.py:32
  87.4 34.7 %all-gather.9.cloned.1.call-done = f32[1,768,768]{1,0,2:T(1,128)} async-done(((f32[1,768,96]{1,0,2:T(1,128)}), f32[1,768,768]{1,0,2:T(1,128)}) %all-gather.9.cloned.1.call-update) | async-done | bytes 2359312 | tf_op jit(solution)/shard_map/all_gather | solution.py:65
  122.1 2.0 constant_dynamic-slice_fusion.1
  125.1 2.7 fusion.21
  127.9 1.2 fusion.18
  132.2 5.8 %collective-permute-start = (bf16[1,768,12]{1,2,0:T(8,128)(2,1)S(1)}, bf16[1,768,12]{1,2,0:T(8,128)(2,1)S(1)}, u32[]{:S(2)}, u32[]{:S(2)}) collective-permute-start(bf16[1,768,12]{1,2,0:T(8,128)(2,1)S(1)} %convert_bitcast_fusion.2), channel_id=1, source_target_pairs={{0,8},{8,0},{16,24},{24,16},{32,40},{40,32},{48,56},{56,48},{64,72... | collective-permute-start | bytes 55304 | tf_op jit(solution)/shard_map/ppermute | solution.py:41
  138.8 3.1 %collective-permute-start.1 = (bf16[2,768,12]{1,2,0:T(8,128)(2,1)S(1)}, bf16[2,768,12]{1,2,0:T(8,128)(2,1)S(1)}, u32[]{:S(2)}, u32[]{:S(2)}) collective-permute-start(bf16[2,768,12]{1,2,0:T(8,128)(2,1)S(1)} %pad_maximum_fusion.5), channel_id=1, source_target_pairs={{0,16},{8,24},{16,0},{24,8},{32,48},{40,56},{48,32},{56,40},{64,80... | collective-permute-start | bytes 110600 | tf_op jit(solution)/shard_map/ppermute | solution.py:41
  141.9 1.7 collective-permute-done.1
  143.7 4.6 %collective-permute-start.2 = (bf16[4,768,12]{1,2,0:T(8,128)(2,1)S(1)}, bf16[4,768,12]{1,2,0:T(8,128)(2,1)S(1)}, u32[]{:S(2)}, u32[]{:S(2)}) collective-permute-start(bf16[4,768,12]{1,2,0:T(8,128)(2,1)S(1)} %pad_maximum_fusion.4), channel_id=1, source_target_pairs={{0,32},{8,40},{16,48},{24,56},{32,0},{40,8},{48,16},{56,24},{64,96... | collective-permute-start | bytes 221192 | tf_op jit(solution)/shard_map/ppermute | solution.py:41
  148.3 2.2 collective-permute-done.2
  150.6 3.3 %collective-permute-start.3 = (bf16[8,768,12]{1,2,0:T(8,128)(2,1)S(1)}, bf16[8,768,12]{1,2,0:T(8,128)(2,1)S(1)}, u32[]{:S(2)}, u32[]{:S(2)}) collective-permute-start(bf16[8,768,12]{1,2,0:T(8,128)(2,1)S(1)} %pad_maximum_fusion.3), channel_id=1, source_target_pairs={{0,64},{8,72},{16,80},{24,88},{32,96},{40,104},{48,112},{56,120},{... | collective-permute-start | bytes 442376 | tf_op jit(solution)/shard_map/ppermute | solution.py:41
  153.9 3.5 %collective-permute-done.3 = bf16[8,768,12]{1,2,0:T(8,128)(2,1)S(1)} collective-permute-done((bf16[8,768,12]{1,2,0:T(8,128)(2,1)S(1)}, bf16[8,768,12]{1,2,0:T(8,128)(2,1)S(1)}, u32[]{:S(2)}, u32[]{:S(2)}) %collective-permute-start.3) | collective-permute-done | bytes 147488 | tf_op jit(solution)/shard_map/ppermute | solution.py:41
  158.4 4.0 %all-to-all-start.3 = ((f32[8,96,12]{1,2,0:T(8,128)}), f32[8,96,12]{1,2,0:T(8,128)S(1)}, u32[]{:S(2)}, u32[]{:S(2)}) async-start(f32[8,96,12]{1,2,0:T(8,128)} %copy.33), calls=%async_computation.3 | async-start | bytes 131072 | tf_op jit(solution)/shard_map/all_to_all | solution.py:27
  162.4 4.4 %collective-permute-start.4 = (bf16[16,768,12]{1,2,0:T(8,128)(2,1)S(1)}, bf16[16,768,12]{1,2,0:T(8,128)(2,1)S(1)}, u32[]{:S(2)}, u32[]{:S(2)}) collective-permute-start(bf16[16,768,12]{1,2,0:T(8,128)(2,1)S(1)} %pad_maximum_fusion.1), channel_id=1, source_target_pairs={{0,128},{8,136},{16,144},{24,152},{32,160},{40,168},{48,176},{56,1... | collective-permute-start | bytes 884744 | tf_op jit(solution)/shard_map/ppermute | solution.py:41
  166.8 3.1 %all-to-all-done.3 = f32[8,96,12]{1,2,0:T(8,128)S(1)} async-done(((f32[8,96,12]{1,2,0:T(8,128)}), f32[8,96,12]{1,2,0:T(8,128)S(1)}, u32[]{:S(2)}, u32[]{:S(2)}) %all-to-all-start.3) | async-done | bytes 36896 | tf_op jit(solution)/shard_map/all_to_all | solution.py:27
  171.2 15.1 %all-to-all-start.4 = ((f32[64,12,96]{2,1,0:T(8,128)}), f32[64,12,96]{2,1,0:T(8,128)S(1)}, u32[]{:S(2)}, u32[]{:S(2)}) async-start(f32[64,12,96]{2,1,0:T(8,128)} %reshape.54), calls=%async_computation.4 | async-start | bytes 1048576 | tf_op jit(solution)/shard_map/all_to_all | solution.py:27
  186.7 7.3 %collective-permute-start.5 = (bf16[32,768,12]{1,0,2:T(8,128)(2,1)S(1)}, bf16[32,768,12]{1,0,2:T(8,128)(2,1)S(1)}, u32[]{:S(2)}, u32[]{:S(2)}) collective-permute-start(bf16[32,768,12]{1,0,2:T(8,128)(2,1)S(1)} %copy.36), channel_id=1, source_target_pairs={{0,256},{8,264},{16,272},{24,280},{32,288},{40,296},{48,304},{56,3... | collective-permute-start | bytes 1769480 | tf_op jit(solution)/shard_map/ppermute | solution.py:41
  194.1 9.4 %all-to-all-done.4 = f32[64,12,96]{2,1,0:T(8,128)S(1)} async-done(((f32[64,12,96]{2,1,0:T(8,128)}), f32[64,12,96]{2,1,0:T(8,128)S(1)}, u32[]{:S(2)}, u32[]{:S(2)}) %all-to-all-start.4) | async-done | bytes 294944 | tf_op jit(solution)/shard_map/all_to_all | solution.py:27
  204.9 30.7 %all-to-all-start.5 = ((bf16[64,12,96]{2,1,0:T(8,128)(2,1)}), bf16[64,12,96]{2,1,0:T(8,128)(2,1)S(1)}, u32[]{:S(2)}, u32[]{:S(2)}) async-start(bf16[64,12,96]{2,1,0:T(8,128)(2,1)} %broadcast_in_dim.10), calls=%async_computation.5 | async-start | bytes 524288 | tf_op jit(solution)/shard_map/all_to_all | solution.py:32
  236.5 12.2 %all-to-all-done.5 = bf16[64,12,96]{2,1,0:T(8,128)(2,1)S(1)} async-done(((bf16[64,12,96]{2,1,0:T(8,128)(2,1)}), bf16[64,12,96]{2,1,0:T(8,128)(2,1)S(1)}, u32[]{:S(2)}, u32[]{:S(2)}) %all-to-all-start.5) | async-done | bytes 147488 | tf_op jit(solution)/shard_map/all_to_all | solution.py:32
  249.7 3.5 %multiply_reduce_fusion = (f32[]{:T(128)}, f32[768,768]{1,0:T(8,128)S(1)}) fusion(bf16[768,768]{0,1:T(8,128)(2,1)} %all-gather.5.cloned.1.call-done, bf16[2,768,768]{2,1,0:T(8,128)(2,1)} %all-gather.7.cloned.1.call-done), kind=kOutput, calls=%fused_computation.9 | convolution fusion | flops 907149312 | bytes 4718596 | tf_op jit(solution)/shard_map/dot_general | solution.py:106
  255.1 2.7 convolution_convert_fusion
  257.8 3.8 %add_convert_fusion = bf16[768,768]{1,0:T(8,128)(2,1)S(1)} fusion(bf16[768,768]{1,0:T(8,128)(2,1)} %multiply_convert_fusion, bf16[768,768]{1,0:T(8,128)(2,1)S(1)} %convolution_convert_fusion), kind=kOutput, calls=%fused_computation.6 | convolution fusion | flops 1817247744 | bytes 3538944 | tf_op jit(solution)/shard_map/dot_general | solution.py:116
  261.6 1.5 fusion.24
  263.0 3.2 %multiply_reduce_fusion.1 = (f32[]{:T(128)}, f32[768,768]{1,0:T(8,128)S(1)}) fusion(bf16[768,768]{0,1:T(8,128)(2,1)S(1)} %reshape.56, bf16[2,768,768]{2,1,0:T(8,128)(2,1)} %all-gather.7.cloned.1.call-done), kind=kOutput, calls=%fused_computation.13 | convolution fusion | flops 907149312 | bytes 4718596 | tf_op jit(solution)/shard_map/dot_general | solution.py:106
  268.2 2.1 add_convert_fusion.2
  270.4 1.5 fusion.25
  (81 shorter events, 19.0 us)
Async XLA Ops:
  8.5 14.9 %all-to-all-start.1 = ((f32[8,12,96]{2,1,0:T(8,128)}), f32[8,12,96]{2,1,0:T(8,128)S(1)}, u32[]{:S(2)}, u32[]{:S(2)}) async-start(f32[8,12,96]{2,1,0:T(8,128)} %broadcast_in_dim.8), calls=%async_computation.1 | async-start | bytes 131072 | tf_op jit(solution)/shard_map/all_to_all | solution.py:32
  17.2 21.7 %copy-start.1 = (f32[768,96]{0,1:T(8,128)S(1)}, f32[768,96]{0,1:T(8,128)}, u32[]{:S(2)}) copy-start(f32[768,96]{0,1:T(8,128)} %param.13) | copy-start | bytes 884740
  18.2 38.4 %copy-start.7 = (f32[12,96]{1,0:T(8,128)S(1)}, f32[12,96]{1,0:T(8,128)}, u32[]{:S(2)}) copy-start(f32[12,96]{1,0:T(8,128)} %param.10) | copy-start | bytes 13828
  23.4 33.2 %all-to-all-start = ((f32[64,12,96]{2,1,0:T(8,128)}), f32[64,12,96]{2,1,0:T(8,128)S(1)}, u32[]{:S(2)}, u32[]{:S(2)}) async-start(f32[64,12,96]{2,1,0:T(8,128)} %reshape.50), calls=%async_computation | async-start | bytes 1048576 | tf_op jit(solution)/shard_map/all_to_all | solution.py:27
  38.8 46.9 %all-gather.5.cloned.1.call-start = ((), (), s32[]{:S(2)}) async-start(), calls=%async_computation.6 | async-start | bytes 1327104 | tf_op jit(solution)/shard_map/all_gather | solution.py:63
  39.6 82.5 %all-gather.9.cloned.1.call-start = ((), (), s32[]{:S(2)}) async-start(), calls=%async_computation.8 | async-start | bytes 2654208 | tf_op jit(solution)/shard_map/all_gather | solution.py:65
  87.4 162.3 %all-gather.7.cloned.1.call-start = ((), (), s32[]{:S(2)}) async-start(), calls=%async_computation.7 | async-start | bytes 2654208 | tf_op jit(solution)/shard_map/all_gather | solution.py:91
  125.1 2.7 copy-start
  125.1 2.7 copy-start.5
  127.9 1.3 copy-start.3
  129.1 0.7 copy-start.4
  129.1 1.4 copy-start.2
  130.6 1.1 copy-start.8
  131.8 18.7 %copy-start.6 = (f32[12,96]{1,0:T(8,128)}, f32[12,96]{1,0:T(8,128)S(1)}, u32[]{:S(2)}) copy-start(f32[12,96]{1,0:T(8,128)S(1)} %get-tuple-element.58) | copy-start | bytes 13828
  132.2 6.6 %collective-permute-start = (bf16[1,768,12]{1,2,0:T(8,128)(2,1)S(1)}, bf16[1,768,12]{1,2,0:T(8,128)(2,1)S(1)}, u32[]{:S(2)}, u32[]{:S(2)}) collective-permute-start(bf16[1,768,12]{1,2,0:T(8,128)(2,1)S(1)} %convert_bitcast_fusion.2), channel_id=1, source_target_pairs={{0,8},{8,0},{16,24},{24,16},{32,40},{40,32},{48,56},{56,48},{64,72... | collective-permute-start | bytes 55304 | tf_op jit(solution)/shard_map/ppermute | solution.py:41
  138.8 4.8 %collective-permute-start.1 = (bf16[2,768,12]{1,2,0:T(8,128)(2,1)S(1)}, bf16[2,768,12]{1,2,0:T(8,128)(2,1)S(1)}, u32[]{:S(2)}, u32[]{:S(2)}) collective-permute-start(bf16[2,768,12]{1,2,0:T(8,128)(2,1)S(1)} %pad_maximum_fusion.5), channel_id=1, source_target_pairs={{0,16},{8,24},{16,0},{24,8},{32,48},{40,56},{48,32},{56,40},{64,80... | collective-permute-start | bytes 110600 | tf_op jit(solution)/shard_map/ppermute | solution.py:41
  143.7 6.9 %collective-permute-start.2 = (bf16[4,768,12]{1,2,0:T(8,128)(2,1)S(1)}, bf16[4,768,12]{1,2,0:T(8,128)(2,1)S(1)}, u32[]{:S(2)}, u32[]{:S(2)}) collective-permute-start(bf16[4,768,12]{1,2,0:T(8,128)(2,1)S(1)} %pad_maximum_fusion.4), channel_id=1, source_target_pairs={{0,32},{8,40},{16,48},{24,56},{32,0},{40,8},{48,16},{56,24},{64,96... | collective-permute-start | bytes 221192 | tf_op jit(solution)/shard_map/ppermute | solution.py:41
  150.6 6.8 %collective-permute-start.3 = (bf16[8,768,12]{1,2,0:T(8,128)(2,1)S(1)}, bf16[8,768,12]{1,2,0:T(8,128)(2,1)S(1)}, u32[]{:S(2)}, u32[]{:S(2)}) collective-permute-start(bf16[8,768,12]{1,2,0:T(8,128)(2,1)S(1)} %pad_maximum_fusion.3), channel_id=1, source_target_pairs={{0,64},{8,72},{16,80},{24,88},{32,96},{40,104},{48,112},{56,120},{... | collective-permute-start | bytes 442376 | tf_op jit(solution)/shard_map/ppermute | solution.py:41
  158.4 11.5 %all-to-all-start.3 = ((f32[8,96,12]{1,2,0:T(8,128)}), f32[8,96,12]{1,2,0:T(8,128)S(1)}, u32[]{:S(2)}, u32[]{:S(2)}) async-start(f32[8,96,12]{1,2,0:T(8,128)} %copy.33), calls=%async_computation.3 | async-start | bytes 131072 | tf_op jit(solution)/shard_map/all_to_all | solution.py:27
  162.4 24.0 %collective-permute-start.4 = (bf16[16,768,12]{1,2,0:T(8,128)(2,1)S(1)}, bf16[16,768,12]{1,2,0:T(8,128)(2,1)S(1)}, u32[]{:S(2)}, u32[]{:S(2)}) collective-permute-start(bf16[16,768,12]{1,2,0:T(8,128)(2,1)S(1)} %pad_maximum_fusion.1), channel_id=1, source_target_pairs={{0,128},{8,136},{16,144},{24,152},{32,160},{40,168},{48,176},{56,1... | collective-permute-start | bytes 884744 | tf_op jit(solution)/shard_map/ppermute | solution.py:41
  171.2 32.3 %all-to-all-start.4 = ((f32[64,12,96]{2,1,0:T(8,128)}), f32[64,12,96]{2,1,0:T(8,128)S(1)}, u32[]{:S(2)}, u32[]{:S(2)}) async-start(f32[64,12,96]{2,1,0:T(8,128)} %reshape.54), calls=%async_computation.4 | async-start | bytes 1048576 | tf_op jit(solution)/shard_map/all_to_all | solution.py:27
  186.5 17.0 %copy-start.9 = (f32[12,96]{1,0:T(8,128)S(1)}, f32[12,96]{1,0:T(8,128)}, u32[]{:S(2)}) copy-start(f32[12,96]{1,0:T(8,128)} %param.9) | copy-start | bytes 13828
  186.7 48.9 %collective-permute-start.5 = (bf16[32,768,12]{1,0,2:T(8,128)(2,1)S(1)}, bf16[32,768,12]{1,0,2:T(8,128)(2,1)S(1)}, u32[]{:S(2)}, u32[]{:S(2)}) collective-permute-start(bf16[32,768,12]{1,0,2:T(8,128)(2,1)S(1)} %copy.36), channel_id=1, source_target_pairs={{0,256},{8,264},{16,272},{24,280},{32,288},{40,296},{48,304},{56,3... | collective-permute-start | bytes 1769480 | tf_op jit(solution)/shard_map/ppermute | solution.py:41
  204.9 43.9 %all-to-all-start.5 = ((bf16[64,12,96]{2,1,0:T(8,128)(2,1)}), bf16[64,12,96]{2,1,0:T(8,128)(2,1)S(1)}, u32[]{:S(2)}, u32[]{:S(2)}) async-start(bf16[64,12,96]{2,1,0:T(8,128)(2,1)} %broadcast_in_dim.10), calls=%async_computation.5 | async-start | bytes 524288 | tf_op jit(solution)/shard_map/all_to_all | solution.py:32
Sparse Core Ops, SparseCore 0:
  42.3 32.8 all-gather.4
  87.5 34.5 all-gather.8
  132.3 43.9 all-gather.6

commit v12 on v9

--- a/solution.py
+++ b/solution.py
@@ -87,28 +87,30 @@
     weights_block = gather_rows(new_master.astype(jnp.bfloat16), "dp").reshape(
         -1, new_master.shape[1]
     )
-    new_bases = []
-    for stat_part, basis_part in zip(stat_whole, (left_full, right_full)):
-        power_part = jnp.dot(
-            stat_part, basis_part.astype(jnp.bfloat16), preferred_element_type=jnp.float32
+    basis_whole = jnp.stack([left_full.astype(jnp.bfloat16), right_full.astype(jnp.bfloat16)])
+    power = jnp.einsum("sij,sjk->sik", stat_whole, basis_whole, preferred_element_type=jnp.float32)
+    total = jnp.sum(power * power, axis=(1, 2), keepdims=True)
+    start = lax.optimization_barrier(
+        (power * lax.rsqrt(total * (4.0 / order_count) + norm_eps)).astype(jnp.bfloat16)
+    )
+    gram = lax.optimization_barrier(
+        jnp.einsum("sij,skj->sik", start, start, preferred_element_type=jnp.float32).astype(
+            jnp.bfloat16
         )
-        total = jnp.sum(power_part * power_part)
-        whole_part = lax.optimization_barrier(
-            (power_part * lax.rsqrt(total * (4.0 / order_count) + norm_eps)).astype(jnp.bfloat16)
-        )
-        gram = lax.optimization_barrier(row_gram(whole_part, whole_part).astype(jnp.bfloat16))
-        square = jnp.dot(gram, gram, preferred_element_type=jnp.float32)
-        poly = (quint_b * gram.astype(jnp.float32) + quint_c * square).astype(jnp.bfloat16)
-        middle = quint_a * whole_part.astype(jnp.float32) + jnp.dot(
-            poly, whole_part, preferred_element_type=jnp.float32
-        )
-        middle = lax.optimization_barrier(middle.astype(jnp.bfloat16))
-        middle_rows = lax.dynamic_slice_in_dim(middle, band_start, band_width, 0)
-        gram_two = row_gram(middle_rows, middle).astype(jnp.bfloat16)
-        new_bases.append(
-            1.5 * middle_rows.astype(jnp.float32)
-            - 0.5 * jnp.dot(gram_two, middle, preferred_element_type=jnp.float32)
-        )
+    )
+    square = jnp.einsum("sij,sjk->sik", gram, gram, preferred_element_type=jnp.float32)
+    poly = (quint_b * gram.astype(jnp.float32) + quint_c * square).astype(jnp.bfloat16)
+    middle = quint_a * start.astype(jnp.float32) + jnp.einsum(
+        "sij,sjk->sik", poly, start, preferred_element_type=jnp.float32
+    )
+    middle = lax.optimization_barrier(middle.astype(jnp.bfloat16))
+    middle_rows = lax.dynamic_slice_in_dim(middle, band_start, band_width, 1)
+    gram_two = jnp.einsum(
+        "sij,skj->sik", middle_rows, middle, preferred_element_type=jnp.float32
+    ).astype(jnp.bfloat16)
+    new_bases = 1.5 * middle_rows.astype(jnp.float32) - 0.5 * jnp.einsum(
+        "sij,sjk->sik", gram_two, middle, preferred_element_type=jnp.float32
+    )
     return (
         weights_block,
         new_master,

time: 229 us -> 225 us (0.983)
  blocking collectives: 81.9 us -> 63.2 us
  waiting for transfers between devices: 60.8 us -> 70.9 us
  starting transfers between devices: 29.4 us -> 35.2 us
  local copies, waits for them, and re-layouts: 11.8 us -> 14.9 us
  matrix products: 24.3 us -> 21.7 us
    all_to_all x2 -> x1, blocking collectives: 47 us -> 28.3 us  [gather_rows(): lax.all_to_all(jnp.broadcast_to(x[None], (count,) + x.shape), axis, 0, 0,...]
    all_to_all x2 -> x3, waiting for transfers between devices: 44.1 us -> 54.2 us  [gather_rows(): lax.all_to_all(jnp.broadcast_to(x[None], (count,) + x.shape), axis, 0, 0,...]
    all_to_all x2 -> x3, starting transfers between devices: 13.9 us -> 19.6 us  [gather_rows(): lax.all_to_all(jnp.broadcast_to(x[None], (count,) + x.shape), axis, 0, 0,...]
    optimization_barrier x0 -> x2, local copies, waits for them, and re-layouts: none -> 3.04 us  [the longest x1 1.57 us: per_device(): pieces, right_full = lax.optimization_barrier((pieces, right_full))]
    dot_general x8 -> x4, matrix products: 19.8 us -> 17.2 us  [the longest x1 8.28 us: per_device(): jnp.einsum('sij,sjk->sik', poly, start, preferred_element_type=jnp.float32)]
    unnamed x26 -> x24, local copies, waits for them, and re-layouts: 4.74 us -> 4.11 us
  transfers between devices with their start and end apart: 6 -> 7, of which waited for: 3 -> 4; matrix products, arithmetic and copies ran while one was open for 4% -> 5% of each run, Pallas kernels for 0% -> 0%
where the time goes in v12:
time: 225 us; the launch traced here: 224 us
  waiting for transfers between devices  70.9 us (32%)
  blocking collectives  63.2 us (28%)
  starting transfers between devices  35.2 us (16%)
  matrix products  21.7 us (10%)
  local copies, waits for them, and re-layouts  14.9 us (7%)
  between operations  14.1 us (6%)
  other arithmetic  4.36 us (2%)
    all_to_all x3, waiting for transfers between devices, gather_rows(): lax.all_to_all(jnp.broadcast_to(x[None], (count,) + x.shape), axis, 0, 0,...  54.2 us
    all_to_all x2, blocking collectives, scatter_sum(): return jnp.sum(lax.all_to_all(chunks, axis, 0, 0, tiled=False), axis=0)  34.9 us
    all_to_all x1, blocking collectives, gather_rows(): lax.all_to_all(jnp.broadcast_to(x[None], (count,) + x.shape), axis, 0, 0,...  28.3 us
    all_to_all x3, starting transfers between devices, gather_rows(): lax.all_to_all(jnp.broadcast_to(x[None], (count,) + x.shape), axis, 0, 0,...  19.6 us
    all_to_all x1, waiting for transfers between devices, scatter_sum(): return jnp.sum(lax.all_to_all(chunks, axis, 0, 0, tiled=False), axis=0)  16.6 us
    all_to_all x1, starting transfers between devices, scatter_sum(): return jnp.sum(lax.all_to_all(chunks, axis, 0, 0, tiled=False), axis=0)  15.4 us
    dot_general x1, matrix products, per_device(): jnp.einsum('sij,sjk->sik', poly, start, preferred_element_type=jnp.float32)  8.28 us
  transfers between devices with their start and end apart: 7, of which 4 were waited for; matrix products, arithmetic and copies ran while one was open for 5% of the time, Pallas kernels for 0%

profile of v12, /device:TPU:1, one launch (start us, length us, event | category | flops | bytes accessed | tf_op | source)
XLA Modules:
  0.0 224.4 jit_solution(9997716023851427241)
XLA Ops:
  7.2 1.4 broadcast_in_dim.8
  8.6 7.7 %all-to-all-start.1 = ((f32[8,12,96]{2,1,0:T(8,128)}), f32[8,12,96]{2,1,0:T(8,128)S(1)}, u32[]{:S(2)}, u32[]{:S(2)}) async-start(f32[8,12,96]{2,1,0:T(8,128)} %broadcast_in_dim.8), calls=%async_computation.1 | async-start | bytes 131072 | tf_op jit(solution)/shard_map/all_to_all | solution.py:32
  16.2 1.0 convert_reduce_fusion
  17.4 0.8 reshape.59
  18.2 5.2 %all-to-all-done.1 = f32[8,12,96]{2,1,0:T(8,128)S(1)} async-done(((f32[8,12,96]{2,1,0:T(8,128)}), f32[8,12,96]{2,1,0:T(8,128)S(1)}, u32[]{:S(2)}, u32[]{:S(2)}) %all-to-all-start.1) | async-done | bytes 36896 | tf_op jit(solution)/shard_map/all_to_all | solution.py:32
  23.4 15.4 %all-to-all-start = ((f32[64,12,96]{2,1,0:T(8,128)}), f32[64,12,96]{2,1,0:T(8,128)S(1)}, u32[]{:S(2)}, u32[]{:S(2)}) async-start(f32[64,12,96]{2,1,0:T(8,128)} %reshape.59), calls=%async_computation | async-start | bytes 1048576 | tf_op jit(solution)/shard_map/all_to_all | solution.py:27
  38.9 0.7 convert.12
  40.0 16.6 %all-to-all-done = f32[64,12,96]{2,1,0:T(8,128)S(1)} async-done(((f32[64,12,96]{2,1,0:T(8,128)}), f32[64,12,96]{2,1,0:T(8,128)S(1)}, u32[]{:S(2)}, u32[]{:S(2)}) %all-to-all-start) | async-done | bytes 294944 | tf_op jit(solution)/shard_map/all_to_all | solution.py:27
  57.5 28.3 %all_to_all.35 = f32[64,2,12,96]{3,1,2,0:T(2,128)S(1)} all-to-all(f32[64,2,12,96]{3,1,2,0:T(2,128)S(1)} %broadcast_in_dim.9), channel_id=1, replica_groups=mesh['dp'=64,'mp'=8] {'dp'}, dimensions={0} | all-to-all | bytes 1179648 | tf_op jit(solution)/shard_map/all_to_all | solution.py:32
  86.4 1.0 copy.27
  87.4 1.2 broadcast_in_dim.10
  88.7 6.2 %all-to-all-start.3 = ((bf16[64,768,12]{1,2,0:T(8,128)(2,1)}), bf16[64,768,12]{1,2,0:T(8,128)(2,1)S(1)}, u32[]{:S(2)}, u32[]{:S(2)}) async-start(bf16[64,768,12]{1,2,0:T(8,128)(2,1)} %broadcast_in_dim.10), calls=%async_computation.3 | async-start | bytes 3145728 | tf_op jit(solution)/shard_map/all_to_all | solution.py:32
  95.0 38.9 %all-to-all-done.3 = bf16[64,768,12]{1,2,0:T(8,128)(2,1)S(1)} async-done(((bf16[64,768,12]{1,2,0:T(8,128)(2,1)}), bf16[64,768,12]{1,2,0:T(8,128)(2,1)S(1)}, u32[]{:S(2)}, u32[]{:S(2)}) %all-to-all-start.3) | async-done | bytes 1179680 | tf_op jit(solution)/shard_map/all_to_all | solution.py:32
  134.3 1.8 copy.37
  136.1 1.1 fusion.29
  137.2 1.1 fusion.9
  138.3 1.3 fusion.8
  139.9 0.7 pad_maximum_fusion
  141.2 9.7 %all_to_all.36 = f32[8,96,12]{1,2,0:T(8,128)S(1)} all-to-all(f32[8,96,12]{1,2,0:T(8,128)S(1)} %copy.28), channel_id=1, replica_groups=mesh['dp'=64,'mp'=8] {'mp'}, dimensions={0} | all-to-all | bytes 73728 | tf_op jit(solution)/shard_map/all_to_all | solution.py:27
  151.4 25.3 %all_to_all.37 = f32[64,12,96]{2,1,0:T(8,128)S(1)} all-to-all(f32[64,12,96]{2,1,0:T(8,128)S(1)} %reshape.64), channel_id=1, replica_groups=mesh['dp'=64,'mp'=8] {'dp'}, dimensions={0} | all-to-all | bytes 589824 | tf_op jit(solution)/shard_map/all_to_all | solution.py:27
  177.4 0.7 broadcast_in_dim.11
  178.1 5.7 %all-to-all-start.6 = ((bf16[64,12,96]{2,1,0:T(8,128)(2,1)}), bf16[64,12,96]{2,1,0:T(8,128)(2,1)S(1)}, u32[]{:S(2)}, u32[]{:S(2)}) async-start(bf16[64,12,96]{2,1,0:T(8,128)(2,1)} %broadcast_in_dim.11), calls=%async_computation.6 | async-start | bytes 524288 | tf_op jit(solution)/shard_map/all_to_all | solution.py:32
  183.9 1.6 copy.32
  185.4 1.5 copy.31
  186.9 10.1 %all-to-all-done.6 = bf16[64,12,96]{2,1,0:T(8,128)(2,1)S(1)} async-done(((bf16[64,12,96]{2,1,0:T(8,128)(2,1)}), bf16[64,12,96]{2,1,0:T(8,128)(2,1)S(1)}, u32[]{:S(2)}, u32[]{:S(2)}) %all-to-all-start.6) | async-done | bytes 147488 | tf_op jit(solution)/shard_map/all_to_all | solution.py:32
  197.1 0.8 copy.33
  197.9 4.3 %multiply_reduce_fusion = (f32[2]{0:T(128)S(1)}, f32[2,768,768]{2,1,0:T(8,128)S(1)}) fusion(bf16[2,768,768]{2,1,0:T(8,128)(2,1)} %all-gather.7.cloned.1.call-done, bf16[1,768,768]{2,1,0:T(8,128)(2,1)S(1)} %bitcast.67, bf16[1,768,768]{2,1,0:T(8,128)(2,1)} %bitcast.68), kind=kOutput, calls=%fused_computation.3 | convolution fusion | flops 1815478272 | bytes 9437192 | tf_op jit(solution)/shard_map/sij,sjk->sik/dot_general | solution.py:91
  202.6 1.4 copy-done.1
  204.1 3.4 %convolution_convert_fusion = bf16[2,768,768]{2,1,0:T(8,128)(2,1)} fusion(bf16[2,768,768]{2,1,0:T(8,128)(2,1)S(1)} %multiply_convert_fusion), kind=kOutput, calls=%fused_computation.12 | convolution fusion | flops 1813118976 | bytes 4718592 | tf_op jit(solution)/shard_map/sij,skj->sik/dot_general | solution.py:97
  207.5 8.3 %add_convert_fusion = bf16[2,768,768]{2,1,0:T(8,128)(2,1)S(1)} fusion(bf16[2,768,768]{2,1,0:T(8,128)(2,1)} %copy-done.1, bf16[2,768,768]{2,1,0:T(8,128)(2,1)} %convolution_convert_fusion), kind=kOutput, calls=%fused_computation | convolution fusion | flops 3634495488 | bytes 7077888 | tf_op jit(solution)/shard_map/sij,sjk->sik/dot_general | solution.py:103
  215.8 1.2 fusion.7
  217.0 0.9 slice_bitcast_fusion
  (57 shorter events, 5.1 us)
Async XLA Ops:
  7.2 31.8 %copy-start = (f32[768,96]{0,1:T(8,128)S(1)}, f32[768,96]{0,1:T(8,128)}, u32[]{:S(2)}) copy-start(f32[768,96]{0,1:T(8,128)} %param.13) | copy-start | bytes 884740
  8.6 14.9 %all-to-all-start.1 = ((f32[8,12,96]{2,1,0:T(8,128)}), f32[8,12,96]{2,1,0:T(8,128)S(1)}, u32[]{:S(2)}, u32[]{:S(2)}) async-start(f32[8,12,96]{2,1,0:T(8,128)} %broadcast_in_dim.8), calls=%async_computation.1 | async-start | bytes 131072 | tf_op jit(solution)/shard_map/all_to_all | solution.py:32
  16.2 40.5 %copy-start.8 = (f32[12,96]{1,0:T(8,128)S(1)}, f32[12,96]{1,0:T(8,128)}, u32[]{:S(2)}) copy-start(f32[12,96]{1,0:T(8,128)} %param.10) | copy-start | bytes 13828
  23.4 33.2 %all-to-all-start = ((f32[64,12,96]{2,1,0:T(8,128)}), f32[64,12,96]{2,1,0:T(8,128)S(1)}, u32[]{:S(2)}, u32[]{:S(2)}) async-start(f32[64,12,96]{2,1,0:T(8,128)} %reshape.59), calls=%async_computation | async-start | bytes 1048576 | tf_op jit(solution)/shard_map/all_to_all | solution.py:27
  38.9 46.9 %all-gather.5.cloned.1.call-start = ((), (), s32[]{:S(2)}) async-start(), calls=%async_computation.7 | async-start | bytes 1327104 | tf_op jit(solution)/shard_map/all_gather | solution.py:48
  39.6 94.6 %all-gather.9.cloned.1.call-start = ((), (), s32[]{:S(2)}) async-start(), calls=%async_computation.9 | async-start | bytes 2654208 | tf_op jit(solution)/shard_map/all_gather | solution.py:50
  57.3 30.1 %copy-start.4 = (f32[768,12]{0,1:T(8,128)S(1)}, f32[768,12]{0,1:T(8,128)}, u32[]{:S(2)}) copy-start(f32[768,12]{0,1:T(8,128)} %param.12) | copy-start | bytes 110596
  88.7 45.2 %all-to-all-start.3 = ((bf16[64,768,12]{1,2,0:T(8,128)(2,1)}), bf16[64,768,12]{1,2,0:T(8,128)(2,1)S(1)}, u32[]{:S(2)}, u32[]{:S(2)}) async-start(bf16[64,768,12]{1,2,0:T(8,128)(2,1)} %broadcast_in_dim.10), calls=%async_computation.3 | async-start | bytes 3145728 | tf_op jit(solution)/shard_map/all_to_all | solution.py:32
  94.9 103.0 %all-gather.7.cloned.1.call-start = ((), (), s32[]{:S(2)}) async-start(), calls=%async_computation.8 | async-start | bytes 2654208 | tf_op jit(solution)/shard_map/all_gather | solution.py:77
  136.1 1.1 copy-start.5
  136.1 2.1 copy-start.6
  137.2 2.4 %copy-start.9 = (f32[12,96]{1,0:T(8,128)S(1)}, f32[12,96]{1,0:T(8,128)}, u32[]{:S(2)}) copy-start(f32[12,96]{1,0:T(8,128)} %param.11) | copy-start | bytes 13828
  138.2 2.4 %copy-start.2 = (f32[96,768]{1,0:T(8,128)}, f32[96,768]{1,0:T(8,128)S(1)}, u32[]{:S(2)}) copy-start(f32[96,768]{1,0:T(8,128)S(1)} %fusion.9) | copy-start | bytes 884740
  139.6 11.3 %copy-start.3 = (f32[96,768]{1,0:T(8,128)}, f32[96,768]{1,0:T(8,128)S(1)}, u32[]{:S(2)}) copy-start(f32[96,768]{1,0:T(8,128)S(1)} %fusion.8) | copy-start | bytes 884740
  139.8 11.6 %copy-start.7 = (f32[12,96]{1,0:T(8,128)}, f32[12,96]{1,0:T(8,128)S(1)}, u32[]{:S(2)}) copy-start(f32[12,96]{1,0:T(8,128)S(1)} %get-tuple-element.44) | copy-start | bytes 13828
  140.8 36.0 %copy-start.10 = (f32[12,96]{1,0:T(8,128)S(1)}, f32[12,96]{1,0:T(8,128)}, u32[]{:S(2)}) copy-start(f32[12,96]{1,0:T(8,128)} %param.9) | copy-start | bytes 13828
  178.1 18.9 %all-to-all-start.6 = ((bf16[64,12,96]{2,1,0:T(8,128)(2,1)}), bf16[64,12,96]{2,1,0:T(8,128)(2,1)S(1)}, u32[]{:S(2)}, u32[]{:S(2)}) async-start(bf16[64,12,96]{2,1,0:T(8,128)(2,1)} %broadcast_in_dim.11), calls=%async_computation.6 | async-start | bytes 524288 | tf_op jit(solution)/shard_map/all_to_all | solution.py:32
  202.6 1.4 copy-start.1
Sparse Core Ops, SparseCore 0:
  42.4 32.8 all-gather.4
  87.5 34.5 all-gather.8
  141.0 33.4 all-gather.6

commit v13 on v12

--- a/solution.py
+++ b/solution.py
@@ -38,20 +38,20 @@
     local_sum = jnp.sum(micro_grads[0], axis=0, dtype=jnp.float32)
     grad_piece = scatter_sum(local_sum, "dp") / (micro_count * dp_count)
     new_moment = beta_one * moment + (1.0 - beta_one) * grad_piece
-    moment_rows = gather_rows(moment, "mp")
-    moment_rows = jnp.moveaxis(moment_rows, 0, 1).reshape(moment.shape[0], -1)
-    moment_right = jnp.dot(moment_rows, right_basis, precision=highest)
-    pieces = gather_rows(jnp.stack([grad_piece, moment_right]), "dp")
+    pieces = gather_rows(jnp.stack([grad_piece, moment]), "dp")
     pieces = jnp.swapaxes(pieces, 0, 1).reshape(2, -1, pieces.shape[-1])
     left_cols = gather_rows(left_basis.astype(jnp.bfloat16), "dp")
     left_full = jnp.moveaxis(left_cols, 0, 1).reshape(left_basis.shape[0], -1)
-    right_full = lax.all_gather(right_basis, "mp", axis=1, tiled=True)
-    pieces, right_full = lax.optimization_barrier((pieces, right_full))
-    grad_full = lax.all_gather(pieces[0], "mp", axis=1, tiled=True)
-    grad_full, left_full = lax.optimization_barrier((grad_full, left_full))
-    moment_turned = lax.dot_general(
+    moment_left = lax.dot_general(
         left_basis, pieces[1], (((0,), (0,)), ((), ())), precision=highest
     )
+    packed = jnp.concatenate([pieces[0], moment_left], axis=0)
+    right_full = lax.all_gather(right_basis, "mp", axis=1, tiled=True)
+    packed, right_full = lax.optimization_barrier((packed, right_full))
+    gathered = lax.all_gather(packed, "mp", axis=1, tiled=True)
+    grad_full = gathered[: pieces.shape[1]]
+    grad_full, left_full = lax.optimization_barrier((grad_full, left_full))
+    moment_turned = jnp.dot(gathered[pieces.shape[1] :], right_basis, precision=highest)
 
     def rotate(matrix):
         left_part = lax.dot_general(left_basis, matrix, (((0,), (0,)), ((), ())), precision=highest)

time: 225 us -> 216 us (0.960)
  starting transfers between devices: 35.2 us -> 29.5 us
  waiting for transfers between devices: 70.9 us -> 66.1 us
    all_to_all x3 -> x2, waiting for transfers between devices: 54.2 us -> 49.1 us  [gather_rows(): lax.all_to_all(jnp.broadcast_to(x[None], (count,) + x.shape), axis, 0, 0,...]
    all_to_all x3 -> x2, starting transfers between devices: 19.6 us -> 14.6 us  [gather_rows(): lax.all_to_all(jnp.broadcast_to(x[None], (count,) + x.shape), axis, 0, 0,...]
  transfers between devices with their start and end apart: 7 -> 6, of which waited for: 4 -> 3; matrix products, arithmetic and copies ran while one was open for 5% -> 5% of each run, Pallas kernels for 0% -> 0%
where the time goes in v13:
time: 216 us
  waiting for transfers between devices  66.1 us (31%)
  blocking collectives  65 us (30%)
  starting transfers between devices  29.5 us (14%)
  matrix products  23 us (11%)
  between operations  14.1 us (7%)
  local copies, waits for them, and re-layouts  13.4 us (6%)
  other arithmetic  4.43 us (2%)
    all_to_all x2, waiting for transfers between devices, gather_rows(): lax.all_to_all(jnp.broadcast_to(x[None], (count,) + x.shape), axis, 0, 0,...  49.1 us
    all_to_all x2, blocking collectives, scatter_sum(): return jnp.sum(lax.all_to_all(chunks, axis, 0, 0, tiled=False), axis=0)  36.8 us
    all_to_all x1, blocking collectives, gather_rows(): lax.all_to_all(jnp.broadcast_to(x[None], (count,) + x.shape), axis, 0, 0,...  28.3 us
    all_to_all x1, waiting for transfers between devices, scatter_sum(): return jnp.sum(lax.all_to_all(chunks, axis, 0, 0, tiled=False), axis=0)  16.9 us
    all_to_all x1, starting transfers between devices, scatter_sum(): return jnp.sum(lax.all_to_all(chunks, axis, 0, 0, tiled=False), axis=0)  14.8 us
    all_to_all x2, starting transfers between devices, gather_rows(): lax.all_to_all(jnp.broadcast_to(x[None], (count,) + x.shape), axis, 0, 0,...  14.6 us
    dot_general x1, matrix products, per_device(): jnp.einsum('sij,sjk->sik', poly, start, preferred_element_type=jnp.float32)  8.28 us
  transfers between devices with their start and end apart: 6, of which 3 were waited for; matrix products, arithmetic and copies ran while one was open for 5% of the time, Pallas kernels for 0%

profile of v13, /device:TPU:1, one launch (start us, length us, event | category | flops | bytes accessed | tf_op | source)
XLA Modules:
  0.0 215.5 jit_solution(16375267789738821870)
XLA Ops:
  7.2 1.1 convert_reduce_fusion
  8.4 0.8 reshape.57
  9.3 14.8 %all-to-all-start = ((f32[64,12,96]{2,1,0:T(8,128)}), f32[64,12,96]{2,1,0:T(8,128)S(1)}, u32[]{:S(2)}, u32[]{:S(2)}) async-start(f32[64,12,96]{2,1,0:T(8,128)} %reshape.57), calls=%async_computation | async-start | bytes 1048576 | tf_op jit(solution)/shard_map/all_to_all | solution.py:27
  24.2 0.7 convert.12
  24.9 16.9 %all-to-all-done = f32[64,12,96]{2,1,0:T(8,128)S(1)} async-done(((f32[64,12,96]{2,1,0:T(8,128)}), f32[64,12,96]{2,1,0:T(8,128)S(1)}, u32[]{:S(2)}, u32[]{:S(2)}) %all-to-all-start) | async-done | bytes 294944 | tf_op jit(solution)/shard_map/all_to_all | solution.py:27
  42.8 28.3 %all_to_all.30 = f32[64,2,12,96]{3,1,2,0:T(2,128)S(1)} all-to-all(f32[64,2,12,96]{3,1,2,0:T(2,128)S(1)} %broadcast_in_dim.6), channel_id=1, replica_groups=mesh['dp'=64,'mp'=8] {'dp'}, dimensions={0} | all-to-all | bytes 1179648 | tf_op jit(solution)/shard_map/all_to_all | solution.py:32
  71.0 0.6 fusion.28
  71.9 0.9 copy.25
  72.9 1.2 broadcast_in_dim.7
  74.1 8.8 %all-to-all-start.2 = ((bf16[64,768,12]{1,2,0:T(8,128)(2,1)}), bf16[64,768,12]{1,2,0:T(8,128)(2,1)S(1)}, u32[]{:S(2)}, u32[]{:S(2)}) async-start(bf16[64,768,12]{1,2,0:T(8,128)(2,1)} %broadcast_in_dim.7), calls=%async_computation.2 | async-start | bytes 3145728 | tf_op jit(solution)/shard_map/all_to_all | solution.py:32
  83.0 38.9 %all-to-all-done.2 = bf16[64,768,12]{1,2,0:T(8,128)(2,1)S(1)} async-done(((bf16[64,768,12]{1,2,0:T(8,128)(2,1)}), bf16[64,768,12]{1,2,0:T(8,128)(2,1)S(1)}, u32[]{:S(2)}, u32[]{:S(2)}) %all-to-all-start.2) | async-done | bytes 1179680 | tf_op jit(solution)/shard_map/all_to_all | solution.py:32
  122.3 1.8 slice.29
  124.2 1.1 fusion.29
  125.2 1.1 fusion.9
  126.3 1.3 fusion.8
  127.9 0.7 pad_maximum_fusion.1
  128.7 1.4 fusion.13
  130.4 11.4 %all_to_all.31 = f32[8,96,12]{1,2,0:T(8,128)S(1)} all-to-all(f32[8,96,12]{1,2,0:T(8,128)S(1)} %copy.26), channel_id=1, replica_groups=mesh['dp'=64,'mp'=8] {'mp'}, dimensions={0} | all-to-all | bytes 73728 | tf_op jit(solution)/shard_map/all_to_all | solution.py:27
  142.4 25.4 %all_to_all.32 = f32[64,12,96]{2,1,0:T(8,128)S(1)} all-to-all(f32[64,12,96]{2,1,0:T(8,128)S(1)} %reshape.60), channel_id=1, replica_groups=mesh['dp'=64,'mp'=8] {'dp'}, dimensions={0} | all-to-all | bytes 589824 | tf_op jit(solution)/shard_map/all_to_all | solution.py:27
  167.9 0.6 fusion.27
  168.5 0.7 broadcast_in_dim.8
  169.2 5.7 %all-to-all-start.5 = ((bf16[64,12,96]{2,1,0:T(8,128)(2,1)}), bf16[64,12,96]{2,1,0:T(8,128)(2,1)S(1)}, u32[]{:S(2)}, u32[]{:S(2)}) async-start(bf16[64,12,96]{2,1,0:T(8,128)(2,1)} %broadcast_in_dim.8), calls=%async_computation.5 | async-start | bytes 524288 | tf_op jit(solution)/shard_map/all_to_all | solution.py:32
  175.0 1.6 copy.30
  176.6 1.5 copy.29
  178.0 10.1 %all-to-all-done.5 = bf16[64,12,96]{2,1,0:T(8,128)(2,1)S(1)} async-done(((bf16[64,12,96]{2,1,0:T(8,128)(2,1)}), bf16[64,12,96]{2,1,0:T(8,128)(2,1)S(1)}, u32[]{:S(2)}, u32[]{:S(2)}) %all-to-all-start.5) | async-done | bytes 147488 | tf_op jit(solution)/shard_map/all_to_all | solution.py:32
  188.2 0.8 copy.31
  189.0 4.3 %multiply_reduce_fusion = (f32[2]{0:T(128)S(1)}, f32[2,768,768]{2,1,0:T(8,128)S(1)}) fusion(bf16[2,768,768]{2,1,0:T(8,128)(2,1)} %all-gather.8.cloned.1.call-done, bf16[1,768,768]{2,1,0:T(8,128)(2,1)S(1)} %bitcast.54, bf16[1,768,768]{2,1,0:T(8,128)(2,1)} %bitcast.55), kind=kOutput, calls=%fused_computation.3 | convolution fusion | flops 1815478272 | bytes 9437192 | tf_op jit(solution)/shard_map/sij,sjk->sik/dot_general | solution.py:91
  193.8 1.4 copy-done.1
  195.2 3.4 %convolution_convert_fusion = bf16[2,768,768]{2,1,0:T(8,128)(2,1)} fusion(bf16[2,768,768]{2,1,0:T(8,128)(2,1)S(1)} %multiply_convert_fusion), kind=kOutput, calls=%fused_computation.11 | convolution fusion | flops 1813118976 | bytes 4718592 | tf_op jit(solution)/shard_map/sij,skj->sik/dot_general | solution.py:97
  198.6 8.3 %add_convert_fusion = bf16[2,768,768]{2,1,0:T(8,128)(2,1)S(1)} fusion(bf16[2,768,768]{2,1,0:T(8,128)(2,1)} %copy-done.1, bf16[2,768,768]{2,1,0:T(8,128)(2,1)} %convolution_convert_fusion), kind=kOutput, calls=%fused_computation | convolution fusion | flops 3634495488 | bytes 7077888 | tf_op jit(solution)/shard_map/sij,sjk->sik/dot_general | solution.py:103
  206.9 1.2 fusion.7
  208.1 0.9 slice_bitcast_fusion
  (53 shorter events, 3.6 us)
Async XLA Ops:
  7.2 17.0 %copy-start = (f32[768,96]{0,1:T(8,128)S(1)}, f32[768,96]{0,1:T(8,128)}, u32[]{:S(2)}) copy-start(f32[768,96]{0,1:T(8,128)} %param.13) | copy-start | bytes 884740
  7.2 34.7 %copy-start.8 = (f32[12,96]{1,0:T(8,128)S(1)}, f32[12,96]{1,0:T(8,128)}, u32[]{:S(2)}) copy-start(f32[12,96]{1,0:T(8,128)} %param.10) | copy-start | bytes 13828
  9.3 32.6 %all-to-all-start = ((f32[64,12,96]{2,1,0:T(8,128)}), f32[64,12,96]{2,1,0:T(8,128)S(1)}, u32[]{:S(2)}, u32[]{:S(2)}) async-start(f32[64,12,96]{2,1,0:T(8,128)} %reshape.57), calls=%async_computation | async-start | bytes 1048576 | tf_op jit(solution)/shard_map/all_to_all | solution.py:27
  24.1 47.8 %all-gather.4.cloned.1.call-start = ((), (), s32[]{:S(2)}) async-start(), calls=%async_computation.6 | async-start | bytes 1327104 | tf_op jit(solution)/shard_map/all_gather | solution.py:49
  24.9 46.8 %copy-start.4 = (f32[768,12]{0,1:T(8,128)S(1)}, f32[768,12]{0,1:T(8,128)}, u32[]{:S(2)}) copy-start(f32[768,12]{0,1:T(8,128)} %param.12) | copy-start | bytes 110596
  24.9 97.4 %all-gather.6.cloned.1.call-start = ((), (), s32[]{:S(2)}) async-start(), calls=%async_computation.7 | async-start | bytes 3096576 | tf_op jit(solution)/shard_map/all_gather | solution.py:51
  74.1 47.8 %all-to-all-start.2 = ((bf16[64,768,12]{1,2,0:T(8,128)(2,1)}), bf16[64,768,12]{1,2,0:T(8,128)(2,1)S(1)}, u32[]{:S(2)}, u32[]{:S(2)}) async-start(bf16[64,768,12]{1,2,0:T(8,128)(2,1)} %broadcast_in_dim.7), calls=%async_computation.2 | async-start | bytes 3145728 | tf_op jit(solution)/shard_map/all_to_all | solution.py:32
  83.0 106.0 %all-gather.8.cloned.1.call-start = ((), (), s32[]{:S(2)}) async-start(), calls=%async_computation.8 | async-start | bytes 2654208 | tf_op jit(solution)/shard_map/all_gather | solution.py:77
  124.1 1.1 copy-start.5
  124.1 2.1 copy-start.6
  125.2 2.4 %copy-start.9 = (f32[12,96]{1,0:T(8,128)S(1)}, f32[12,96]{1,0:T(8,128)}, u32[]{:S(2)}) copy-start(f32[12,96]{1,0:T(8,128)} %param.11) | copy-start | bytes 13828
  126.3 2.4 %copy-start.2 = (f32[96,768]{1,0:T(8,128)}, f32[96,768]{1,0:T(8,128)S(1)}, u32[]{:S(2)}) copy-start(f32[96,768]{1,0:T(8,128)S(1)} %fusion.9) | copy-start | bytes 884740
  127.6 14.6 %copy-start.3 = (f32[96,768]{1,0:T(8,128)}, f32[96,768]{1,0:T(8,128)S(1)}, u32[]{:S(2)}) copy-start(f32[96,768]{1,0:T(8,128)S(1)} %fusion.8) | copy-start | bytes 884740
  127.8 14.6 %copy-start.7 = (f32[12,96]{1,0:T(8,128)}, f32[12,96]{1,0:T(8,128)S(1)}, u32[]{:S(2)}) copy-start(f32[12,96]{1,0:T(8,128)S(1)} %get-tuple-element.44) | copy-start | bytes 13828
  130.1 37.8 %copy-start.10 = (f32[12,96]{1,0:T(8,128)S(1)}, f32[12,96]{1,0:T(8,128)}, u32[]{:S(2)}) copy-start(f32[12,96]{1,0:T(8,128)} %param.9) | copy-start | bytes 13828
  169.2 18.9 %all-to-all-start.5 = ((bf16[64,12,96]{2,1,0:T(8,128)(2,1)}), bf16[64,12,96]{2,1,0:T(8,128)(2,1)S(1)}, u32[]{:S(2)}, u32[]{:S(2)}) async-start(bf16[64,12,96]{2,1,0:T(8,128)(2,1)} %broadcast_in_dim.8), calls=%async_computation.5 | async-start | bytes 524288 | tf_op jit(solution)/shard_map/all_to_all | solution.py:32
  193.7 1.4 copy-start.1
Sparse Core Ops, SparseCore 0:
  27.6 38.1 all-gather.3
  73.0 41.0 all-gather.5
  130.3 35.6 all-gather.7

commit v14 on v13

--- a/solution.py
+++ b/solution.py
@@ -90,20 +90,16 @@
     basis_whole = jnp.stack([left_full.astype(jnp.bfloat16), right_full.astype(jnp.bfloat16)])
     power = jnp.einsum("sij,sjk->sik", stat_whole, basis_whole, preferred_element_type=jnp.float32)
     total = jnp.sum(power * power, axis=(1, 2), keepdims=True)
-    start = lax.optimization_barrier(
-        (power * lax.rsqrt(total * (4.0 / order_count) + norm_eps)).astype(jnp.bfloat16)
-    )
-    gram = lax.optimization_barrier(
-        jnp.einsum("sij,skj->sik", start, start, preferred_element_type=jnp.float32).astype(
-            jnp.bfloat16
-        )
+    start = (power * lax.rsqrt(total * (4.0 / order_count) + norm_eps)).astype(jnp.bfloat16)
+    gram = jnp.einsum("sij,skj->sik", start, start, preferred_element_type=jnp.float32).astype(
+        jnp.bfloat16
     )
     square = jnp.einsum("sij,sjk->sik", gram, gram, preferred_element_type=jnp.float32)
     poly = (quint_b * gram.astype(jnp.float32) + quint_c * square).astype(jnp.bfloat16)
     middle = quint_a * start.astype(jnp.float32) + jnp.einsum(
         "sij,sjk->sik", poly, start, preferred_element_type=jnp.float32
     )
-    middle = lax.optimization_barrier(middle.astype(jnp.bfloat16))
+    middle = middle.astype(jnp.bfloat16)
     middle_rows = lax.dynamic_slice_in_dim(middle, band_start, band_width, 1)
     gram_two = jnp.einsum(
         "sij,skj->sik", middle_rows, middle, preferred_element_type=jnp.float32

time: 216 us -> 218 us (level)
  no operation moved by 1% of the time
where the time goes in v14:
time: 218 us
  waiting for transfers between devices  66.1 us (30%)
  blocking collectives  65 us (30%)
  starting transfers between devices  29.5 us (14%)
  matrix products  24.4 us (11%)
  local copies, waits for them, and re-layouts  14.8 us (7%)
  between operations  14 us (6%)
  other arithmetic  3.98 us (2%)
    all_to_all x2, waiting for transfers between devices, gather_rows(): lax.all_to_all(jnp.broadcast_to(x[None], (count,) + x.shape), axis, 0, 0,...  49.1 us
    all_to_all x2, blocking collectives, scatter_sum(): return jnp.sum(lax.all_to_all(chunks, axis, 0, 0, tiled=False), axis=0)  36.8 us
    all_to_all x1, blocking collectives, gather_rows(): lax.all_to_all(jnp.broadcast_to(x[None], (count,) + x.shape), axis, 0, 0,...  28.3 us
    all_to_all x1, waiting for transfers between devices, scatter_sum(): return jnp.sum(lax.all_to_all(chunks, axis, 0, 0, tiled=False), axis=0)  16.9 us
    all_to_all x1, starting transfers between devices, scatter_sum(): return jnp.sum(lax.all_to_all(chunks, axis, 0, 0, tiled=False), axis=0)  14.8 us
    all_to_all x2, starting transfers between devices, gather_rows(): lax.all_to_all(jnp.broadcast_to(x[None], (count,) + x.shape), axis, 0, 0,...  14.6 us
    dot_general x1, matrix products, per_device(): jnp.einsum('sij,sjk->sik', poly, start, preferred_element_type=jnp.float32)  9.6 us
  transfers between devices with their start and end apart: 6, of which 3 were waited for; matrix products, arithmetic and copies ran while one was open for 5% of the time, Pallas kernels for 0%

profile of v14, /device:TPU:1, one launch (start us, length us, event | category | flops | bytes accessed | tf_op | source)
XLA Modules:
  0.0 217.9 jit_solution(14761972339999643079)
XLA Ops:
  7.2 1.1 convert_reduce_fusion
  8.4 0.8 reshape.57
  9.3 14.8 %all-to-all-start = ((f32[64,12,96]{2,1,0:T(8,128)}), f32[64,12,96]{2,1,0:T(8,128)S(1)}, u32[]{:S(2)}, u32[]{:S(2)}) async-start(f32[64,12,96]{2,1,0:T(8,128)} %reshape.57), calls=%async_computation | async-start | bytes 1048576 | tf_op jit(solution)/shard_map/all_to_all | solution.py:27
  24.2 0.7 convert.12
  24.9 16.9 %all-to-all-done = f32[64,12,96]{2,1,0:T(8,128)S(1)} async-done(((f32[64,12,96]{2,1,0:T(8,128)}), f32[64,12,96]{2,1,0:T(8,128)S(1)}, u32[]{:S(2)}, u32[]{:S(2)}) %all-to-all-start) | async-done | bytes 294944 | tf_op jit(solution)/shard_map/all_to_all | solution.py:27
  42.8 28.3 %all_to_all.30 = f32[64,2,12,96]{3,1,2,0:T(2,128)S(1)} all-to-all(f32[64,2,12,96]{3,1,2,0:T(2,128)S(1)} %broadcast_in_dim.6), channel_id=1, replica_groups=mesh['dp'=64,'mp'=8] {'dp'}, dimensions={0} | all-to-all | bytes 1179648 | tf_op jit(solution)/shard_map/all_to_all | solution.py:32
  71.0 0.6 fusion.28
  71.9 0.9 copy.25
  72.9 1.2 broadcast_in_dim.7
  74.1 8.8 %all-to-all-start.2 = ((bf16[64,768,12]{1,2,0:T(8,128)(2,1)}), bf16[64,768,12]{1,2,0:T(8,128)(2,1)S(1)}, u32[]{:S(2)}, u32[]{:S(2)}) async-start(bf16[64,768,12]{1,2,0:T(8,128)(2,1)} %broadcast_in_dim.7), calls=%async_computation.2 | async-start | bytes 3145728 | tf_op jit(solution)/shard_map/all_to_all | solution.py:32
  83.0 38.9 %all-to-all-done.2 = bf16[64,768,12]{1,2,0:T(8,128)(2,1)S(1)} async-done(((bf16[64,768,12]{1,2,0:T(8,128)(2,1)}), bf16[64,768,12]{1,2,0:T(8,128)(2,1)S(1)}, u32[]{:S(2)}, u32[]{:S(2)}) %all-to-all-start.2) | async-done | bytes 1179680 | tf_op jit(solution)/shard_map/all_to_all | solution.py:32
  122.3 1.8 slice.29
  124.2 1.1 fusion.29
  125.2 1.3 fusion.8
  126.6 1.1 fusion.9
  127.6 0.7 copy-done.2
  128.4 0.7 pad_maximum_fusion.1
  129.4 1.5 fusion.13
  131.2 11.4 %all_to_all.31 = f32[8,96,12]{1,2,0:T(8,128)S(1)} all-to-all(f32[8,96,12]{1,2,0:T(8,128)S(1)} %copy.26), channel_id=1, replica_groups=mesh['dp'=64,'mp'=8] {'mp'}, dimensions={0} | all-to-all | bytes 73728 | tf_op jit(solution)/shard_map/all_to_all | solution.py:27
  143.1 25.4 %all_to_all.32 = f32[64,12,96]{2,1,0:T(8,128)S(1)} all-to-all(f32[64,12,96]{2,1,0:T(8,128)S(1)} %reshape.60), channel_id=1, replica_groups=mesh['dp'=64,'mp'=8] {'dp'}, dimensions={0} | all-to-all | bytes 589824 | tf_op jit(solution)/shard_map/all_to_all | solution.py:27
  169.2 0.7 broadcast_in_dim.8
  169.9 5.7 %all-to-all-start.5 = ((bf16[64,12,96]{2,1,0:T(8,128)(2,1)}), bf16[64,12,96]{2,1,0:T(8,128)(2,1)S(1)}, u32[]{:S(2)}, u32[]{:S(2)}) async-start(bf16[64,12,96]{2,1,0:T(8,128)(2,1)} %broadcast_in_dim.8), calls=%async_computation.5 | async-start | bytes 524288 | tf_op jit(solution)/shard_map/all_to_all | solution.py:32
  175.7 1.6 copy.30
  177.3 1.5 copy.29
  178.7 10.1 %all-to-all-done.5 = bf16[64,12,96]{2,1,0:T(8,128)(2,1)S(1)} async-done(((bf16[64,12,96]{2,1,0:T(8,128)(2,1)}), bf16[64,12,96]{2,1,0:T(8,128)(2,1)S(1)}, u32[]{:S(2)}, u32[]{:S(2)}) %all-to-all-start.5) | async-done | bytes 147488 | tf_op jit(solution)/shard_map/all_to_all | solution.py:32
  188.9 0.8 copy.31
  189.7 4.3 %multiply_reduce_fusion = (f32[2]{0:T(128)S(1)}, f32[2,768,768]{2,1,0:T(8,128)S(1)}) fusion(bf16[2,768,768]{2,1,0:T(8,128)(2,1)} %all-gather.8.cloned.1.call-done, bf16[1,768,768]{2,1,0:T(8,128)(2,1)S(1)} %bitcast.51, bf16[1,768,768]{2,1,0:T(8,128)(2,1)} %bitcast.52), kind=kOutput, calls=%fused_computation.3 | convolution fusion | flops 1815478272 | bytes 9437192 | tf_op jit(solution)/shard_map/sij,sjk->sik/dot_general | solution.py:91
  194.0 2.1 copy-done.10
  196.1 3.6 %convolution_convert_fusion = bf16[2,768,768]{2,1,0:T(8,128)(2,1)} fusion(f32[2,768,768]{2,1,0:T(8,128)S(1)} %get-tuple-element.47, f32[2]{0:T(128)S(1)} %add_rsqrt_fusion), kind=kOutput, calls=%fused_computation.11 | convolution fusion | flops 1815478272 | bytes 7077896 | tf_op jit(solution)/shard_map/sij,skj->sik/dot_general | solution.py:94
  199.7 9.6 %add_convert_fusion = bf16[2,768,768]{2,1,0:T(8,128)(2,1)S(1)} fusion(bf16[2,768,768]{2,1,0:T(8,128)(2,1)} %convolution_convert_fusion, f32[2,768,768]{2,1,0:T(8,128)} %copy-done.10, f32[2]{0:T(128)S(1)} %add_rsqrt_fusion), kind=kOutput, calls=%fused_computation | convolution fusion | flops 3639214080 | bytes 9437192 | tf_op jit(solution)/shard_map/sij,sjk->sik/dot_general | solution.py:99
  209.3 1.2 fusion.7
  210.5 0.9 slice_bitcast_fusion
  (52 shorter events, 3.8 us)
Async XLA Ops:
  7.2 17.0 %copy-start = (f32[768,96]{0,1:T(8,128)S(1)}, f32[768,96]{0,1:T(8,128)}, u32[]{:S(2)}) copy-start(f32[768,96]{0,1:T(8,128)} %param.13) | copy-start | bytes 884740
  7.2 34.7 %copy-start.7 = (f32[12,96]{1,0:T(8,128)S(1)}, f32[12,96]{1,0:T(8,128)}, u32[]{:S(2)}) copy-start(f32[12,96]{1,0:T(8,128)} %param.10) | copy-start | bytes 13828
  9.3 32.6 %all-to-all-start = ((f32[64,12,96]{2,1,0:T(8,128)}), f32[64,12,96]{2,1,0:T(8,128)S(1)}, u32[]{:S(2)}, u32[]{:S(2)}) async-start(f32[64,12,96]{2,1,0:T(8,128)} %reshape.57), calls=%async_computation | async-start | bytes 1048576 | tf_op jit(solution)/shard_map/all_to_all | solution.py:27
  24.1 47.8 %all-gather.4.cloned.1.call-start = ((), (), s32[]{:S(2)}) async-start(), calls=%async_computation.6 | async-start | bytes 1327104 | tf_op jit(solution)/shard_map/all_gather | solution.py:49
  24.9 46.8 %copy-start.3 = (f32[768,12]{0,1:T(8,128)S(1)}, f32[768,12]{0,1:T(8,128)}, u32[]{:S(2)}) copy-start(f32[768,12]{0,1:T(8,128)} %param.12) | copy-start | bytes 110596
  24.9 97.4 %all-gather.6.cloned.1.call-start = ((), (), s32[]{:S(2)}) async-start(), calls=%async_computation.7 | async-start | bytes 3096576 | tf_op jit(solution)/shard_map/all_gather | solution.py:51
  74.1 47.8 %all-to-all-start.2 = ((bf16[64,768,12]{1,2,0:T(8,128)(2,1)}), bf16[64,768,12]{1,2,0:T(8,128)(2,1)S(1)}, u32[]{:S(2)}, u32[]{:S(2)}) async-start(bf16[64,768,12]{1,2,0:T(8,128)(2,1)} %broadcast_in_dim.7), calls=%async_computation.2 | async-start | bytes 3145728 | tf_op jit(solution)/shard_map/all_to_all | solution.py:32
  83.0 106.8 %all-gather.8.cloned.1.call-start = ((), (), s32[]{:S(2)}) async-start(), calls=%async_computation.8 | async-start | bytes 2654208 | tf_op jit(solution)/shard_map/all_gather | solution.py:77
  124.1 1.1 copy-start.4
  124.1 2.4 %copy-start.5 = (f32[96,768]{1,0:T(8,128)S(1)}, f32[96,768]{1,0:T(8,128)}, u32[]{:S(2)}) copy-start(f32[96,768]{1,0:T(8,128)} %param.14) | copy-start | bytes 884740
  126.5 2.8 %copy-start.1 = (f32[96,768]{1,0:T(8,128)}, f32[96,768]{1,0:T(8,128)S(1)}, u32[]{:S(2)}) copy-start(f32[96,768]{1,0:T(8,128)S(1)} %fusion.8) | copy-start | bytes 884740
  126.5 2.6 %copy-start.8 = (f32[12,96]{1,0:T(8,128)S(1)}, f32[12,96]{1,0:T(8,128)}, u32[]{:S(2)}) copy-start(f32[12,96]{1,0:T(8,128)} %param.11) | copy-start | bytes 13828
  127.6 0.7 copy-start.2
  129.4 39.1 %copy-start.6 = (f32[12,96]{1,0:T(8,128)}, f32[12,96]{1,0:T(8,128)S(1)}, u32[]{:S(2)}) copy-start(f32[12,96]{1,0:T(8,128)S(1)} %get-tuple-element.44) | copy-start | bytes 13828
  130.8 37.8 %copy-start.9 = (f32[12,96]{1,0:T(8,128)S(1)}, f32[12,96]{1,0:T(8,128)}, u32[]{:S(2)}) copy-start(f32[12,96]{1,0:T(8,128)} %param.9) | copy-start | bytes 13828
  169.9 18.9 %all-to-all-start.5 = ((bf16[64,12,96]{2,1,0:T(8,128)(2,1)}), bf16[64,12,96]{2,1,0:T(8,128)(2,1)S(1)}, u32[]{:S(2)}, u32[]{:S(2)}) async-start(bf16[64,12,96]{2,1,0:T(8,128)(2,1)} %broadcast_in_dim.8), calls=%async_computation.5 | async-start | bytes 524288 | tf_op jit(solution)/shard_map/all_to_all | solution.py:32
  194.0 2.1 copy-start.10
Sparse Core Ops, SparseCore 0:
  27.6 38.1 all-gather.3
  73.0 41.0 all-gather.5
  131.0 35.6 all-gather.7

commit v15 on v13

--- a/solution.py
+++ b/solution.py
@@ -40,8 +40,11 @@
     new_moment = beta_one * moment + (1.0 - beta_one) * grad_piece
     pieces = gather_rows(jnp.stack([grad_piece, moment]), "dp")
     pieces = jnp.swapaxes(pieces, 0, 1).reshape(2, -1, pieces.shape[-1])
-    left_cols = gather_rows(left_basis.astype(jnp.bfloat16), "dp")
-    left_full = jnp.moveaxis(left_cols, 0, 1).reshape(left_basis.shape[0], -1)
+    left_flat = left_basis.T.astype(jnp.bfloat16).reshape(1, -1)
+    left_cols = lax.all_to_all(
+        jnp.broadcast_to(left_flat, (lax.axis_size("dp"), left_flat.shape[1])), "dp", 0, 0, tiled=False
+    )
+    left_full = left_cols.reshape(-1, left_basis.shape[0]).T
     moment_left = lax.dot_general(
         left_basis, pieces[1], (((0,), (0,)), ((), ())), precision=highest
     )

time: 216 us -> 235 us (1.088)
  other arithmetic: 4.43 us -> 20.7 us
  waiting for transfers between devices: 66.1 us -> 58.9 us
  local copies, waits for them, and re-layouts: 13.4 us -> 16.8 us
    all_to_all x2 -> x1, waiting for transfers between devices: 49.1 us -> 11.6 us  [gather_rows(): lax.all_to_all(jnp.broadcast_to(x[None], (count,) + x.shape), axis, 0, 0,...]
    all_to_all x0 -> x1, waiting for transfers between devices: none -> 30.4 us  [per_device(): lax.all_to_all(jnp.broadcast_to(left_flat, (lax.axis_size('dp'), left_fla...]
    all_to_all x0 -> x1, starting transfers between devices: none -> 8.6 us  [per_device(): lax.all_to_all(jnp.broadcast_to(left_flat, (lax.axis_size('dp'), left_fla...]
    all_to_all x2 -> x1, starting transfers between devices: 14.6 us -> 6.09 us  [gather_rows(): lax.all_to_all(jnp.broadcast_to(x[None], (count,) + x.shape), axis, 0, 0,...]
    broadcast_in_dim x0 -> x1, other arithmetic: none -> 7.76 us  [per_device(): jnp.broadcast_to(left_flat, (lax.axis_size('dp'), left_flat.shape[1]))]
    all_to_all x0 -> x1, other arithmetic: none -> 7.12 us  [per_device(): lax.all_to_all(jnp.broadcast_to(left_flat, (lax.axis_size('dp'), left_fla...]
    reshape x1 -> x2, local copies, waits for them, and re-layouts: 0.29 us -> 3.5 us  [per_device(): left_full = left_cols.reshape(-1, left_basis.shape[0]).T]
    dot_general x1, matrix products: 3.44 us -> 5.82 us  [per_device(): jnp.einsum('sij,skj->sik', start, start, preferred_element_type=jnp.float32)]
  transfers between devices with their start and end apart: 6 -> 6, of which waited for: 3 -> 3; matrix products, arithmetic and copies ran while one was open for 5% -> 13% of each run, Pallas kernels for 0% -> 0%
where the time goes in v15:
time: 235 us; the launch traced here: 232 us
  blocking collectives  66.1 us (28%)
  waiting for transfers between devices  58.9 us (25%)
  starting transfers between devices  29.8 us (13%)
  matrix products  25.3 us (11%)
  other arithmetic  20.7 us (9%)
  local copies, waits for them, and re-layouts  16.8 us (7%)
  between operations  14.4 us (6%)
    all_to_all x2, blocking collectives, scatter_sum(): return jnp.sum(lax.all_to_all(chunks, axis, 0, 0, tiled=False), axis=0)  37.3 us
    all_to_all x1, waiting for transfers between devices, per_device(): lax.all_to_all(jnp.broadcast_to(left_flat, (lax.axis_size('dp'), left_fla...  30.4 us
    all_to_all x1, blocking collectives, gather_rows(): lax.all_to_all(jnp.broadcast_to(x[None], (count,) + x.shape), axis, 0, 0,...  28.8 us
    all_to_all x1, waiting for transfers between devices, scatter_sum(): return jnp.sum(lax.all_to_all(chunks, axis, 0, 0, tiled=False), axis=0)  16.9 us
    all_to_all x1, starting transfers between devices, scatter_sum(): return jnp.sum(lax.all_to_all(chunks, axis, 0, 0, tiled=False), axis=0)  14.8 us
    all_to_all x1, waiting for transfers between devices, gather_rows(): lax.all_to_all(jnp.broadcast_to(x[None], (count,) + x.shape), axis, 0, 0,...  11.6 us
    all_to_all x1, starting transfers between devices, per_device(): lax.all_to_all(jnp.broadcast_to(left_flat, (lax.axis_size('dp'), left_fla...  8.6 us
    dot_general x1, matrix products, per_device(): jnp.einsum('sij,sjk->sik', poly, start, preferred_element_type=jnp.float32)  8.28 us
  transfers between devices with their start and end apart: 6, of which 3 were waited for; matrix products, arithmetic and copies ran while one was open for 13% of the time, Pallas kernels for 0%

profile of v15, /device:TPU:1, one launch (start us, length us, event | category | flops | bytes accessed | tf_op | source)
XLA Modules:
  0.0 232.2 jit_solution(13340996838526251358)
XLA Ops:
  7.2 1.1 convert_reduce_fusion
  8.4 0.8 reshape.66
  9.3 14.8 %all-to-all-start = ((f32[64,12,96]{2,1,0:T(8,128)}), f32[64,12,96]{2,1,0:T(8,128)S(1)}, u32[]{:S(2)}, u32[]{:S(2)}) async-start(f32[64,12,96]{2,1,0:T(8,128)} %reshape.66), calls=%async_computation | async-start | bytes 1048576 | tf_op jit(solution)/shard_map/all_to_all | solution.py:27
  24.9 16.9 %all-to-all-done = f32[64,12,96]{2,1,0:T(8,128)S(1)} async-done(((f32[64,12,96]{2,1,0:T(8,128)}), f32[64,12,96]{2,1,0:T(8,128)S(1)}, u32[]{:S(2)}, u32[]{:S(2)}) %all-to-all-start) | async-done | bytes 294944 | tf_op jit(solution)/shard_map/all_to_all | solution.py:27
  42.7 28.8 %all_to_all.31 = f32[64,2,12,96]{3,1,2,0:T(2,128)S(1)} all-to-all(f32[64,2,12,96]{3,1,2,0:T(2,128)S(1)} %broadcast_in_dim.8), channel_id=1, replica_groups=mesh['dp'=64,'mp'=8] {'dp'}, dimensions={0} | all-to-all | bytes 1179648 | tf_op jit(solution)/shard_map/all_to_all | solution.py:32
  72.4 0.9 copy.24
  73.5 1.2 broadcast_in_dim.10
  75.2 7.8 %reduce.2 = bf16[64,9216]{1,0:T(8,128)(2,1)S(1)} reduce(bf16[64,1,9216]{2,1,0:T(2,128)(2,1)S(1)} %broadcast_in_dim.10, bf16[]{:T(256)} %broadcast.60), dimensions={1}, to_apply=%broadcast_in_dim.10.reduce_sub_computation | reduce | bytes 2359298 | tf_op jit(solution)/shard_map/broadcast_in_dim | solution.py:45
  83.0 1.7 reshape.72
  84.7 8.6 %all-to-all-start.2 = ((bf16[64,2,4608]{2,1,0:T(2,128)(2,1)}), bf16[64,2,4608]{2,1,0:T(2,128)(2,1)S(1)}, u32[]{:S(2)}, u32[]{:S(2)}) async-start(bf16[64,2,4608]{2,1,0:T(2,128)(2,1)} %reshape.72), calls=%async_computation.2 | async-start | bytes 2359296 | tf_op jit(solution)/shard_map/all_to_all | solution.py:44
  93.5 30.4 %all-to-all-done.2 = bf16[64,2,4608]{2,1,0:T(2,128)(2,1)S(1)} async-done(((bf16[64,2,4608]{2,1,0:T(2,128)(2,1)}), bf16[64,2,4608]{2,1,0:T(2,128)(2,1)S(1)}, u32[]{:S(2)}, u32[]{:S(2)}) %all-to-all-start.2) | async-done | bytes 1179680 | tf_op jit(solution)/shard_map/all_to_all | solution.py:44
  123.9 1.0 reshape.73
  124.8 7.1 %reduce.1 = bf16[64,9216]{1,0:T(8,128)(2,1)S(1)} reduce(bf16[64,1,9216]{2,1,0:T(2,128)(2,1)S(1)} %reshape.73, bf16[]{:T(256)} %constant.50), dimensions={1}, to_apply=%all_to_all.21.reduce_sub_computation | reduce | bytes 2359298 | tf_op jit(solution)/shard_map/all_to_all | solution.py:44
  132.0 1.9 reshape.67
  133.8 1.6 copy.25
  135.5 1.8 slice.29
  137.4 1.1 fusion.29
  138.5 1.1 fusion.9
  139.6 1.3 fusion.8
  141.9 1.4 fusion.13
  143.7 11.7 %all_to_all.32 = f32[8,96,12]{1,2,0:T(8,128)S(1)} all-to-all(f32[8,96,12]{1,2,0:T(8,128)S(1)} %copy.26), channel_id=1, replica_groups=mesh['dp'=64,'mp'=8] {'mp'}, dimensions={0} | all-to-all | bytes 73728 | tf_op jit(solution)/shard_map/all_to_all | solution.py:27
  156.0 25.6 %all_to_all.33 = f32[64,12,96]{2,1,0:T(8,128)S(1)} all-to-all(f32[64,12,96]{2,1,0:T(8,128)S(1)} %reshape.69), channel_id=1, replica_groups=mesh['dp'=64,'mp'=8] {'dp'}, dimensions={0} | all-to-all | bytes 589824 | tf_op jit(solution)/shard_map/all_to_all | solution.py:27
  183.0 6.1 %all-to-all-start.5 = ((bf16[64,12,96]{2,1,0:T(8,128)(2,1)}), bf16[64,12,96]{2,1,0:T(8,128)(2,1)S(1)}, u32[]{:S(2)}, u32[]{:S(2)}) async-start(bf16[64,12,96]{2,1,0:T(8,128)(2,1)} %broadcast_in_dim.11), calls=%async_computation.5 | async-start | bytes 524288 | tf_op jit(solution)/shard_map/all_to_all | solution.py:32
  189.1 1.4 copy.29
  190.6 11.6 %all-to-all-done.5 = bf16[64,12,96]{2,1,0:T(8,128)(2,1)S(1)} async-done(((bf16[64,12,96]{2,1,0:T(8,128)(2,1)}), bf16[64,12,96]{2,1,0:T(8,128)(2,1)S(1)}, u32[]{:S(2)}, u32[]{:S(2)}) %all-to-all-start.5) | async-done | bytes 147488 | tf_op jit(solution)/shard_map/all_to_all | solution.py:32
  202.3 0.8 copy.30
  203.1 4.3 %multiply_reduce_fusion = (f32[2]{0:T(128)S(1)}, f32[2,768,768]{2,1,0:T(8,128)S(1)}) fusion(bf16[2,768,768]{2,1,0:T(8,128)(2,1)} %all-gather.8.cloned.1.call-done, bf16[1,768,768]{2,1,0:T(8,128)(2,1)} %bitcast.54, bf16[1,768,768]{2,1,0:T(8,128)(2,1)S(1)} %bitcast.53), kind=kOutput, calls=%fused_computation.3 | convolution fusion | flops 1815478272 | bytes 9437192 | tf_op jit(solution)/shard_map/sij,sjk->sik/dot_general | solution.py:94
  207.4 1.9 multiply_convert_fusion
  209.2 5.8 %convolution_convert_fusion = bf16[2,768,768]{2,1,0:T(8,128)(2,1)} fusion(bf16[2,768,768]{2,1,0:T(8,128)(2,1)} %multiply_convert_fusion), kind=kOutput, calls=%fused_computation.11 | convolution fusion | flops 1813118976 | bytes 4718592 | tf_op jit(solution)/shard_map/sij,skj->sik/dot_general | solution.py:100
  215.0 8.3 %add_convert_fusion = bf16[2,768,768]{2,1,0:T(8,128)(2,1)S(1)} fusion(bf16[2,768,768]{2,1,0:T(8,128)(2,1)} %multiply_convert_fusion, bf16[2,768,768]{2,1,0:T(8,128)(2,1)} %convolution_convert_fusion), kind=kOutput, calls=%fused_computation | convolution fusion | flops 3634495488 | bytes 7077888 | tf_op jit(solution)/shard_map/sij,sjk->sik/dot_general | solution.py:106
  223.3 1.2 fusion.7
  224.5 0.9 slice_bitcast_fusion
  (65 shorter events, 7.0 us)
Async XLA Ops:
  7.2 17.0 %copy-start = (f32[768,96]{0,1:T(8,128)S(1)}, f32[768,96]{0,1:T(8,128)}, u32[]{:S(2)}) copy-start(f32[768,96]{0,1:T(8,128)} %param.13) | copy-start | bytes 884740
  7.2 34.7 %copy-start.11 = (f32[12,96]{1,0:T(8,128)S(1)}, f32[12,96]{1,0:T(8,128)}, u32[]{:S(2)}) copy-start(f32[12,96]{1,0:T(8,128)} %param.10) | copy-start | bytes 13828
  9.3 32.6 %all-to-all-start = ((f32[64,12,96]{2,1,0:T(8,128)}), f32[64,12,96]{2,1,0:T(8,128)S(1)}, u32[]{:S(2)}, u32[]{:S(2)}) async-start(f32[64,12,96]{2,1,0:T(8,128)} %reshape.66), calls=%async_computation | async-start | bytes 1048576 | tf_op jit(solution)/shard_map/all_to_all | solution.py:27
  24.1 48.3 %all-gather.4.cloned.1.call-start = ((), (), s32[]{:S(2)}) async-start(), calls=%async_computation.6 | async-start | bytes 1327104 | tf_op jit(solution)/shard_map/all_gather | solution.py:52
  24.8 47.3 %copy-start.6 = (f32[768,12]{0,1:T(8,128)S(1)}, f32[768,12]{0,1:T(8,128)}, u32[]{:S(2)}) copy-start(f32[768,12]{0,1:T(8,128)} %param.12) | copy-start | bytes 110596
  24.9 110.7 %all-gather.6.cloned.1.call-start = ((), (), s32[]{:S(2)}) async-start(), calls=%async_computation.7 | async-start | bytes 3096576 | tf_op jit(solution)/shard_map/all_gather | solution.py:54
  84.7 39.2 %all-to-all-start.2 = ((bf16[64,2,4608]{2,1,0:T(2,128)(2,1)}), bf16[64,2,4608]{2,1,0:T(2,128)(2,1)S(1)}, u32[]{:S(2)}, u32[]{:S(2)}) async-start(bf16[64,2,4608]{2,1,0:T(2,128)(2,1)} %reshape.72), calls=%async_computation.2 | async-start | bytes 2359296 | tf_op jit(solution)/shard_map/all_to_all | solution.py:44
  93.3 109.8 %all-gather.8.cloned.1.call-start = ((), (), s32[]{:S(2)}) async-start(), calls=%async_computation.8 | async-start | bytes 2654208 | tf_op jit(solution)/shard_map/all_gather | solution.py:80
  135.5 1.9 copy-start.7
  137.4 1.1 copy-start.8
  137.4 2.2 copy-start.9
  138.4 2.4 %copy-start.1 = (f32[768,96]{0,1:T(8,128)S(1)}, f32[768,96]{0,1:T(8,128)}, u32[]{:S(2)}) copy-start(f32[768,96]{0,1:T(8,128)} %param.13) | copy-start | bytes 884740
  138.4 2.4 %copy-start.12 = (f32[12,96]{1,0:T(8,128)S(1)}, f32[12,96]{1,0:T(8,128)}, u32[]{:S(2)}) copy-start(f32[12,96]{1,0:T(8,128)} %param.11) | copy-start | bytes 13828
  139.5 2.4 %copy-start.2 = (f32[96,768]{1,0:T(8,128)}, f32[96,768]{1,0:T(8,128)S(1)}, u32[]{:S(2)}) copy-start(f32[96,768]{1,0:T(8,128)S(1)} %fusion.9) | copy-start | bytes 884740
  140.9 15.1 %copy-start.3 = (f32[96,768]{1,0:T(8,128)}, f32[96,768]{1,0:T(8,128)S(1)}, u32[]{:S(2)}) copy-start(f32[96,768]{1,0:T(8,128)S(1)} %fusion.8) | copy-start | bytes 884740
  141.1 14.9 %copy-start.10 = (f32[12,96]{1,0:T(8,128)}, f32[12,96]{1,0:T(8,128)S(1)}, u32[]{:S(2)}) copy-start(f32[12,96]{1,0:T(8,128)S(1)} %get-tuple-element.44) | copy-start | bytes 13828
  143.4 38.3 %copy-start.13 = (f32[12,96]{1,0:T(8,128)S(1)}, f32[12,96]{1,0:T(8,128)}, u32[]{:S(2)}) copy-start(f32[12,96]{1,0:T(8,128)} %param.9) | copy-start | bytes 13828
  143.7 45.5 %copy-start.4 = (bf16[768,768]{0,1:T(8,128)(2,1)S(1)}, bf16[768,768]{0,1:T(8,128)(2,1)}, u32[]{:S(2)}) copy-start(bf16[768,768]{0,1:T(8,128)(2,1)} %all-gather.4.cloned.1.call-done) | copy-start | bytes 3538948
  181.6 21.5 %copy-start.5 = (bf16[768,768]{0,1:T(8,128)(2,1)S(1)}, bf16[768,768]{0,1:T(8,128)(2,1)}, u32[]{:S(2)}) copy-start(bf16[768,768]{0,1:T(8,128)(2,1)} %copy.25) | copy-start | bytes 3538948
  183.0 19.1 %all-to-all-start.5 = ((bf16[64,12,96]{2,1,0:T(8,128)(2,1)}), bf16[64,12,96]{2,1,0:T(8,128)(2,1)S(1)}, u32[]{:S(2)}, u32[]{:S(2)}) async-start(bf16[64,12,96]{2,1,0:T(8,128)(2,1)} %broadcast_in_dim.11), calls=%async_computation.5 | async-start | bytes 524288 | tf_op jit(solution)/shard_map/all_to_all | solution.py:32
Sparse Core Ops, SparseCore 0:
  27.6 38.1 all-gather.3
  73.5 40.5 all-gather.5
  143.5 36.0 all-gather.7
